TPU v7x, 512 devices: a whole 4x4x16 slice. The times are simulated.
512 devices in a mesh: section: 4 (over x_hi, core), ctx: 32 (over x_lo, z), dp: 4 (over y).
Axes of the slice: x: 4 (x_hi: 2, x_lo: 2; x = x_hi * 2 + x_lo), y: 4, z: 16, core: 2. Of those that a mesh axis runs over, the one named last changes fastest.
Arguments:
- inputs: bfloat16 [4, 8192, 4096], P('section', 'ctx', 'dp'), may hold values from -6 to 6
- upstream: bfloat16 [4, 8192, 4096], P('section', 'ctx', 'dp'), may hold values from -6 to 6
- short_filter: bfloat16 [4, 21, 256], P('section', None, 'dp'), may hold values from -2 to 2
- medium_filter: bfloat16 [4, 128, 256], P('section', None, 'dp'), may hold values from -0.5 to 0.5
Outputs:
- incoming: bfloat16 [4, 8192, 4096], P('section', 'ctx', 'dp')
- grad_short: float32 [4, 21, 256], P('section', None, ('dp', 'ctx'))
- grad_medium: float32 [4, 128, 256], P('section', None, ('dp', 'ctx'))
All inputs are finite; a program needn't handle non-finite values.
Results may differ from a plain program's by a relative error of at most 0.0071.
Values may be sent and summed in bfloat16 or wider, within the bound.
No kernel may reach another device: no remote copies, remote signals or barrier semaphores. Data moves between devices by JAX's collectives and lax.ppermute only.
A program may use at most 64 MiB of HBM per device.

v0:
```python
import jax
import jax.numpy as jnp
from jax import lax
from jax.sharding import PartitionSpec as P


def passed_along(block, axis, distance):
    devices = range(lax.axis_size(axis))
    route = [(i - distance, i) for i in devices if i - distance in devices]
    return lax.ppermute(block, axis, route)


def owned_sum(partial_terms, axis):
    axis_len = lax.axis_size(axis)
    row_count, col_count = partial_terms.shape
    width = col_count // axis_len
    chunks = partial_terms.reshape(row_count, axis_len, width).transpose(1, 2, 0)
    chunks = chunks.reshape(axis_len, width * row_count)
    if axis_len & (axis_len - 1):
        gathered = lax.all_gather(chunks, axis, axis=0, tiled=False)
        return jnp.sum(gathered[:, lax.axis_index(axis)], axis=0).reshape(width, row_count).T
    here = lax.axis_index(axis)
    span = axis_len // 2
    while span >= 1:
        upper = (here // span) % 2
        kept = lax.dynamic_slice_in_dim(chunks, upper * span, span, 0)
        sent = lax.dynamic_slice_in_dim(chunks, (1 - upper) * span, span, 0)
        route = [(i, i ^ span) for i in range(axis_len)]
        chunks = kept + lax.ppermute(sent, axis, route)
        span //= 2
    return chunks[0].reshape(width, row_count).T


def band_matrix(filter_taps, out_rows):
    tap_count, group_count = filter_taps.shape
    leading = jnp.flip(filter_taps, 0).T
    padded = jnp.concatenate([leading, jnp.zeros((group_count, out_rows), filter_taps.dtype)], 1)
    span_len = out_rows + tap_count - 1
    tiled_rows = jnp.tile(padded, (1, out_rows))[:, : out_rows * span_len]
    return tiled_rows.reshape(group_count, out_rows, span_len)


def diagonal_sums(cross_terms, tap_count):
    group_count, out_rows, span_len = cross_terms.shape
    flat_view = jnp.pad(
        cross_terms.reshape(group_count, out_rows * span_len), ((0, 0), (0, out_rows))
    )
    skewed = flat_view.reshape(group_count, out_rows, span_len + 1)
    return jnp.flip(jnp.sum(skewed[:, :, :tap_count], axis=1), 1)


def short_features(padded, chan_short, out_rows):
    lag_count = chan_short.shape[1]
    running = jnp.zeros((3, out_rows, padded.shape[1]), jnp.float32)
    for offset in range(lag_count):
        first_row = lag_count - 1 - offset
        running = running + chan_short[:, offset, None, :] * padded[
            None, first_row : first_row + out_rows
        ].astype(jnp.float32)
    return running.astype(jnp.bfloat16)


def medium_terms(medium_taps, kv_pad, gate_ext, row_block):
    tap_count, group_count = medium_taps.shape
    seq_rows = gate_ext.shape[0] - tap_count + 1
    chan_count = kv_pad.shape[1]
    group_width = chan_count // group_count
    span_len = row_block + tap_count - 1
    block_count = seq_rows // row_block
    toeplitz = band_matrix(medium_taps, row_block)
    kv_groups = kv_pad.reshape(-1, group_count, group_width)
    gate_groups = gate_ext.reshape(-1, group_count, group_width)
    starts = [b * row_block for b in range(block_count)]
    kv_win = jnp.concatenate([kv_groups[b : b + span_len] for b in starts], axis=2)
    gate_win = jnp.concatenate([gate_groups[b : b + span_len] for b in starts], axis=2)
    mixed_out = jnp.einsum("gts,sgn->tgn", toeplitz, kv_win, preferred_element_type=jnp.float32)
    back_out = jnp.flip(
        jnp.einsum(
            "gts,sgn->tgn", toeplitz, jnp.flip(gate_win, 0), preferred_element_type=jnp.float32
        ),
        0,
    )
    cross_terms = jnp.einsum(
        "tgn,sgn->gts", gate_win[:row_block], kv_win, preferred_element_type=jnp.float32
    )
    taps_grad = diagonal_sums(cross_terms, tap_count).T

    def unblock(values_in):
        split = values_in.reshape(row_block, group_count, block_count, group_width)
        return split.transpose(2, 0, 1, 3).reshape(seq_rows, chan_count)

    return unblock(mixed_out), unblock(back_out), taps_grad


def per_device(inputs, upstream, short_filter, medium_filter):
    signal = inputs[0]
    grad_out = upstream[0]
    seq_rows, chan_count = signal.shape
    tap_count = medium_filter.shape[1]
    group_count = medium_filter.shape[2]
    lag_count = short_filter.shape[1] // 3
    group_width = chan_count // group_count
    short_rim = lag_count - 1
    medium_rim = tap_count - 1
    chan_short = jnp.broadcast_to(
        short_filter[0].astype(jnp.float32).reshape(3, lag_count, group_count, 1),
        (3, lag_count, group_count, group_width),
    ).reshape(3, lag_count, chan_count)
    medium_taps = medium_filter[0]
    zero_rim = jnp.zeros((short_rim, chan_count), jnp.bfloat16)
    features_local = short_features(jnp.concatenate([zero_rim, signal], 0), chan_short, seq_rows)
    kv_local = (
        features_local[1].astype(jnp.float32) * features_local[2].astype(jnp.float32)
    ).astype(jnp.bfloat16)
    signal_rim, kv_rim = passed_along(
        (signal[seq_rows - short_rim :], kv_local[seq_rows - medium_rim :]), "ctx", 1
    )
    signal_pad = jnp.concatenate([signal_rim, signal], 0)
    head_features = short_features(signal_pad[: 2 * short_rim], chan_short, short_rim)
    features = jnp.concatenate([head_features, features_local[:, short_rim:]], 1)
    query_in = features[0]
    key_in = features[1]
    value_in = features[2]
    head_products = (
        key_in[:short_rim].astype(jnp.float32) * value_in[:short_rim].astype(jnp.float32)
    ).astype(jnp.bfloat16)
    products = jnp.concatenate([head_products, kv_local[short_rim:]], 0)
    kv_pad = jnp.concatenate([kv_rim, products], 0)
    gate_grad = (grad_out.astype(jnp.float32) * query_in.astype(jnp.float32)).astype(jnp.bfloat16)
    gate_rim = passed_along(gate_grad[:medium_rim], "ctx", -1)
    gate_ext = jnp.concatenate([gate_grad, gate_rim], 0)
    mixed_out, back_out, taps_grad = medium_terms(medium_taps, kv_pad, gate_ext, 128)
    query_grad = (grad_out.astype(jnp.float32) * mixed_out).astype(jnp.bfloat16)
    key_grad = (back_out * value_in.astype(jnp.float32)).astype(jnp.bfloat16)
    value_grad = (back_out * key_in.astype(jnp.float32)).astype(jnp.bfloat16)
    feature_grads = jnp.stack([query_grad, key_grad, value_grad])
    feature_rim = passed_along(feature_grads[:, :short_rim], "ctx", -1)
    grads_pad = jnp.concatenate([feature_grads, feature_rim], 1)
    running = jnp.zeros((seq_rows, chan_count), jnp.float32)
    short_rows = []
    for offset in range(lag_count):
        running = running + jnp.sum(
            chan_short[:, offset, None, :]
            * grads_pad[:, offset : offset + seq_rows].astype(jnp.float32),
            axis=0,
        )
        lag_start = short_rim - offset
        short_rows.append(
            jnp.sum(
                feature_grads.astype(jnp.float32)
                * signal_pad[None, lag_start : lag_start + seq_rows].astype(jnp.float32),
                axis=1,
            )
        )
    input_grad = running.astype(jnp.bfloat16)
    short_grad = jnp.stack(short_rows, 1).reshape(3 * lag_count, group_count, group_width).sum(-1)
    short_part = owned_sum(short_grad, "ctx")[None]
    medium_part = owned_sum(taps_grad, "ctx")[None]
    incoming = passed_along(input_grad[None], "section", -1)
    return (incoming, short_part, medium_part)


def solution(mesh):
    in_specs = (
        P("section", "ctx", "dp"),
        P("section", "ctx", "dp"),
        P("section", None, "dp"),
        P("section", None, "dp"),
    )
    out_specs = (
        P("section", "ctx", "dp"),
        P("section", None, ("dp", "ctx")),
        P("section", None, ("dp", "ctx")),
    )
    return jax.shard_map(
        per_device, mesh=mesh, in_specs=in_specs, out_specs=out_specs, check_vma=False
    )
```

profile of v0, /device:TPU:1, one launch (start us, length us, event | category | flops | bytes accessed | tf_op | source)
XLA Modules:
  0.0 242.8 jit_solution(7511240758306321144)
XLA Ops:
  1.4 4.4 %collective-permute-start.1 = (bf16[6,1024]{1,0:T(8,128)(2,1)S(1)}, bf16[6,1024]{1,0:T(8,128)(2,1)S(1)}, u32[]{:S(2)}, u32[]{:S(2)}) collective-permute-start(bf16[6,1024]{1,0:T(8,128)(2,1)S(1)} %get-tuple-element.48), channel_id=1, source_target_pairs={{0,4},{4,8},{8,12},{12,16},{16,20},{20,24},{24,28},{28,32},{32,36}... | collective-permute-start | bytes 36872 | tf_op jit(solution)/shard_map/ppermute | solution.py:10
  5.8 1.1 bitcast_convert_fusion.1
  8.7 2.6 %copy.99 = bf16[8,8,128,256]{3,1,2,0:T(8,128)(2,1)S(1)} copy(bf16[8,8,128,256]{3,2,1,0:T(8,128)(2,1)S(1)} %bitcast.87) | data formatting | bytes 8388608
  11.4 2.2 slice.283
  13.6 15.9 %reshape.181 = bf16[64,128,255]{2,1,0:T(8,128)(2,1)} reshape(bf16[64,32640]{1,0:T(8,128)(2,1)} %slice.283) | data formatting | bytes 8355840 | tf_op jit(solution)/shard_map/reshape | solution.py:40
  29.8 1.2 copy.69
  32.0 4.3 %fusion.18 = (f32[256,1024]{1,0:T(8,128)}, f32[256,1024]{1,0:T(8,128)}, f32[256,1024]{1,0:T(8,128)}, f32[256,1024]{1,0:T(8,128)}, f32[256,1024]{1,0:T(8,128)}, /...) fusion(bf16[6,1024]{1,0:T(8,128)(2,1)S(1)} %collective-permute-, ...), kind=kLoop, calls=%fused_computation.58 | loop fusion | flops 7864320 | bytes 13119488 | tf_op jit(solution)/shard_map/convert_element_type | solution.py:151
  36.3 2.6 %copy.68 = f32[256,1024]{0,1:T(8,128)} copy(f32[256,1024]{1,0:T(8,128)} %get-tuple-element.42) | data formatting | bytes 2097152 | tf_op jit(solution)/shard_map/convert_element_type | solution.py:59
  38.9 2.6 %copy.67 = f32[256,1024]{0,1:T(8,128)} copy(f32[256,1024]{1,0:T(8,128)} %get-tuple-element.41) | data formatting | bytes 2097152 | tf_op jit(solution)/shard_map/convert_element_type | solution.py:59
  41.5 2.5 %copy.66 = f32[256,1024]{0,1:T(8,128)} copy(f32[256,1024]{1,0:T(8,128)} %get-tuple-element.40) | data formatting | bytes 2097152 | tf_op jit(solution)/shard_map/convert_element_type | solution.py:59
  44.0 2.5 %copy.65 = f32[256,1024]{0,1:T(8,128)} copy(f32[256,1024]{1,0:T(8,128)} %get-tuple-element.39) | data formatting | bytes 2097152 | tf_op jit(solution)/shard_map/convert_element_type | solution.py:59
  46.5 2.5 %copy.64 = f32[256,1024]{0,1:T(8,128)} copy(f32[256,1024]{1,0:T(8,128)} %get-tuple-element.44) | data formatting | bytes 2097152 | tf_op jit(solution)/shard_map/convert_element_type | solution.py:59
  49.1 1.3 copy.63
  50.4 7.0 %add_convert_fusion = bf16[3,256,1024]{1,2,0:T(8,128)(2,1)S(1)} fusion(f32[256,1024]{0,1:T(8,128)} %copy.68, f32[3,1024]{1,0:T(4,128)S(1)} %get-tuple-element.58, f32[256,1024]{0,1:T(8,128)} %copy.67, f32[3,1024]{1,0:T(4,128)S(1)} %get-tuple-element.59, f32[256,1024]{0,1:T(8,128)} %copy.66, f32[3,1024]{1,0:T(4,128)S(1)} %get-tuple-element.60, ...), kind=kLoop, calls=%fused_computation.23 | loop fusion | flops 11010048 | bytes 8998912 | tf_op jit(solution)/shard_map/convert_element_type | solution.py:60
  57.9 1.0 copy.73
  58.9 1.1 copy.72
  61.0 1.0 copy.70
  62.2 4.3 %collective-permute-start = (bf16[127,1024]{0,1:T(8,128)(2,1)S(1)}, bf16[127,1024]{0,1:T(8,128)(2,1)}, u32[]{:S(2)}, u32[]{:S(2)}) collective-permute-start(bf16[127,1024]{0,1:T(8,128)(2,1)S(1)} %slice_bitcast_fusion.2), channel_id=1, source_target_pairs={{0,4},{4,8},{8,12},{12,16},{16,20},{20,24},{24,28},{28,32},{32,36}... | collective-permute-start | bytes 780296 | tf_op jit(solution)/shard_map/ppermute | solution.py:10
  67.4 6.1 %add_convert_fusion.1 = bf16[3,6,1024]{1,2,0:T(8,128)(2,1)S(1)} fusion(f32[6,1024]{0,1:T(8,128)} %copy.75, f32[3,1024]{1,0:T(4,128)S(1)} %get-tuple-element.58, f32[6,1024]{0,1:T(8,128)S(1)} %copy.74, f32[3,1024]{1,0:T(4,128)S(1)} %get-tuple-element.59, f32[6,1024]{0,1:T(8,128)} %copy.73, f32[3,1024]{1,0:T(4,128)S(1)} %get-tuple-element.60, ...), kind=kLoop, calls=%fused_computation.28 | loop fusion | flops 258048 | bytes 294912 | tf_op jit(solution)/shard_map/convert_element_type | solution.py:60
  75.2 1.6 slice_bitcast_fusion
  76.9 1.6 pad_maximum_fusion.10
  78.5 1.5 fusion.11
  80.0 1.5 copy.113
  81.5 3.1 %reshape.183 = f32[1,256,1024]{1,2,0:T(8,128)} reshape(f32[2,128,64,16]{1,0,3,2:T(2,128)} %bitcast.101) | data formatting | bytes 2097152 | tf_op jit(solution)/shard_map/reshape | solution.py:90
  84.6 1.8 fusion.8
  87.1 1.3 collective-permute-start.2
  88.5 2.5 %copy.82 = f32[256,1024]{0,1:T(8,128)} copy(f32[256,1024]{1,0:T(8,128)} %get-tuple-element.30) | data formatting | bytes 2097152 | tf_op jit(solution)/shard_map/convert_element_type | solution.py:151
  91.1 2.5 %copy.81 = f32[256,1024]{0,1:T(8,128)} copy(f32[256,1024]{1,0:T(8,128)} %get-tuple-element.29) | data formatting | bytes 2097152 | tf_op jit(solution)/shard_map/convert_element_type | solution.py:151
  93.6 2.6 %copy.80 = f32[256,1024]{0,1:T(8,128)} copy(f32[256,1024]{1,0:T(8,128)} %get-tuple-element.28) | data formatting | bytes 2097152 | tf_op jit(solution)/shard_map/convert_element_type | solution.py:151
  96.2 2.6 %copy.83 = f32[256,1024]{0,1:T(8,128)} copy(f32[256,1024]{1,0:T(8,128)} %get-tuple-element.31) | data formatting | bytes 2097152 | tf_op jit(solution)/shard_map/convert_element_type | solution.py:151
  98.7 2.6 %copy.84 = f32[256,1024]{0,1:T(8,128)} copy(f32[256,1024]{1,0:T(8,128)} %get-tuple-element.33) | data formatting | bytes 2097152 | tf_op jit(solution)/shard_map/convert_element_type | solution.py:151
  101.3 2.5 %copy.85 = f32[256,1024]{0,1:T(8,128)} copy(f32[256,1024]{1,0:T(8,128)} %get-tuple-element.32) | data formatting | bytes 2097152 | tf_op jit(solution)/shard_map/convert_element_type | solution.py:151
  103.9 1.1 pad_maximum_fusion.8
  105.0 1.2 pad_maximum_fusion.2
  106.2 4.5 %fusion.10 = f32[64,128,255]{2,1,0:T(8,128)} fusion(bf16[255,64,16]{0,2,1:T(8,128)(2,1)S(1)} %bitcast.97, bf16[255,64,16]{0,2,1:T(8,128)(2,1)S(1)} %bitcast.95, bf16[255,64,16]{0,2,1:T(8,128)(2,1)S(1)} %bitcast.91, bf16[255,64,16]{0,2,1:T(8,128)(2,1)S(1)} %bitcast.99), kind=kOutput, calls=%fused_computation.51 | convolution fusion | flops 136830976 | bytes 10444800 | tf_op jit(solution)/shard_map/tgn,sgn->gts/dot_general | solution.py:83
  110.7 3.7 %reverse = bf16[256,64,32]{0,2,1:T(8,128)(2,1)} reverse(bf16[256,64,32]{0,2,1:T(8,128)(2,1)} %bitcast.100), dimensions={0} | reverse | bytes 2097152
  114.4 5.0 %convolution_bitcast_fusion = f32[128,64,32]{0,2,1:T(8,128)} fusion(bf16[64,128,255]{2,1,0:T(8,128)(2,1)} %reshape.181, bf16[256,64,32]{0,2,1:T(8,128)(2,1)} %reverse), kind=kOutput, calls=%fused_computation.31 | convolution fusion | flops 133693440 | bytes 6275072 | tf_op jit(solution)/shard_map/gts,sgn->tgn/dot_general | solution.py:78
  119.4 2.3 rev.18
  121.8 2.7 %copy.112 = f32[128,64,2,16]{0,2,3,1:T(2,128)} copy(f32[128,64,2,16]{0,3,2,1:T(8,128)} %bitcast.102) | data formatting | bytes 2097152 | tf_op jit(solution)/shard_map/reshape | solution.py:89
  124.5 3.1 %reshape.185 = f32[1,256,1024]{1,2,0:T(8,128)} reshape(f32[2,128,64,16]{1,0,3,2:T(2,128)} %bitcast.103) | data formatting | bytes 2097152 | tf_op jit(solution)/shard_map/reshape | solution.py:90
  127.6 1.9 multiply_convert_fusion.1
  130.1 5.2 %fusion.4 = (f32[3,1024]{1,0:T(4,128)S(1)}, f32[3,1024]{1,0:T(4,128)S(1)}, f32[3,1024]{1,0:T(4,128)S(1)}, f32[3,1024]{1,0:T(4,128)S(1)}, f32[3,1024]{1,0:T(4,128...) fusion(f32[256,1024]{0,1:T(8,128)S(1)} %copy-done.12, ...), kind=kLoop, calls=%fused_computation.13 | loop fusion | flops 14658560 | bytes 10059776 | tf_op jit(solution)/shard_map/reduce_sum | solution.py:149
  136.4 9.1 %collective-permute-start.5 = (f32[16,42]{0,1:T(8,128)S(1)}, f32[16,42]{0,1:T(8,128)S(1)}, u32[]{:S(2)}, u32[]{:S(2)}) collective-permute-start(f32[16,42]{0,1:T(8,128)S(1)} %copy.98), channel_id=1, source_target_pairs={{0,64},{4,68},{8,72},{12,76},{16,80},{20,84},{24,88},{28,92},{32,9... | collective-permute-start | bytes 8072 | tf_op jit(solution)/shard_map/ppermute | solution.py:29
  145.6 1.2 pad_maximum_fusion.1
  147.3 1.5 collective-permute-start.3
  148.9 9.3 %reshape.189 = f32[64,32640]{1,0:T(8,128)} reshape(f32[64,128,255]{2,1,0:T(8,128)} %fusion.10) | data formatting | bytes 16711680 | tf_op jit(solution)/shard_map/reshape | solution.py:46
  158.1 4.0 %pad.6 = f32[64,32768]{1,0:T(8,128)S(1)} pad(f32[64,32640]{1,0:T(8,128)} %reshape.189, f32[]{:T(128)} %constant.104.clone.1), padding=0_0x0_128 | pad | bytes 16744452 | tf_op jit(solution)/shard_map/jit(_pad)/pad | solution.py:45
  162.2 2.5 %copy.100 = f32[8,8,128,256]{3,2,1,0:T(8,128)S(1)} copy(f32[8,8,128,256]{3,1,2,0:T(8,128)S(1)} %bitcast.85) | data formatting | bytes 16777216
  164.8 11.1 %collective-permute-start.6 = (f32[8,42]{0,1:T(8,128)S(1)}, f32[8,42]{0,1:T(8,128)S(1)}, u32[]{:S(2)}, u32[]{:S(2)}) collective-permute-start(f32[8,42]{0,1:T(8,128)S(1)} %constant_dynamic-slice_fusion.11), channel_id=1, source_target_pairs={{0,32},{4,36},{8,40},{12,44},{16,48},{20,52},{24,56},{28,60},{32,0... | collective-permute-start | bytes 4040 | tf_op jit(solution)/shard_map/ppermute | solution.py:29
  176.5 1.8 collective-permute-done.6
  178.5 4.4 %collective-permute-start.7 = (f32[4,42]{0,1:T(8,128)S(1)}, f32[4,42]{0,1:T(8,128)S(1)}, u32[]{:S(2)}, u32[]{:S(2)}) collective-permute-start(f32[4,42]{0,1:T(8,128)S(1)} %constant_dynamic-slice_fusion.10), channel_id=1, source_target_pairs={{0,16},{4,20},{8,24},{12,28},{16,0},{20,4},{24,8},{28,12},{32,48},... | collective-permute-start | bytes 2024 | tf_op jit(solution)/shard_map/ppermute | solution.py:29
  182.9 3.4 %collective-permute-start.10 = (f32[16,256]{1,0:T(8,128)S(1)}, f32[16,256]{1,0:T(8,128)S(1)}, u32[]{:S(2)}, u32[]{:S(2)}) collective-permute-start(f32[16,256]{1,0:T(8,128)S(1)} %constant_dynamic-slice_fusion.7), channel_id=1, source_target_pairs={{0,64},{4,68},{8,72},{12,76},{16,80},{20,84},{24,88},{28,92},{32,9... | collective-permute-start | bytes 49160 | tf_op jit(solution)/shard_map/ppermute | solution.py:29
  187.3 3.0 %collective-permute-start.8 = (f32[2,42]{0,1:T(8,128)S(1)}, f32[2,42]{0,1:T(8,128)S(1)}, u32[]{:S(2)}, u32[]{:S(2)}) collective-permute-start(f32[2,42]{0,1:T(8,128)S(1)} %constant_dynamic-slice_fusion.9), channel_id=1, source_target_pairs={{0,8},{4,12},{8,0},{12,4},{16,24},{20,28},{24,16},{28,20},{32,40},... | collective-permute-start | bytes 1016 | tf_op jit(solution)/shard_map/ppermute | solution.py:29
  190.4 10.2 %collective-permute-start.11 = (f32[8,256]{1,0:T(8,128)S(1)}, f32[8,256]{1,0:T(8,128)S(1)}, u32[]{:S(2)}, u32[]{:S(2)}) collective-permute-start(f32[8,256]{1,0:T(8,128)S(1)} %constant_dynamic-slice_fusion.6), channel_id=1, source_target_pairs={{0,32},{4,36},{8,40},{12,44},{16,48},{20,52},{24,56},{28,60},{32,0... | collective-permute-start | bytes 24584 | tf_op jit(solution)/shard_map/ppermute | solution.py:29
  200.7 2.8 %collective-permute-done.11 = f32[8,256]{1,0:T(8,128)S(1)} collective-permute-done((f32[8,256]{1,0:T(8,128)S(1)}, f32[8,256]{1,0:T(8,128)S(1)}, u32[]{:S(2)}, u32[]{:S(2)}) %collective-permute-start.11) | collective-permute-done | bytes 8224 | tf_op jit(solution)/shard_map/ppermute | solution.py:29
  203.5 6.3 %collective-permute-start.12 = (f32[4,256]{1,0:T(4,128)S(1)}, f32[4,256]{1,0:T(4,128)S(1)}, u32[]{:S(2)}, u32[]{:S(2)}) collective-permute-start(f32[4,256]{1,0:T(4,128)S(1)} %constant_dynamic-slice_fusion.4), channel_id=1, source_target_pairs={{0,16},{4,20},{8,24},{12,28},{16,0},{20,4},{24,8},{28,12},{32,48},... | collective-permute-start | bytes 12296 | tf_op jit(solution)/shard_map/ppermute | solution.py:29
  209.9 3.3 %collective-permute-start.9 = (f32[1,42]{0,1:T(8,128)S(1)}, f32[1,42]{0,1:T(8,128)S(1)}, u32[]{:S(2)}, u32[]{:S(2)}) collective-permute-start(f32[1,42]{0,1:T(8,128)S(1)} %constant_dynamic-slice_fusion.8), channel_id=1, source_target_pairs={{0,4},{4,0},{8,12},{12,8},{16,20},{20,16},{24,28},{28,24},{32,36},... | collective-permute-start | bytes 512 | tf_op jit(solution)/shard_map/ppermute | solution.py:29
  213.3 1.9 collective-permute-start.13
  215.2 1.2 copy.79
  216.4 1.4 pad_maximum_fusion
  217.9 6.1 %multiply_reduce_fusion.5 = (f32[256,1024]{0,1:T(8,128)S(1)}, f32[256,1024]{0,1:T(8,128)S(1)}, f32[256,1024]{0,1:T(8,128)S(1)}, f32[256,1024]{0,1:T(8,128)S(1)},...) fusion(bf16[3,262,1024]{1,2,0:T(8,128)(2,1)S(1)} %pad_maximum_fusion, f32[3,1024]{1,0:T(4,128)S(1)} %get-tuple-element.63, ...), kind=kLoop, calls=%fused_computation.22 | loop fusion | flops 12582912 | bytes 15802368 | tf_op jit(solution)/shard_map/reduce_sum | solution.py:142
  224.4 8.1 %collective-permute-start.4 = (bf16[1,256,1024]{1,2,0:T(8,128)(2,1)S(1)}, bf16[1,256,1024]{1,2,0:T(8,128)(2,1)S(1)}, u32[]{:S(2)}, u32[]{:S(2)}) collective-permute-start(bf16[1,256,1024]{1,2,0:T(8,128)(2,1)S(1)} %fusion.12), channel_id=1, source_target_pairs={{128,0},{256,128},{384,256},{129,1},{257,129},{385,257},{130,2},{2... | collective-permute-start | bytes 1572872 | tf_op jit(solution)/shard_map/ppermute | solution.py:10
  232.5 4.0 %collective-permute-start.14 = (f32[1,256]{1,0:T(1,128)S(1)}, f32[1,256]{1,0:T(1,128)S(1)}, u32[]{:S(2)}, u32[]{:S(2)}) collective-permute-start(f32[1,256]{1,0:T(1,128)S(1)} %constant_dynamic-slice_fusion), channel_id=1, source_target_pairs={{0,4},{4,0},{8,12},{12,8},{16,20},{20,16},{24,28},{28,24},{32,36},... | collective-permute-start | bytes 3080 | tf_op jit(solution)/shard_map/ppermute | solution.py:29
  238.0 3.7 %collective-permute-done.4 = bf16[1,256,1024]{1,2,0:T(8,128)(2,1)S(1)} collective-permute-done((bf16[1,256,1024]{1,2,0:T(8,128)(2,1)S(1)}, bf16[1,256,1024]{1,2,0:T(8,128)(2,1)S(1)}, u32[]{:S(2)}, u32[]{:S(2)}) %collective-permute-start.4) | collective-permute-done | bytes 524320 | tf_op jit(solution)/shard_map/ppermute | solution.py:10
  (115 shorter events, 16.0 us)
Async XLA Ops:
  0.6 7.7 %copy-start.18 = (bf16[1,128,64]{1,2,0:T(8,128)(2,1)S(1)}, bf16[1,128,64]{1,2,0:T(8,128)(2,1)}, u32[]{:S(2)}) copy-start(bf16[1,128,64]{1,2,0:T(8,128)(2,1)} %param.7) | copy-start | bytes 49156
  1.4 30.6 %collective-permute-start.1 = (bf16[6,1024]{1,0:T(8,128)(2,1)S(1)}, bf16[6,1024]{1,0:T(8,128)(2,1)S(1)}, u32[]{:S(2)}, u32[]{:S(2)}) collective-permute-start(bf16[6,1024]{1,0:T(8,128)(2,1)S(1)} %get-tuple-element.48), channel_id=1, source_target_pairs={{0,4},{4,8},{8,12},{12,16},{16,20},{20,24},{24,28},{28,32},{32,36}... | collective-permute-start | bytes 36872 | tf_op jit(solution)/shard_map/ppermute | solution.py:10
  13.6 17.4 %copy-start.17 = (bf16[1,256,1024]{2,1,0:T(8,128)(2,1)S(1)}, bf16[1,256,1024]{2,1,0:T(8,128)(2,1)}, u32[]{:S(2)}) copy-start(bf16[1,256,1024]{2,1,0:T(8,128)(2,1)} %param.5) | copy-start | bytes 1572868
  29.4 2.6 %copy-start.7 = (bf16[1,256,1024]{2,1,0:T(8,128)(2,1)S(1)}, bf16[1,256,1024]{2,1,0:T(8,128)(2,1)}, u32[]{:S(2)}) copy-start(bf16[1,256,1024]{2,1,0:T(8,128)(2,1)} %param.4) | copy-start | bytes 1572868
  29.8 20.6 %copy-start.3 = (f32[256,1024]{0,1:T(8,128)}, f32[256,1024]{0,1:T(8,128)S(1)}, u32[]{:S(2)}) copy-start(f32[256,1024]{0,1:T(8,128)S(1)} %copy.62) | copy-start | bytes 3145732
  57.5 10.0 %copy-start.16 = (f32[6,1024]{0,1:T(8,128)S(1)}, f32[6,1024]{0,1:T(8,128)}, u32[]{:S(2)}) copy-start(f32[6,1024]{0,1:T(8,128)} %copy.69) | copy-start | bytes 73732
  57.6 16.0 %copy-start.15 = (bf16[1,256,1024]{1,2,0:T(8,128)(2,1)}, bf16[1,256,1024]{1,2,0:T(8,128)(2,1)S(1)}, u32[]{:S(2)}) copy-start(bf16[1,256,1024]{1,2,0:T(8,128)(2,1)S(1)} %multiply_convert_fusion.2) | copy-start | bytes 1572868
  62.2 14.7 %collective-permute-start = (bf16[127,1024]{0,1:T(8,128)(2,1)S(1)}, bf16[127,1024]{0,1:T(8,128)(2,1)}, u32[]{:S(2)}, u32[]{:S(2)}) collective-permute-start(bf16[127,1024]{0,1:T(8,128)(2,1)S(1)} %slice_bitcast_fusion.2), channel_id=1, source_target_pairs={{0,4},{4,8},{8,12},{12,16},{16,20},{20,24},{24,28},{28,32},{32,36}... | collective-permute-start | bytes 780296 | tf_op jit(solution)/shard_map/ppermute | solution.py:10
  73.6 0.9 copy-start.1
  74.5 3.9 %copy-start = (bf16[64,128,255]{2,1,0:T(8,128)(2,1)S(1)}, bf16[64,128,255]{2,1,0:T(8,128)(2,1)}, u32[]{:S(2)}) copy-start(bf16[64,128,255]{2,1,0:T(8,128)(2,1)} %reshape.181) | copy-start | bytes 12533764
  78.4 1.5 copy-start.8
  78.5 1.5 copy-start.10
  80.0 4.6 %copy-start.2 = (bf16[3,6,1024]{1,2,0:T(8,128)(2,1)S(1)}, bf16[3,6,1024]{1,2,0:T(8,128)(2,1)}, u32[]{:S(2)}) copy-start(bf16[3,6,1024]{1,2,0:T(8,128)(2,1)} %copy-done.1) | copy-start | bytes 110596
  87.1 16.8 %collective-permute-start.2 = (bf16[127,1024]{0,1:T(8,128)(2,1)}, bf16[127,1024]{0,1:T(8,128)(2,1)}, u32[]{:S(2)}, u32[]{:S(2)}) collective-permute-start(bf16[127,1024]{0,1:T(8,128)(2,1)} %slice_bitcast_fusion.1), channel_id=1, source_target_pairs={{4,0},{8,4},{12,8},{16,12},{20,16},{24,20},{28,24},{32,28},{36,32}... | collective-permute-start | bytes 780296 | tf_op jit(solution)/shard_map/ppermute | solution.py:10
  103.9 2.3 copy-start.9
  103.9 2.4 copy-start.11
  127.6 1.9 copy-start.4
  127.6 2.0 copy-start.12
  127.6 2.2 copy-start.13
  127.6 2.5 %copy-start.14 = (f32[256,1024]{0,1:T(8,128)S(1)}, f32[256,1024]{0,1:T(8,128)}, u32[]{:S(2)}) copy-start(f32[256,1024]{0,1:T(8,128)} %copy.80) | copy-start | bytes 3145732
  129.6 5.8 %copy-start.5 = (bf16[1,256,1024]{1,2,0:T(8,128)(2,1)}, bf16[1,256,1024]{1,2,0:T(8,128)(2,1)S(1)}, u32[]{:S(2)}) copy-start(bf16[1,256,1024]{1,2,0:T(8,128)(2,1)S(1)} %get-tuple-element.21) | copy-start | bytes 1572868
  136.4 28.3 %collective-permute-start.5 = (f32[16,42]{0,1:T(8,128)S(1)}, f32[16,42]{0,1:T(8,128)S(1)}, u32[]{:S(2)}, u32[]{:S(2)}) collective-permute-start(f32[16,42]{0,1:T(8,128)S(1)} %copy.98), channel_id=1, source_target_pairs={{0,64},{4,68},{8,72},{12,76},{16,80},{20,84},{24,88},{28,92},{32,9... | collective-permute-start | bytes 8072 | tf_op jit(solution)/shard_map/ppermute | solution.py:29
  147.3 68.0 %collective-permute-start.3 = (bf16[3,6,1024]{2,1,0:T(8,128)(2,1)S(1)}, bf16[3,6,1024]{2,1,0:T(8,128)(2,1)S(1)}, u32[]{:S(2)}, u32[]{:S(2)}) collective-permute-start(bf16[3,6,1024]{2,1,0:T(8,128)(2,1)S(1)} %copy.78), channel_id=1, source_target_pairs={{4,0},{8,4},{12,8},{16,12},{20,16},{24,20},{28,24},{32,28},{36,32}... | collective-permute-start | bytes 110600 | tf_op jit(solution)/shard_map/ppermute | solution.py:10
  164.7 51.8 %copy-start.6 = (bf16[1,256,1024]{1,2,0:T(8,128)(2,1)S(1)}, bf16[1,256,1024]{1,2,0:T(8,128)(2,1)}, u32[]{:S(2)}) copy-start(bf16[1,256,1024]{1,2,0:T(8,128)(2,1)} %copy-done.5) | copy-start | bytes 1572868
  164.8 13.5 %collective-permute-start.6 = (f32[8,42]{0,1:T(8,128)S(1)}, f32[8,42]{0,1:T(8,128)S(1)}, u32[]{:S(2)}, u32[]{:S(2)}) collective-permute-start(f32[8,42]{0,1:T(8,128)S(1)} %constant_dynamic-slice_fusion.11), channel_id=1, source_target_pairs={{0,32},{4,36},{8,40},{12,44},{16,48},{20,52},{24,56},{28,60},{32,0... | collective-permute-start | bytes 4040 | tf_op jit(solution)/shard_map/ppermute | solution.py:29
  178.5 8.7 %collective-permute-start.7 = (f32[4,42]{0,1:T(8,128)S(1)}, f32[4,42]{0,1:T(8,128)S(1)}, u32[]{:S(2)}, u32[]{:S(2)}) collective-permute-start(f32[4,42]{0,1:T(8,128)S(1)} %constant_dynamic-slice_fusion.10), channel_id=1, source_target_pairs={{0,16},{4,20},{8,24},{12,28},{16,0},{20,4},{24,8},{28,12},{32,48},... | collective-permute-start | bytes 2024 | tf_op jit(solution)/shard_map/ppermute | solution.py:29
  182.9 7.4 %collective-permute-start.10 = (f32[16,256]{1,0:T(8,128)S(1)}, f32[16,256]{1,0:T(8,128)S(1)}, u32[]{:S(2)}, u32[]{:S(2)}) collective-permute-start(f32[16,256]{1,0:T(8,128)S(1)} %constant_dynamic-slice_fusion.7), channel_id=1, source_target_pairs={{0,64},{4,68},{8,72},{12,76},{16,80},{20,84},{24,88},{28,92},{32,9... | collective-permute-start | bytes 49160 | tf_op jit(solution)/shard_map/ppermute | solution.py:29
  187.3 13.3 %collective-permute-start.8 = (f32[2,42]{0,1:T(8,128)S(1)}, f32[2,42]{0,1:T(8,128)S(1)}, u32[]{:S(2)}, u32[]{:S(2)}) collective-permute-start(f32[2,42]{0,1:T(8,128)S(1)} %constant_dynamic-slice_fusion.9), channel_id=1, source_target_pairs={{0,8},{4,12},{8,0},{12,4},{16,24},{20,28},{24,16},{28,20},{32,40},... | collective-permute-start | bytes 1016 | tf_op jit(solution)/shard_map/ppermute | solution.py:29
  190.4 13.1 %collective-permute-start.11 = (f32[8,256]{1,0:T(8,128)S(1)}, f32[8,256]{1,0:T(8,128)S(1)}, u32[]{:S(2)}, u32[]{:S(2)}) collective-permute-start(f32[8,256]{1,0:T(8,128)S(1)} %constant_dynamic-slice_fusion.6), channel_id=1, source_target_pairs={{0,32},{4,36},{8,40},{12,44},{16,48},{20,52},{24,56},{28,60},{32,0... | collective-permute-start | bytes 24584 | tf_op jit(solution)/shard_map/ppermute | solution.py:29
  203.5 9.7 %collective-permute-start.12 = (f32[4,256]{1,0:T(4,128)S(1)}, f32[4,256]{1,0:T(4,128)S(1)}, u32[]{:S(2)}, u32[]{:S(2)}) collective-permute-start(f32[4,256]{1,0:T(4,128)S(1)} %constant_dynamic-slice_fusion.4), channel_id=1, source_target_pairs={{0,16},{4,20},{8,24},{12,28},{16,0},{20,4},{24,8},{28,12},{32,48},... | collective-permute-start | bytes 12296 | tf_op jit(solution)/shard_map/ppermute | solution.py:29
  209.9 26.6 %collective-permute-start.9 = (f32[1,42]{0,1:T(8,128)S(1)}, f32[1,42]{0,1:T(8,128)S(1)}, u32[]{:S(2)}, u32[]{:S(2)}) collective-permute-start(f32[1,42]{0,1:T(8,128)S(1)} %constant_dynamic-slice_fusion.8), channel_id=1, source_target_pairs={{0,4},{4,0},{8,12},{12,8},{16,20},{20,16},{24,28},{28,24},{32,36},... | collective-permute-start | bytes 512 | tf_op jit(solution)/shard_map/ppermute | solution.py:29
  213.3 19.2 %collective-permute-start.13 = (f32[2,256]{1,0:T(2,128)S(1)}, f32[2,256]{1,0:T(2,128)S(1)}, u32[]{:S(2)}, u32[]{:S(2)}) collective-permute-start(f32[2,256]{1,0:T(2,128)S(1)} %constant_dynamic-slice_fusion.2), channel_id=1, source_target_pairs={{0,8},{4,12},{8,0},{12,4},{16,24},{20,28},{24,16},{28,20},{32,40},... | collective-permute-start | bytes 6152 | tf_op jit(solution)/shard_map/ppermute | solution.py:29
  224.4 17.3 %collective-permute-start.4 = (bf16[1,256,1024]{1,2,0:T(8,128)(2,1)S(1)}, bf16[1,256,1024]{1,2,0:T(8,128)(2,1)S(1)}, u32[]{:S(2)}, u32[]{:S(2)}) collective-permute-start(bf16[1,256,1024]{1,2,0:T(8,128)(2,1)S(1)} %fusion.12), channel_id=1, source_target_pairs={{128,0},{256,128},{384,256},{129,1},{257,129},{385,257},{130,2},{2... | collective-permute-start | bytes 1572872 | tf_op jit(solution)/shard_map/ppermute | solution.py:10
  232.5 4.9 %collective-permute-start.14 = (f32[1,256]{1,0:T(1,128)S(1)}, f32[1,256]{1,0:T(1,128)S(1)}, u32[]{:S(2)}, u32[]{:S(2)}) collective-permute-start(f32[1,256]{1,0:T(1,128)S(1)} %constant_dynamic-slice_fusion), channel_id=1, source_target_pairs={{0,4},{4,0},{8,12},{12,8},{16,20},{20,16},{24,28},{28,24},{32,36},... | collective-permute-start | bytes 3080 | tf_op jit(solution)/shard_map/ppermute | solution.py:29
where the time goes:
time: 246 us; the launch traced here: 243 us
  local copies, waits for them, and re-layouts  101 us (41%)
  starting transfers between devices  76.3 us (31%)
  other arithmetic  43.4 us (18%)
  matrix products  11 us (4%)
  waiting for transfers between devices  9.33 us (4%)
    ppermute x10, starting transfers between devices, owned_sum(): chunks = kept + lax.ppermute(sent, axis, route)  56.8 us
    convert_element_type x13, local copies, waits for them, and re-layouts, short_features(): running = running + chan_short[:, offset, None, :] * padded[None, first_r...  20.6 us
    ppermute x5, starting transfers between devices, passed_along(): return lax.ppermute(block, axis, route)  19.5 us
    reshape x1, local copies, waits for them, and re-layouts, band_matrix(): return tiled_rows.reshape(group_count, out_rows, span_len)  15.9 us
    convert_element_type x6, local copies, waits for them, and re-layouts, per_device(): signal_pad[None, lag_start:lag_start + seq_rows].astype(jnp.float32)  15.3 us
    convert_element_type x2, other arithmetic, short_features(): return running.astype(jnp.bfloat16)  13.2 us
    unnamed x50, local copies, waits for them, and re-layouts  12.5 us
    reshape x1, local copies, waits for them, and re-layouts, diagonal_sums(): cross_terms.reshape(group_count, out_rows * span_len)  9.26 us
  transfers between devices with their start and end apart: 15, of which 5 were waited for; matrix products, arithmetic and copies ran while one was open for 33% of the time, Pallas kernels for 0%

commit v1 on v0

--- a/solution.py
+++ b/solution.py
@@ -14,21 +14,8 @@
     axis_len = lax.axis_size(axis)
     row_count, col_count = partial_terms.shape
     width = col_count // axis_len
-    chunks = partial_terms.reshape(row_count, axis_len, width).transpose(1, 2, 0)
-    chunks = chunks.reshape(axis_len, width * row_count)
-    if axis_len & (axis_len - 1):
-        gathered = lax.all_gather(chunks, axis, axis=0, tiled=False)
-        return jnp.sum(gathered[:, lax.axis_index(axis)], axis=0).reshape(width, row_count).T
-    here = lax.axis_index(axis)
-    span = axis_len // 2
-    while span >= 1:
-        upper = (here // span) % 2
-        kept = lax.dynamic_slice_in_dim(chunks, upper * span, span, 0)
-        sent = lax.dynamic_slice_in_dim(chunks, (1 - upper) * span, span, 0)
-        route = [(i, i ^ span) for i in range(axis_len)]
-        chunks = kept + lax.ppermute(sent, axis, route)
-        span //= 2
-    return chunks[0].reshape(width, row_count).T
+    chunks = partial_terms.reshape(row_count, axis_len, width).transpose(1, 0, 2)
+    return jnp.sum(lax.all_to_all(chunks, axis, 0, 0, tiled=False), axis=0)
 
 
 def band_matrix(filter_taps, out_rows):
@@ -154,8 +141,10 @@
         )
     input_grad = running.astype(jnp.bfloat16)
     short_grad = jnp.stack(short_rows, 1).reshape(3 * lag_count, group_count, group_width).sum(-1)
-    short_part = owned_sum(short_grad, "ctx")[None]
-    medium_part = owned_sum(taps_grad, "ctx")[None]
+    short_count = short_grad.shape[0]
+    both_part = owned_sum(jnp.concatenate([short_grad, taps_grad], 0), "ctx")
+    short_part = both_part[None, :short_count]
+    medium_part = both_part[None, short_count:]
     incoming = passed_along(input_grad[None], "section", -1)
     return (incoming, short_part, medium_part)
 

time: 246 us -> 204 us (0.83)
  starting transfers between devices: 76.3 us -> 33.2 us
  local copies, waits for them, and re-layouts: 101 us -> 107 us
    ppermute x10 -> x0, starting transfers between devices: 56.8 us -> none  [owned_sum(): chunks = kept + lax.ppermute(sent, axis, route)]
    all_to_all x0 -> x1, starting transfers between devices: none -> 18 us  [owned_sum(): return jnp.sum(lax.all_to_all(chunks, axis, 0, 0, tiled=False), axis=0)]
    ppermute x10 -> x0, waiting for transfers between devices: 5.59 us -> none  [owned_sum(): chunks = kept + lax.ppermute(sent, axis, route)]
    ppermute x5, starting transfers between devices: 19.5 us -> 15.2 us  [passed_along(): return lax.ppermute(block, axis, route)]
    ppermute x5, waiting for transfers between devices: 3.74 us -> 7.94 us  [passed_along(): return lax.ppermute(block, axis, route)]
    slice x2, local copies, waits for them, and re-layouts: 0.44 us -> 3.49 us  [per_device(): feature_rim = passed_along(feature_grads[:, :short_rim], 'ctx', -1)]
    convert_element_type x13, local copies, waits for them, and re-layouts: 20.6 us -> 23.6 us  [short_features(): running = running + chan_short[:, offset, None, :] * padded[None, first_r...]
    unnamed x50 -> x55, local copies, waits for them, and re-layouts: 12.5 us -> 12.6 us
  transfers between devices with their start and end apart: 15 -> 6, of which waited for: 5 -> 1; matrix products, arithmetic and copies ran while one was open for 33% -> 34% of each run, Pallas kernels for 0% -> 0%
where the time goes in v1:
time: 204 us; the launch traced here: 202 us
  local copies, waits for them, and re-layouts  107 us (52%)
  other arithmetic  42.4 us (21%)
  starting transfers between devices  33.2 us (16%)
  matrix products  11 us (5%)
  waiting for transfers between devices  7.94 us (4%)
    convert_element_type x13, local copies, waits for them, and re-layouts, short_features(): running = running + chan_short[:, offset, None, :] * padded[None, first_r...  23.6 us
    all_to_all x1, starting transfers between devices, owned_sum(): return jnp.sum(lax.all_to_all(chunks, axis, 0, 0, tiled=False), axis=0)  18 us
    reshape x1, local copies, waits for them, and re-layouts, band_matrix(): return tiled_rows.reshape(group_count, out_rows, span_len)  15.9 us
    convert_element_type x6, local copies, waits for them, and re-layouts, per_device(): signal_pad[None, lag_start:lag_start + seq_rows].astype(jnp.float32)  15.2 us
    ppermute x5, starting transfers between devices, passed_along(): return lax.ppermute(block, axis, route)  15.2 us
    convert_element_type x2, other arithmetic, short_features(): return running.astype(jnp.bfloat16)  13.1 us
    unnamed x55, local copies, waits for them, and re-layouts  12.6 us
    reshape x1, local copies, waits for them, and re-layouts, diagonal_sums(): cross_terms.reshape(group_count, out_rows * span_len)  9.26 us
  transfers between devices with their start and end apart: 6, of which 1 were waited for; matrix products, arithmetic and copies ran while one was open for 34% of the time, Pallas kernels for 0%

profile of v1, /device:TPU:1, one launch (start us, length us, event | category | flops | bytes accessed | tf_op | source)
XLA Modules:
  0.0 202.3 jit_solution(13320131947946531487)
XLA Ops:
  0.6 0.7 bitcast_convert_fusion
  1.4 4.4 %collective-permute-start.1 = (bf16[6,1024]{1,0:T(8,128)(2,1)S(1)}, bf16[6,1024]{1,0:T(8,128)(2,1)S(1)}, u32[]{:S(2)}, u32[]{:S(2)}) collective-permute-start(bf16[6,1024]{1,0:T(8,128)(2,1)S(1)} %get-tuple-element.57), channel_id=1, source_target_pairs={{0,4},{4,8},{8,12},{12,16},{16,20},{20,24},{24,28},{28,32},{32,36}... | collective-permute-start | bytes 36872 | tf_op jit(solution)/shard_map/ppermute | solution.py:10
  5.8 1.1 bitcast_convert_fusion.1
  6.9 0.7 reshape.181
  8.7 1.2 copy.128
  10.3 2.6 %copy.158 = bf16[8,8,128,256]{3,1,2,0:T(8,128)(2,1)S(1)} copy(bf16[8,8,128,256]{3,2,1,0:T(8,128)(2,1)S(1)} %bitcast.75) | data formatting | bytes 8388608
  12.9 2.2 %slice.291 = bf16[64,32640]{1,0:T(8,128)(2,1)} slice(bf16[64,32768]{1,0:T(8,128)(2,1)S(1)} %bitcast.76), slice={[0:64], [0:32640]} | slice | bytes 8355840 | tf_op jit(solution)/shard_map/slice | solution.py:26
  15.1 15.9 %reshape.172 = bf16[64,128,255]{2,1,0:T(8,128)(2,1)} reshape(bf16[64,32640]{1,0:T(8,128)(2,1)} %slice.291) | data formatting | bytes 8355840 | tf_op jit(solution)/shard_map/reshape | solution.py:27
  31.0 1.0 copy.120
  32.1 4.3 %fusion.18 = (f32[256,1024]{1,0:T(8,128)}, f32[256,1024]{1,0:T(8,128)}, f32[256,1024]{1,0:T(8,128)}, f32[256,1024]{1,0:T(8,128)}, f32[256,1024]{1,0:T(8,128)}, /...) fusion(bf16[6,1024]{1,0:T(8,128)(2,1)S(1)} %collective-permute-, ...), kind=kLoop, calls=%fused_computation.58 | loop fusion | flops 7864320 | bytes 13119488 | tf_op jit(solution)/shard_map/convert_element_type | solution.py:138
  36.4 2.6 %copy.122 = f32[256,1024]{0,1:T(8,128)} copy(f32[256,1024]{1,0:T(8,128)} %get-tuple-element.52) | data formatting | bytes 2097152 | tf_op jit(solution)/shard_map/convert_element_type | solution.py:46
  39.0 2.6 %copy.123 = f32[256,1024]{0,1:T(8,128)} copy(f32[256,1024]{1,0:T(8,128)} %get-tuple-element.53) | data formatting | bytes 2097152 | tf_op jit(solution)/shard_map/convert_element_type | solution.py:46
  41.5 2.5 %copy.124 = f32[256,1024]{0,1:T(8,128)} copy(f32[256,1024]{1,0:T(8,128)} %get-tuple-element.48) | data formatting | bytes 2097152 | tf_op jit(solution)/shard_map/convert_element_type | solution.py:46
  44.1 2.5 %copy.125 = f32[256,1024]{0,1:T(8,128)} copy(f32[256,1024]{1,0:T(8,128)} %get-tuple-element.49) | data formatting | bytes 2097152 | tf_op jit(solution)/shard_map/convert_element_type | solution.py:46
  46.6 2.5 %copy.126 = f32[256,1024]{0,1:T(8,128)} copy(f32[256,1024]{1,0:T(8,128)} %get-tuple-element.50) | data formatting | bytes 2097152 | tf_op jit(solution)/shard_map/convert_element_type | solution.py:46
  49.1 1.3 copy.127
  50.5 7.0 %add_convert_fusion = bf16[3,256,1024]{1,2,0:T(8,128)(2,1)S(1)} fusion(f32[256,1024]{0,1:T(8,128)} %copy.127, f32[3,1024]{1,0:T(4,128)S(1)} %get-tuple-element.65, f32[256,1024]{0,1:T(8,128)} %copy.126, f32[3,1024]{1,0:T(4,128)S(1)} %get-tuple-element.66, f32[256,1024]{0,1:T(8,128)} %copy.125, f32[3,1024]{1,0:T(4,128)S(1)} %get-tuple-element.67, ...), kind=kLoop, calls=%fused_computation.23 | loop fusion | flops 11010048 | bytes 8998912 | tf_op jit(solution)/shard_map/convert_element_type | solution.py:47
  57.8 4.3 %collective-permute-start = (bf16[127,1024]{0,1:T(8,128)(2,1)S(1)}, bf16[127,1024]{0,1:T(8,128)(2,1)}, u32[]{:S(2)}, u32[]{:S(2)}) collective-permute-start(bf16[127,1024]{0,1:T(8,128)(2,1)S(1)} %slice_bitcast_fusion.2), channel_id=1, source_target_pairs={{0,4},{4,8},{8,12},{12,16},{16,20},{20,24},{24,28},{28,32},{32,36}... | collective-permute-start | bytes 780296 | tf_op jit(solution)/shard_map/ppermute | solution.py:10
  62.8 1.0 copy.129
  63.7 1.0 copy.130
  64.7 1.8 copy.131
  66.5 1.8 copy.132
  68.3 1.8 copy.133
  70.1 1.0 copy.134
  71.1 6.1 %add_convert_fusion.1 = bf16[3,6,1024]{1,2,0:T(8,128)(2,1)S(1)} fusion(f32[6,1024]{0,1:T(8,128)} %copy.134, f32[3,1024]{1,0:T(4,128)S(1)} %get-tuple-element.65, f32[6,1024]{0,1:T(8,128)} %copy.133, f32[3,1024]{1,0:T(4,128)S(1)} %get-tuple-element.66, f32[6,1024]{0,1:T(8,128)} %copy.132, f32[3,1024]{1,0:T(4,128)S(1)} %get-tuple-element.67, ...), kind=kLoop, calls=%fused_computation.28 | loop fusion | flops 258048 | bytes 294912 | tf_op jit(solution)/shard_map/convert_element_type | solution.py:47
  77.2 0.9 copy-done.1
  78.1 0.7 slice.292
  79.1 1.9 pad_maximum_fusion.10
  81.0 1.5 fusion.11
  82.5 1.5 copy.170
  84.0 3.1 %reshape.174 = f32[1,256,1024]{1,2,0:T(8,128)} reshape(f32[2,128,64,16]{1,0,3,2:T(2,128)} %bitcast.89) | data formatting | bytes 2097152 | tf_op jit(solution)/shard_map/reshape | solution.py:77
  87.1 1.8 fusion.8
  88.9 0.7 slice_bitcast_fusion.1
  89.6 1.3 collective-permute-start.2
  90.9 2.5 %copy.139 = f32[256,1024]{0,1:T(8,128)} copy(f32[256,1024]{1,0:T(8,128)} %get-tuple-element.37) | data formatting | bytes 2097152 | tf_op jit(solution)/shard_map/convert_element_type | solution.py:138
  93.4 2.5 %copy.140 = f32[256,1024]{0,1:T(8,128)} copy(f32[256,1024]{1,0:T(8,128)} %get-tuple-element.38) | data formatting | bytes 2097152 | tf_op jit(solution)/shard_map/convert_element_type | solution.py:138
  96.0 2.5 %copy.141 = f32[256,1024]{0,1:T(8,128)} copy(f32[256,1024]{1,0:T(8,128)} %get-tuple-element.39) | data formatting | bytes 2097152 | tf_op jit(solution)/shard_map/convert_element_type | solution.py:138
  98.5 2.6 %copy.142 = f32[256,1024]{0,1:T(8,128)} copy(f32[256,1024]{1,0:T(8,128)} %get-tuple-element.40) | data formatting | bytes 2097152 | tf_op jit(solution)/shard_map/convert_element_type | solution.py:138
  101.0 2.5 %copy.143 = f32[256,1024]{0,1:T(8,128)} copy(f32[256,1024]{1,0:T(8,128)} %get-tuple-element.42) | data formatting | bytes 2097152 | tf_op jit(solution)/shard_map/convert_element_type | solution.py:138
  103.6 2.6 %copy.144 = f32[256,1024]{0,1:T(8,128)} copy(f32[256,1024]{1,0:T(8,128)} %get-tuple-element.41) | data formatting | bytes 2097152 | tf_op jit(solution)/shard_map/convert_element_type | solution.py:138
  106.1 1.1 pad_maximum_fusion.8
  107.3 1.2 pad_maximum_fusion.2
  108.5 4.5 %fusion.10 = f32[64,128,255]{2,1,0:T(8,128)} fusion(bf16[255,64,16]{0,2,1:T(8,128)(2,1)S(1)} %bitcast.85, bf16[255,64,16]{0,2,1:T(8,128)(2,1)S(1)} %bitcast.83, bf16[255,64,16]{0,2,1:T(8,128)(2,1)S(1)} %bitcast.79, bf16[255,64,16]{0,2,1:T(8,128)(2,1)S(1)} %bitcast.87), kind=kOutput, calls=%fused_computation.51 | convolution fusion | flops 136830976 | bytes 10444800 | tf_op jit(solution)/shard_map/tgn,sgn->gts/dot_general | solution.py:70
  113.0 3.6 %reverse = bf16[256,64,32]{0,2,1:T(8,128)(2,1)} reverse(bf16[256,64,32]{0,2,1:T(8,128)(2,1)} %bitcast.88), dimensions={0} | reverse | bytes 2097152
  116.7 5.0 %convolution_bitcast_fusion = f32[128,64,32]{0,2,1:T(8,128)} fusion(bf16[64,128,255]{2,1,0:T(8,128)(2,1)} %reshape.172, bf16[256,64,32]{0,2,1:T(8,128)(2,1)} %reverse), kind=kOutput, calls=%fused_computation.31 | convolution fusion | flops 133693440 | bytes 6275072 | tf_op jit(solution)/shard_map/gts,sgn->tgn/dot_general | solution.py:65
  121.7 2.3 %rev.18 = f32[128,64,32]{0,2,1:T(8,128)} reverse(f32[128,64,32]{0,2,1:T(8,128)} %convolution_bitcast_fusion), dimensions={0} | reverse | bytes 2097152 | tf_op jit(solution)/shard_map/jit(_flip)/rev | solution.py:64
  124.0 2.8 %copy.169 = f32[128,64,2,16]{0,2,3,1:T(2,128)} copy(f32[128,64,2,16]{0,3,2,1:T(8,128)} %bitcast.90) | data formatting | bytes 2097152 | tf_op jit(solution)/shard_map/reshape | solution.py:76
  126.8 3.1 %reshape.176 = f32[1,256,1024]{1,2,0:T(8,128)} reshape(f32[2,128,64,16]{1,0,3,2:T(2,128)} %bitcast.91) | data formatting | bytes 2097152 | tf_op jit(solution)/shard_map/reshape | solution.py:77
  129.8 1.9 multiply_convert_fusion.1
  131.8 1.3 pad_maximum_fusion.1
  134.0 4.1 %fusion.4 = (f32[3,1024]{1,0:T(4,128)S(1)}, f32[3,1024]{1,0:T(4,128)S(1)}, f32[3,1024]{1,0:T(4,128)S(1)}, f32[3,1024]{1,0:T(4,128)S(1)}, f32[3,1024]{1,0:T(4,128...) fusion(f32[256,1024]{0,1:T(8,128)S(1)} %copy-done.14, ...), kind=kLoop, calls=%fused_computation.13 | loop fusion | flops 14658560 | bytes 10059776 | tf_op jit(solution)/shard_map/reduce_sum | solution.py:136
  139.0 9.3 %reshape.178 = f32[64,32640]{1,0:T(8,128)} reshape(f32[64,128,255]{2,1,0:T(8,128)} %fusion.10) | data formatting | bytes 16711680 | tf_op jit(solution)/shard_map/reshape | solution.py:33
  148.2 4.0 %pad.6 = f32[64,32768]{1,0:T(8,128)S(1)} pad(f32[64,32640]{1,0:T(8,128)} %reshape.178, f32[]{:T(128)} %constant.3.clone.1), padding=0_0x0_128 | pad | bytes 16744452 | tf_op jit(solution)/shard_map/jit(_pad)/pad | solution.py:32
  152.3 2.5 %copy.159 = f32[8,8,128,256]{3,2,1,0:T(8,128)S(1)} copy(f32[8,8,128,256]{3,1,2,0:T(8,128)S(1)} %bitcast.73) | data formatting | bytes 16777216
  155.4 2.1 %slice.299 = bf16[3,6,1024]{1,2,0:T(8,128)(2,1)} slice(bf16[3,256,1024]{1,2,0:T(8,128)(2,1)} %pad_maximum_fusion.1), slice={[0:3], [0:6], [0:1024]} | slice | bytes 73728 | tf_op jit(solution)/shard_map/slice | solution.py:124
  157.4 1.4 copy.137
  158.9 1.3 collective-permute-start.3
  160.9 18.0 %all-to-all-start = ((f32[32,149,2]{1,2,0:T(2,128)}), f32[32,149,2]{1,2,0:T(2,128)S(1)}, u32[]{:S(2)}, u32[]{:S(2)}) async-start(f32[32,149,2]{1,2,0:T(2,128)} %bitcast.22), calls=%async_computation | async-start | bytes 131072 | tf_op jit(solution)/shard_map/all_to_all | solution.py:18
  178.9 1.2 copy.138
  180.1 1.4 pad_maximum_fusion
  181.5 6.1 %multiply_reduce_fusion.5 = (f32[256,1024]{0,1:T(8,128)S(1)}, f32[256,1024]{0,1:T(8,128)S(1)}, f32[256,1024]{0,1:T(8,128)S(1)}, f32[256,1024]{0,1:T(8,128)S(1)},...) fusion(bf16[3,262,1024]{1,2,0:T(8,128)(2,1)S(1)} %pad_maximum_fusion, f32[3,1024]{1,0:T(4,128)S(1)} %get-tuple-element.70, ...), kind=kLoop, calls=%fused_computation.22 | loop fusion | flops 12582912 | bytes 15802368 | tf_op jit(solution)/shard_map/reduce_sum | solution.py:129
  188.1 4.0 %collective-permute-start.4 = (bf16[1,256,1024]{1,2,0:T(8,128)(2,1)S(1)}, bf16[1,256,1024]{1,2,0:T(8,128)(2,1)S(1)}, u32[]{:S(2)}, u32[]{:S(2)}) collective-permute-start(bf16[1,256,1024]{1,2,0:T(8,128)(2,1)S(1)} %fusion.12), channel_id=1, source_target_pairs={{128,0},{256,128},{384,256},{129,1},{257,129},{385,257},{130,2},{2... | collective-permute-start | bytes 1572872 | tf_op jit(solution)/shard_map/ppermute | solution.py:10
  193.3 7.9 %collective-permute-done.4 = bf16[1,256,1024]{1,2,0:T(8,128)(2,1)S(1)} collective-permute-done((bf16[1,256,1024]{1,2,0:T(8,128)(2,1)S(1)}, bf16[1,256,1024]{1,2,0:T(8,128)(2,1)S(1)}, u32[]{:S(2)}, u32[]{:S(2)}) %collective-permute-start.4) | collective-permute-done | bytes 524320 | tf_op jit(solution)/shard_map/ppermute | solution.py:10
  201.3 1.0 copy.147
  (85 shorter events, 7.5 us)
Async XLA Ops:
  0.6 9.3 %copy-start.22 = (bf16[1,128,64]{1,2,0:T(8,128)(2,1)S(1)}, bf16[1,128,64]{1,2,0:T(8,128)(2,1)}, u32[]{:S(2)}) copy-start(bf16[1,128,64]{1,2,0:T(8,128)(2,1)} %param.7) | copy-start | bytes 49156
  1.4 30.7 %collective-permute-start.1 = (bf16[6,1024]{1,0:T(8,128)(2,1)S(1)}, bf16[6,1024]{1,0:T(8,128)(2,1)S(1)}, u32[]{:S(2)}, u32[]{:S(2)}) collective-permute-start(bf16[6,1024]{1,0:T(8,128)(2,1)S(1)} %get-tuple-element.57), channel_id=1, source_target_pairs={{0,4},{4,8},{8,12},{12,16},{16,20},{20,24},{24,28},{28,32},{32,36}... | collective-permute-start | bytes 36872 | tf_op jit(solution)/shard_map/ppermute | solution.py:10
  8.7 41.8 %copy-start.3 = (f32[256,1024]{0,1:T(8,128)}, f32[256,1024]{0,1:T(8,128)S(1)}, u32[]{:S(2)}) copy-start(f32[256,1024]{0,1:T(8,128)S(1)} %copy.121) | copy-start | bytes 3145732
  15.1 15.9 %copy-start.21 = (bf16[1,256,1024]{2,1,0:T(8,128)(2,1)S(1)}, bf16[1,256,1024]{2,1,0:T(8,128)(2,1)}, u32[]{:S(2)}) copy-start(bf16[1,256,1024]{2,1,0:T(8,128)(2,1)} %param.5) | copy-start | bytes 1572868
  15.1 16.9 %copy-start.7 = (bf16[1,256,1024]{2,1,0:T(8,128)(2,1)S(1)}, bf16[1,256,1024]{2,1,0:T(8,128)(2,1)}, u32[]{:S(2)}) copy-start(bf16[1,256,1024]{2,1,0:T(8,128)(2,1)} %param.4) | copy-start | bytes 1572868
  57.5 13.6 %copy-start.20 = (f32[6,1024]{0,1:T(8,128)S(1)}, f32[6,1024]{0,1:T(8,128)}, u32[]{:S(2)}) copy-start(f32[6,1024]{0,1:T(8,128)} %copy.128) | copy-start | bytes 73732
  57.7 5.1 %copy-start.18 = (bf16[1,256,1024]{1,2,0:T(8,128)(2,1)}, bf16[1,256,1024]{1,2,0:T(8,128)(2,1)S(1)}, u32[]{:S(2)}) copy-start(bf16[1,256,1024]{1,2,0:T(8,128)(2,1)S(1)} %multiply_convert_fusion.2) | copy-start | bytes 1572868
  57.8 21.3 %collective-permute-start = (bf16[127,1024]{0,1:T(8,128)(2,1)S(1)}, bf16[127,1024]{0,1:T(8,128)(2,1)}, u32[]{:S(2)}, u32[]{:S(2)}) collective-permute-start(bf16[127,1024]{0,1:T(8,128)(2,1)S(1)} %slice_bitcast_fusion.2), channel_id=1, source_target_pairs={{0,4},{4,8},{8,12},{12,16},{16,20},{20,24},{24,28},{28,32},{32,36}... | collective-permute-start | bytes 780296 | tf_op jit(solution)/shard_map/ppermute | solution.py:10
  71.1 7.8 %copy-start.19 = (bf16[1,256,1024]{1,2,0:T(8,128)(2,1)S(1)}, bf16[1,256,1024]{1,2,0:T(8,128)(2,1)}, u32[]{:S(2)}) copy-start(bf16[1,256,1024]{1,2,0:T(8,128)(2,1)} %copy-done.18) | copy-start | bytes 1572868
  77.2 0.9 copy-start.1
  78.1 2.9 %copy-start = (bf16[64,128,255]{2,1,0:T(8,128)(2,1)S(1)}, bf16[64,128,255]{2,1,0:T(8,128)(2,1)}, u32[]{:S(2)}) copy-start(bf16[64,128,255]{2,1,0:T(8,128)(2,1)} %reshape.172) | copy-start | bytes 12533764
  81.0 1.5 copy-start.8
  81.0 1.5 copy-start.10
  82.5 4.6 %copy-start.2 = (bf16[3,6,1024]{1,2,0:T(8,128)(2,1)S(1)}, bf16[3,6,1024]{1,2,0:T(8,128)(2,1)}, u32[]{:S(2)}) copy-start(bf16[3,6,1024]{1,2,0:T(8,128)(2,1)} %copy-done.1) | copy-start | bytes 110596
  89.6 16.5 %collective-permute-start.2 = (bf16[127,1024]{0,1:T(8,128)(2,1)}, bf16[127,1024]{0,1:T(8,128)(2,1)}, u32[]{:S(2)}, u32[]{:S(2)}) collective-permute-start(bf16[127,1024]{0,1:T(8,128)(2,1)} %slice_bitcast_fusion.1), channel_id=1, source_target_pairs={{4,0},{8,4},{12,8},{16,12},{20,16},{24,20},{28,24},{32,28},{36,32}... | collective-permute-start | bytes 780296 | tf_op jit(solution)/shard_map/ppermute | solution.py:10
  106.1 2.4 %copy-start.9 = (bf16[255,1024]{0,1:T(8,128)(2,1)S(1)}, bf16[255,1024]{0,1:T(8,128)(2,1)}, u32[]{:S(2)}) copy-start(bf16[255,1024]{0,1:T(8,128)(2,1)} %copy-done.8) | copy-start | bytes 1566724
  106.1 2.4 %copy-start.11 = (bf16[255,1024]{0,1:T(8,128)(2,1)S(1)}, bf16[255,1024]{0,1:T(8,128)(2,1)}, u32[]{:S(2)}) copy-start(bf16[255,1024]{0,1:T(8,128)(2,1)} %copy-done.10) | copy-start | bytes 1566724
  129.8 3.3 %copy-start.4 = (f32[256,1024]{0,1:T(8,128)S(1)}, f32[256,1024]{0,1:T(8,128)}, u32[]{:S(2)}) copy-start(f32[256,1024]{0,1:T(8,128)} %copy-done.3) | copy-start | bytes 3145732
  129.8 3.3 %copy-start.12 = (f32[256,1024]{0,1:T(8,128)S(1)}, f32[256,1024]{0,1:T(8,128)}, u32[]{:S(2)}) copy-start(f32[256,1024]{0,1:T(8,128)} %copy.139) | copy-start | bytes 3145732
  129.8 3.3 %copy-start.13 = (f32[256,1024]{0,1:T(8,128)S(1)}, f32[256,1024]{0,1:T(8,128)}, u32[]{:S(2)}) copy-start(f32[256,1024]{0,1:T(8,128)} %copy.140) | copy-start | bytes 3145732
  129.8 3.3 %copy-start.14 = (f32[256,1024]{0,1:T(8,128)S(1)}, f32[256,1024]{0,1:T(8,128)}, u32[]{:S(2)}) copy-start(f32[256,1024]{0,1:T(8,128)} %copy.141) | copy-start | bytes 3145732
  129.8 3.3 %copy-start.15 = (f32[256,1024]{0,1:T(8,128)S(1)}, f32[256,1024]{0,1:T(8,128)}, u32[]{:S(2)}) copy-start(f32[256,1024]{0,1:T(8,128)} %copy.142) | copy-start | bytes 3145732
  129.8 3.6 %copy-start.16 = (f32[256,1024]{0,1:T(8,128)S(1)}, f32[256,1024]{0,1:T(8,128)}, u32[]{:S(2)}) copy-start(f32[256,1024]{0,1:T(8,128)} %copy.143) | copy-start | bytes 3145732
  129.8 4.2 %copy-start.17 = (f32[256,1024]{0,1:T(8,128)S(1)}, f32[256,1024]{0,1:T(8,128)}, u32[]{:S(2)}) copy-start(f32[256,1024]{0,1:T(8,128)} %copy.144) | copy-start | bytes 3145732
  131.8 6.3 %copy-start.5 = (bf16[1,256,1024]{1,2,0:T(8,128)(2,1)}, bf16[1,256,1024]{1,2,0:T(8,128)(2,1)S(1)}, u32[]{:S(2)}) copy-start(bf16[1,256,1024]{1,2,0:T(8,128)(2,1)S(1)} %get-tuple-element.30) | copy-start | bytes 1572868
  154.8 25.3 %copy-start.6 = (bf16[1,256,1024]{1,2,0:T(8,128)(2,1)S(1)}, bf16[1,256,1024]{1,2,0:T(8,128)(2,1)}, u32[]{:S(2)}) copy-start(bf16[1,256,1024]{1,2,0:T(8,128)(2,1)} %copy-done.5) | copy-start | bytes 1572868
  158.9 20.0 %collective-permute-start.3 = (bf16[3,6,1024]{2,1,0:T(8,128)(2,1)S(1)}, bf16[3,6,1024]{2,1,0:T(8,128)(2,1)S(1)}, u32[]{:S(2)}, u32[]{:S(2)}) collective-permute-start(bf16[3,6,1024]{2,1,0:T(8,128)(2,1)S(1)} %copy.137), channel_id=1, source_target_pairs={{4,0},{8,4},{12,8},{16,12},{20,16},{24,20},{28,24},{32,28},{36,32}... | collective-permute-start | bytes 110600 | tf_op jit(solution)/shard_map/ppermute | solution.py:10
  160.9 31.2 %all-to-all-start = ((f32[32,149,2]{1,2,0:T(2,128)}), f32[32,149,2]{1,2,0:T(2,128)S(1)}, u32[]{:S(2)}, u32[]{:S(2)}) async-start(f32[32,149,2]{1,2,0:T(2,128)} %bitcast.22), calls=%async_computation | async-start | bytes 131072 | tf_op jit(solution)/shard_map/all_to_all | solution.py:18
  188.1 13.2 %collective-permute-start.4 = (bf16[1,256,1024]{1,2,0:T(8,128)(2,1)S(1)}, bf16[1,256,1024]{1,2,0:T(8,128)(2,1)S(1)}, u32[]{:S(2)}, u32[]{:S(2)}) collective-permute-start(bf16[1,256,1024]{1,2,0:T(8,128)(2,1)S(1)} %fusion.12), channel_id=1, source_target_pairs={{128,0},{256,128},{384,256},{129,1},{257,129},{385,257},{130,2},{2... | collective-permute-start | bytes 1572872 | tf_op jit(solution)/shard_map/ppermute | solution.py:10

commit v2 on v1

--- a/solution.py
+++ b/solution.py
@@ -124,23 +124,24 @@
     feature_rim = passed_along(feature_grads[:, :short_rim], "ctx", -1)
     grads_pad = jnp.concatenate([feature_grads, feature_rim], 1)
     running = jnp.zeros((seq_rows, chan_count), jnp.float32)
-    short_rows = []
     for offset in range(lag_count):
         running = running + jnp.sum(
             chan_short[:, offset, None, :]
             * grads_pad[:, offset : offset + seq_rows].astype(jnp.float32),
             axis=0,
         )
-        lag_start = short_rim - offset
-        short_rows.append(
-            jnp.sum(
-                feature_grads.astype(jnp.float32)
-                * signal_pad[None, lag_start : lag_start + seq_rows].astype(jnp.float32),
-                axis=1,
-            )
-        )
     input_grad = running.astype(jnp.bfloat16)
-    short_grad = jnp.stack(short_rows, 1).reshape(3 * lag_count, group_count, group_width).sum(-1)
+    lag_windows = jnp.stack(
+        [signal_pad[short_rim - offset : short_rim - offset + seq_rows] for offset in range(lag_count)],
+        1,
+    ).reshape(seq_rows, lag_count, group_count, group_width)
+    grad_groups = feature_grads.reshape(3, seq_rows, group_count, group_width)
+    cross_short = jnp.einsum(
+        "ftgc,tigd->gficd", grad_groups, lag_windows, preferred_element_type=jnp.float32
+    )
+    same_chan = jnp.eye(group_width, dtype=jnp.float32)
+    short_grad = jnp.sum(cross_short * same_chan, axis=(3, 4)).transpose(1, 2, 0)
+    short_grad = short_grad.reshape(3 * lag_count, group_count)
     short_count = short_grad.shape[0]
     both_part = owned_sum(jnp.concatenate([short_grad, taps_grad], 0), "ctx")
     short_part = both_part[None, :short_count]

time: 204 us -> 209 us (1.025)
  matrix products: 11 us -> 17.2 us
  other arithmetic: 42.4 us -> 37.6 us
  local copies, waits for them, and re-layouts: 107 us -> 110 us
    convert_element_type x6 -> x0, local copies, waits for them, and re-layouts: 15.2 us -> none  [per_device(): signal_pad[None, lag_start:lag_start + seq_rows].astype(jnp.float32)]
    slice x0 -> x6, local copies, waits for them, and re-layouts: none -> 9.66 us  [per_device(): signal_pad[short_rim - offset:short_rim - offset + seq_rows]]
    unnamed x55 -> x48, local copies, waits for them, and re-layouts: 12.6 us -> 21.2 us
    convert_element_type x1, other arithmetic: 4.34 us -> 0.01 us  [per_device(): same_chan = jnp.eye(group_width, dtype=jnp.float32)]
    reduce_sum x2 -> x0, other arithmetic: 4.32 us -> none  [the longest x1 4.07 us: per_device(): jnp.sum(feature_grads.astype(jnp.float32) * signal_pad[None, lag_start:la...]
    dot_general x0 -> x1, matrix products: none -> 3.57 us  [per_device(): jnp.einsum('ftgc,tigd->gficd', grad_groups, lag_windows, preferred_elemen...]
    concatenate x1, other arithmetic: 0.08 us -> 3.42 us  [per_device(): signal_pad = jnp.concatenate([signal_rim, signal], 0)]
    dot_general x1, matrix products: 1.47 us -> 4.03 us  [medium_terms(): jnp.einsum('gts,sgn->tgn', toeplitz, kv_win, preferred_element_type=jnp.f...]
  transfers between devices with their start and end apart: 6 -> 6, of which waited for: 1 -> 1; matrix products, arithmetic and copies ran while one was open for 34% -> 35% of each run, Pallas kernels for 0% -> 0%
where the time goes in v2:
time: 209 us; the launch traced here: 207 us
  local copies, waits for them, and re-layouts  110 us (53%)
  other arithmetic  37.6 us (18%)
  starting transfers between devices  33.1 us (16%)
  matrix products  17.2 us (8%)
  waiting for transfers between devices  7.94 us (4%)
    convert_element_type x13, local copies, waits for them, and re-layouts, short_features(): running = running + chan_short[:, offset, None, :] * padded[None, first_r...  21.3 us
    unnamed x48, local copies, waits for them, and re-layouts  21.2 us
    all_to_all x1, starting transfers between devices, owned_sum(): return jnp.sum(lax.all_to_all(chunks, axis, 0, 0, tiled=False), axis=0)  18 us
    reshape x1, local copies, waits for them, and re-layouts, band_matrix(): return tiled_rows.reshape(group_count, out_rows, span_len)  15.9 us
    ppermute x5, starting transfers between devices, passed_along(): return lax.ppermute(block, axis, route)  15.2 us
    convert_element_type x2, other arithmetic, short_features(): return running.astype(jnp.bfloat16)  13.3 us
    slice x6, local copies, waits for them, and re-layouts, per_device(): signal_pad[short_rim - offset:short_rim - offset + seq_rows]  9.66 us
    reshape x1, local copies, waits for them, and re-layouts, diagonal_sums(): cross_terms.reshape(group_count, out_rows * span_len)  9.24 us
  transfers between devices with their start and end apart: 6, of which 1 were waited for; matrix products, arithmetic and copies ran while one was open for 35% of the time, Pallas kernels for 0%

profile of v2, /device:TPU:1, one launch (start us, length us, event | category | flops | bytes accessed | tf_op | source)
XLA Modules:
  0.0 207.3 jit_solution(7692984271892895069)
XLA Ops:
  1.4 4.4 %collective-permute-start.1 = (bf16[6,1024]{1,0:T(8,128)(2,1)S(1)}, bf16[6,1024]{1,0:T(8,128)(2,1)S(1)}, u32[]{:S(2)}, u32[]{:S(2)}) collective-permute-start(bf16[6,1024]{1,0:T(8,128)(2,1)S(1)} %get-tuple-element.42), channel_id=1, source_target_pairs={{0,4},{4,8},{8,12},{12,16},{16,20},{20,24},{24,28},{28,32},{32,36}... | collective-permute-start | bytes 36872 | tf_op jit(solution)/shard_map/ppermute | solution.py:10
  5.8 1.1 bitcast_convert_fusion.1
  6.9 1.2 copy.124
  10.8 1.1 copy.113
  12.3 2.6 %copy.146 = bf16[8,8,128,256]{3,1,2,0:T(8,128)(2,1)S(1)} copy(bf16[8,8,128,256]{3,2,1,0:T(8,128)(2,1)S(1)} %bitcast.103) | data formatting | bytes 8388608
  14.9 2.2 %slice.291 = bf16[64,32640]{1,0:T(8,128)(2,1)} slice(bf16[64,32768]{1,0:T(8,128)(2,1)S(1)} %bitcast.104), slice={[0:64], [0:32640]} | slice | bytes 8355840 | tf_op jit(solution)/shard_map/slice | solution.py:26
  17.1 15.9 %reshape.186 = bf16[64,128,255]{2,1,0:T(8,128)(2,1)} reshape(bf16[64,32640]{1,0:T(8,128)(2,1)} %slice.291) | data formatting | bytes 8355840 | tf_op jit(solution)/shard_map/reshape | solution.py:27
  33.0 1.0 copy.105
  34.1 3.4 %pad_maximum_fusion.6 = (bf16[256,1024]{1,0:T(8,128)(2,1)}, bf16[256,1024]{1,0:T(8,128)(2,1)}, bf16[256,1024]{1,0:T(8,128)(2,1)}, bf16[256,1024]{1,0:T(8,128)(2,...) fusion(bf16[256,1024]{1,0:T(8,128)(2,1)S(1)} %bitcast.108, ...), kind=kLoop, calls=%fused_computation.55 | loop fusion | flops 7864320 | bytes 9973760 | tf_op jit(solution)/shard_map/concatenate | solution.py:105
  37.5 2.6 %copy.107 = f32[256,1024]{0,1:T(8,128)} copy(f32[256,1024]{1,0:T(8,128)} %get-tuple-element.37) | data formatting | bytes 2097152 | tf_op jit(solution)/shard_map/convert_element_type | solution.py:46
  40.1 2.5 %copy.108 = f32[256,1024]{0,1:T(8,128)} copy(f32[256,1024]{1,0:T(8,128)} %get-tuple-element.38) | data formatting | bytes 2097152 | tf_op jit(solution)/shard_map/convert_element_type | solution.py:46
  42.6 2.5 %copy.109 = f32[256,1024]{0,1:T(8,128)} copy(f32[256,1024]{1,0:T(8,128)} %get-tuple-element.33) | data formatting | bytes 2097152 | tf_op jit(solution)/shard_map/convert_element_type | solution.py:46
  45.1 2.6 %copy.110 = f32[256,1024]{0,1:T(8,128)} copy(f32[256,1024]{1,0:T(8,128)} %get-tuple-element.34) | data formatting | bytes 2097152 | tf_op jit(solution)/shard_map/convert_element_type | solution.py:46
  47.7 2.6 %copy.111 = f32[256,1024]{0,1:T(8,128)} copy(f32[256,1024]{1,0:T(8,128)} %get-tuple-element.35) | data formatting | bytes 2097152 | tf_op jit(solution)/shard_map/convert_element_type | solution.py:46
  50.3 1.3 copy.112
  51.6 7.0 %add_convert_fusion = bf16[3,256,1024]{1,2,0:T(8,128)(2,1)S(1)} fusion(f32[256,1024]{0,1:T(8,128)} %copy.112, f32[3,1024]{1,0:T(4,128)S(1)} %get-tuple-element.50, f32[256,1024]{0,1:T(8,128)} %copy.111, f32[3,1024]{1,0:T(4,128)S(1)} %get-tuple-element.51, f32[256,1024]{0,1:T(8,128)} %copy.110, f32[3,1024]{1,0:T(4,128)S(1)} %get-tuple-element.52, ...), kind=kLoop, calls=%fused_computation.11 | loop fusion | flops 11010048 | bytes 8998912 | tf_op jit(solution)/shard_map/convert_element_type | solution.py:47
  58.8 0.9 slice_bitcast_fusion.2
  59.7 4.2 %collective-permute-start = (bf16[127,1024]{0,1:T(8,128)(2,1)}, bf16[127,1024]{0,1:T(8,128)(2,1)}, u32[]{:S(2)}, u32[]{:S(2)}) collective-permute-start(bf16[127,1024]{0,1:T(8,128)(2,1)} %slice_bitcast_fusion.2), channel_id=1, source_target_pairs={{0,4},{4,8},{8,12},{12,16},{16,20},{20,24},{24,28},{28,32},{32,36}... | collective-permute-start | bytes 780296 | tf_op jit(solution)/shard_map/ppermute | solution.py:10
  64.0 1.0 copy.114
  65.0 1.0 copy.115
  66.0 1.0 copy.116
  67.0 1.0 copy.117
  68.1 1.0 copy.118
  69.1 1.0 copy.119
  70.1 6.3 %add_convert_fusion.1 = bf16[3,6,1024]{1,2,0:T(8,128)(2,1)S(1)} fusion(f32[6,1024]{0,1:T(8,128)} %copy.119, f32[3,1024]{1,0:T(4,128)S(1)} %get-tuple-element.50, f32[6,1024]{0,1:T(8,128)} %copy.118, f32[3,1024]{1,0:T(4,128)S(1)} %get-tuple-element.51, f32[6,1024]{0,1:T(8,128)} %copy.117, f32[3,1024]{1,0:T(4,128)S(1)} %get-tuple-element.52, ...), kind=kLoop, calls=%fused_computation.21 | loop fusion | flops 258048 | bytes 294912 | tf_op jit(solution)/shard_map/convert_element_type | solution.py:47
  77.4 1.2 copy.125
  78.6 2.1 %copy.126 = bf16[256,1024]{0,1:T(8,128)(2,1)} copy(bf16[256,1024]{1,0:T(8,128)(2,1)} %get-tuple-element.24) | data formatting | bytes 1048576 | tf_op jit(solution)/shard_map/slice | solution.py:135
  81.8 1.9 constant_dynamic-update-slice_fusion.4
  85.2 2.0 copy.128
  87.3 1.3 slice_bitcast_fusion
  88.6 1.6 pad_maximum_fusion.10
  90.1 4.0 %fusion.9 = f32[64,32,128]{2,1,0:T(8,128)S(1)} fusion(bf16[64,128,255]{2,1,0:T(8,128)(2,1)} %reshape.186, bf16[255,64,16]{0,2,1:T(8,128)(2,1)S(1)} %bitcast.115, bf16[255,64,16]{0,2,1:T(8,128)(2,1)S(1)} %bitcast.113), kind=kOutput, calls=%fused_computation.45 | convolution fusion | flops 135782400 | bytes 6270976 | tf_op jit(solution)/shard_map/gts,sgn->tgn/dot_general | solution.py:63
  94.2 1.6 copy.158
  95.8 3.0 %reshape.188 = f32[1,256,1024]{1,2,0:T(8,128)} reshape(f32[2,128,64,16]{1,0,3,2:T(2,128)} %bitcast.120) | data formatting | bytes 2097152 | tf_op jit(solution)/shard_map/reshape | solution.py:77
  98.8 1.8 fusion.6
  101.4 1.3 collective-permute-start.2
  103.5 2.0 copy.129
  105.6 2.0 copy.130
  107.6 2.0 constant_dynamic-update-slice_fusion.1
  109.6 1.9 constant_dynamic-update-slice_fusion
  111.6 1.0 pad_maximum_fusion.8
  112.6 1.2 pad_maximum_fusion.2
  113.8 4.5 %fusion.8 = f32[64,128,255]{2,1,0:T(8,128)} fusion(bf16[255,64,16]{0,2,1:T(8,128)(2,1)S(1)} %bitcast.116, bf16[255,64,16]{0,2,1:T(8,128)(2,1)S(1)} %bitcast.114, bf16[255,64,16]{0,2,1:T(8,128)(2,1)S(1)} %bitcast.107, bf16[255,64,16]{0,2,1:T(8,128)(2,1)S(1)} %bitcast.118), kind=kOutput, calls=%fused_computation.44 | convolution fusion | flops 136830976 | bytes 10444800 | tf_op jit(solution)/shard_map/tgn,sgn->gts/dot_general | solution.py:70
  118.3 3.7 %reverse = bf16[256,64,32]{0,2,1:T(8,128)(2,1)} reverse(bf16[256,64,32]{0,2,1:T(8,128)(2,1)} %bitcast.119), dimensions={0} | reverse | bytes 2097152
  122.0 5.0 %convolution_bitcast_fusion = f32[128,64,32]{0,2,1:T(8,128)} fusion(bf16[64,128,255]{2,1,0:T(8,128)(2,1)} %reshape.186, bf16[256,64,32]{0,2,1:T(8,128)(2,1)} %reverse), kind=kOutput, calls=%fused_computation.24 | convolution fusion | flops 133693440 | bytes 6275072 | tf_op jit(solution)/shard_map/gts,sgn->tgn/dot_general | solution.py:65
  127.0 2.3 %rev.18 = f32[128,64,32]{0,2,1:T(8,128)} reverse(f32[128,64,32]{0,2,1:T(8,128)} %convolution_bitcast_fusion), dimensions={0} | reverse | bytes 2097152 | tf_op jit(solution)/shard_map/jit(_flip)/rev | solution.py:64
  129.3 2.7 %copy.157 = f32[128,64,2,16]{0,2,3,1:T(2,128)} copy(f32[128,64,2,16]{0,3,2,1:T(8,128)} %bitcast.121) | data formatting | bytes 2097152 | tf_op jit(solution)/shard_map/reshape | solution.py:76
  132.0 3.1 %reshape.190 = f32[1,256,1024]{1,2,0:T(8,128)} reshape(f32[2,128,64,16]{1,0,3,2:T(2,128)} %bitcast.122) | data formatting | bytes 2097152 | tf_op jit(solution)/shard_map/reshape | solution.py:77
  135.1 1.8 multiply_convert_fusion.1
  137.6 1.3 pad_maximum_fusion.1
  139.7 3.6 %fusion = f32[64,3,7]{1,2,0:T(8,128)S(1)} fusion(f32[16,16]{0,1:T(8,128)S(1)} %fusion.21, bf16[256,7,64,16]{0,3,1,2:T(8,128)(2,1)S(1)} %copy-done.14, bf16[1,256,64,16]{1,3,0,2:T(8,128)(2,1)S(1)} %bitcast.112, bf16[1,256,64,16]{1,3,0,2:T(8,128)(2,1)S(1)} %bitcast.111, bf16[1,256,64,16]{1,3,0,2:T(8,128)(2,1)S(1)} %bitcast.110), kind=kOutput, calls=%fused_computation.1 | convolution fusion | flops 181566144 | bytes 5249280 | tf_op jit(solution)/shard_map/ftgc,tigd->gficd/dot_general | solution.py:139
  143.9 9.2 %reshape.191 = f32[64,32640]{1,0:T(8,128)} reshape(f32[64,128,255]{2,1,0:T(8,128)} %fusion.8) | data formatting | bytes 16711680 | tf_op jit(solution)/shard_map/reshape | solution.py:33
  153.2 4.0 %pad.6 = f32[64,32768]{1,0:T(8,128)S(1)} pad(f32[64,32640]{1,0:T(8,128)} %reshape.191, f32[]{:T(128)} %constant.3.clone.1), padding=0_0x0_128 | pad | bytes 16744452 | tf_op jit(solution)/shard_map/jit(_pad)/pad | solution.py:32
  157.2 2.5 %copy.147 = f32[8,8,128,256]{3,2,1,0:T(8,128)S(1)} copy(f32[8,8,128,256]{3,1,2,0:T(8,128)S(1)} %bitcast.101) | data formatting | bytes 16777216
  160.3 2.1 %slice.299 = bf16[3,6,1024]{1,2,0:T(8,128)(2,1)} slice(bf16[3,256,1024]{1,2,0:T(8,128)(2,1)} %pad_maximum_fusion.1), slice={[0:3], [0:6], [0:1024]} | slice | bytes 73728 | tf_op jit(solution)/shard_map/slice | solution.py:124
  162.4 1.4 copy.122
  163.8 1.3 collective-permute-start.3
  165.9 18.0 %all-to-all-start = ((f32[32,149,2]{1,2,0:T(2,128)}), f32[32,149,2]{1,2,0:T(2,128)S(1)}, u32[]{:S(2)}, u32[]{:S(2)}) async-start(f32[32,149,2]{1,2,0:T(2,128)} %maximum_bitcast_fusion.2), calls=%async_computation | async-start | bytes 131072 | tf_op jit(solution)/shard_map/all_to_all | solution.py:18
  183.9 1.2 copy.123
  185.1 1.4 pad_maximum_fusion
  186.5 6.1 %multiply_reduce_fusion.5 = (f32[256,1024]{0,1:T(8,128)S(1)}, f32[256,1024]{0,1:T(8,128)S(1)}, f32[256,1024]{0,1:T(8,128)S(1)}, f32[256,1024]{0,1:T(8,128)S(1)},...) fusion(bf16[3,262,1024]{1,2,0:T(8,128)(2,1)S(1)} %pad_maximum_fusion, f32[3,1024]{1,0:T(4,128)S(1)} %get-tuple-element.55, ...), kind=kLoop, calls=%fused_computation.9 | loop fusion | flops 12582912 | bytes 15802368 | tf_op jit(solution)/shard_map/reduce_sum | solution.py:128
  193.1 4.0 %collective-permute-start.4 = (bf16[1,256,1024]{1,2,0:T(8,128)(2,1)S(1)}, bf16[1,256,1024]{1,2,0:T(8,128)(2,1)S(1)}, u32[]{:S(2)}, u32[]{:S(2)}) collective-permute-start(bf16[1,256,1024]{1,2,0:T(8,128)(2,1)S(1)} %fusion.10), channel_id=1, source_target_pairs={{128,0},{256,128},{384,256},{129,1},{257,129},{385,257},{130,2},{2... | collective-permute-start | bytes 1572872 | tf_op jit(solution)/shard_map/ppermute | solution.py:10
  198.4 7.9 %collective-permute-done.4 = bf16[1,256,1024]{1,2,0:T(8,128)(2,1)S(1)} collective-permute-done((bf16[1,256,1024]{1,2,0:T(8,128)(2,1)S(1)}, bf16[1,256,1024]{1,2,0:T(8,128)(2,1)S(1)}, u32[]{:S(2)}, u32[]{:S(2)}) %collective-permute-start.4) | collective-permute-done | bytes 524320 | tf_op jit(solution)/shard_map/ppermute | solution.py:10
  206.3 1.0 copy.133
  (71 shorter events, 14.3 us)
Async XLA Ops:
  1.4 32.7 %collective-permute-start.1 = (bf16[6,1024]{1,0:T(8,128)(2,1)S(1)}, bf16[6,1024]{1,0:T(8,128)(2,1)S(1)}, u32[]{:S(2)}, u32[]{:S(2)}) collective-permute-start(bf16[6,1024]{1,0:T(8,128)(2,1)S(1)} %get-tuple-element.42), channel_id=1, source_target_pairs={{0,4},{4,8},{8,12},{12,16},{16,20},{20,24},{24,28},{28,32},{32,36}... | collective-permute-start | bytes 36872 | tf_op jit(solution)/shard_map/ppermute | solution.py:10
  6.9 5.0 %copy-start.15 = (bf16[1,128,64]{1,2,0:T(8,128)(2,1)S(1)}, bf16[1,128,64]{1,2,0:T(8,128)(2,1)}, u32[]{:S(2)}) copy-start(bf16[1,128,64]{1,2,0:T(8,128)(2,1)} %param.7) | copy-start | bytes 49156
  17.1 15.9 %copy-start.13 = (bf16[1,256,1024]{2,1,0:T(8,128)(2,1)S(1)}, bf16[1,256,1024]{2,1,0:T(8,128)(2,1)}, u32[]{:S(2)}) copy-start(bf16[1,256,1024]{2,1,0:T(8,128)(2,1)} %param.5) | copy-start | bytes 1572868
  17.1 16.9 %copy-start.2 = (bf16[1,256,1024]{2,1,0:T(8,128)(2,1)S(1)}, bf16[1,256,1024]{2,1,0:T(8,128)(2,1)}, u32[]{:S(2)}) copy-start(bf16[1,256,1024]{2,1,0:T(8,128)(2,1)} %param.4) | copy-start | bytes 1572868
  58.6 11.5 %copy-start.10 = (f32[6,1024]{0,1:T(8,128)S(1)}, f32[6,1024]{0,1:T(8,128)}, u32[]{:S(2)}) copy-start(f32[6,1024]{0,1:T(8,128)} %copy.113) | copy-start | bytes 73732
  58.8 17.6 %copy-start.9 = (bf16[1,256,1024]{1,2,0:T(8,128)(2,1)}, bf16[1,256,1024]{1,2,0:T(8,128)(2,1)S(1)}, u32[]{:S(2)}) copy-start(bf16[1,256,1024]{1,2,0:T(8,128)(2,1)S(1)} %multiply_convert_fusion.2) | copy-start | bytes 1572868
  59.7 28.9 %collective-permute-start = (bf16[127,1024]{0,1:T(8,128)(2,1)}, bf16[127,1024]{0,1:T(8,128)(2,1)}, u32[]{:S(2)}, u32[]{:S(2)}) collective-permute-start(bf16[127,1024]{0,1:T(8,128)(2,1)} %slice_bitcast_fusion.2), channel_id=1, source_target_pairs={{0,4},{4,8},{8,12},{12,16},{16,20},{20,24},{24,28},{28,32},{32,36}... | collective-permute-start | bytes 780296 | tf_op jit(solution)/shard_map/ppermute | solution.py:10
  70.1 10.6 %copy-start.11 = (bf16[256,1024]{1,0:T(8,128)(2,1)S(1)}, bf16[256,1024]{1,0:T(8,128)(2,1)}, u32[]{:S(2)}) copy-start(bf16[256,1024]{1,0:T(8,128)(2,1)} %get-tuple-element.25) | copy-start | bytes 1572868
  76.4 0.9 copy-start
  90.1 4.1 %copy-start.5 = (bf16[255,1024]{0,1:T(8,128)(2,1)}, bf16[255,1024]{0,1:T(8,128)(2,1)S(1)}, u32[]{:S(2)}) copy-start(bf16[255,1024]{0,1:T(8,128)(2,1)S(1)} %get-tuple-element.20) | copy-start | bytes 1566724
  90.1 4.1 %copy-start.7 = (bf16[255,1024]{0,1:T(8,128)(2,1)}, bf16[255,1024]{0,1:T(8,128)(2,1)S(1)}, u32[]{:S(2)}) copy-start(bf16[255,1024]{0,1:T(8,128)(2,1)S(1)} %get-tuple-element.21) | copy-start | bytes 1566724
  94.2 4.6 %copy-start.1 = (bf16[3,6,1024]{1,2,0:T(8,128)(2,1)S(1)}, bf16[3,6,1024]{1,2,0:T(8,128)(2,1)}, u32[]{:S(2)}) copy-start(bf16[3,6,1024]{1,2,0:T(8,128)(2,1)} %copy-done) | copy-start | bytes 110596
  98.8 3.9 %copy-start.12 = (bf16[256,1024]{0,1:T(8,128)(2,1)S(1)}, bf16[256,1024]{0,1:T(8,128)(2,1)}, u32[]{:S(2)}) copy-start(bf16[256,1024]{0,1:T(8,128)(2,1)} %copy.128) | copy-start | bytes 1572868
  101.4 10.2 %collective-permute-start.2 = (bf16[127,1024]{0,1:T(8,128)(2,1)}, bf16[127,1024]{0,1:T(8,128)(2,1)}, u32[]{:S(2)}, u32[]{:S(2)}) collective-permute-start(bf16[127,1024]{0,1:T(8,128)(2,1)} %slice_bitcast_fusion.1), channel_id=1, source_target_pairs={{4,0},{8,4},{12,8},{16,12},{20,16},{24,20},{28,24},{32,28},{36,32}... | collective-permute-start | bytes 780296 | tf_op jit(solution)/shard_map/ppermute | solution.py:10
  107.6 6.2 %copy-start.6 = (bf16[255,1024]{0,1:T(8,128)(2,1)S(1)}, bf16[255,1024]{0,1:T(8,128)(2,1)}, u32[]{:S(2)}) copy-start(bf16[255,1024]{0,1:T(8,128)(2,1)} %copy-done.5) | copy-start | bytes 1566724
  107.6 6.2 %copy-start.8 = (bf16[255,1024]{0,1:T(8,128)(2,1)S(1)}, bf16[255,1024]{0,1:T(8,128)(2,1)}, u32[]{:S(2)}) copy-start(bf16[255,1024]{0,1:T(8,128)(2,1)} %copy-done.7) | copy-start | bytes 1566724
  136.9 6.4 %copy-start.3 = (bf16[1,256,1024]{1,2,0:T(8,128)(2,1)}, bf16[1,256,1024]{1,2,0:T(8,128)(2,1)S(1)}, u32[]{:S(2)}) copy-start(bf16[1,256,1024]{1,2,0:T(8,128)(2,1)S(1)} %get-tuple-element.19) | copy-start | bytes 1572868
  136.9 2.8 %copy-start.14 = (bf16[256,7,64,16]{0,3,1,2:T(8,128)(2,1)S(1)}, bf16[256,7,64,16]{0,3,1,2:T(8,128)(2,1)}, u32[]{:S(2)}) copy-start(bf16[256,7,64,16]{0,3,1,2:T(8,128)(2,1)} %constant_dynamic-update-slice_fusion) | copy-start | bytes 11010052
  159.7 25.4 %copy-start.4 = (bf16[1,256,1024]{1,2,0:T(8,128)(2,1)S(1)}, bf16[1,256,1024]{1,2,0:T(8,128)(2,1)}, u32[]{:S(2)}) copy-start(bf16[1,256,1024]{1,2,0:T(8,128)(2,1)} %copy-done.3) | copy-start | bytes 1572868
  163.8 20.1 %collective-permute-start.3 = (bf16[3,6,1024]{2,1,0:T(8,128)(2,1)S(1)}, bf16[3,6,1024]{2,1,0:T(8,128)(2,1)S(1)}, u32[]{:S(2)}, u32[]{:S(2)}) collective-permute-start(bf16[3,6,1024]{2,1,0:T(8,128)(2,1)S(1)} %copy.122), channel_id=1, source_target_pairs={{4,0},{8,4},{12,8},{16,12},{20,16},{24,20},{28,24},{32,28},{36,32}... | collective-permute-start | bytes 110600 | tf_op jit(solution)/shard_map/ppermute | solution.py:10
  165.9 31.2 %all-to-all-start = ((f32[32,149,2]{1,2,0:T(2,128)}), f32[32,149,2]{1,2,0:T(2,128)S(1)}, u32[]{:S(2)}, u32[]{:S(2)}) async-start(f32[32,149,2]{1,2,0:T(2,128)} %maximum_bitcast_fusion.2), calls=%async_computation | async-start | bytes 131072 | tf_op jit(solution)/shard_map/all_to_all | solution.py:18
  193.1 13.2 %collective-permute-start.4 = (bf16[1,256,1024]{1,2,0:T(8,128)(2,1)S(1)}, bf16[1,256,1024]{1,2,0:T(8,128)(2,1)S(1)}, u32[]{:S(2)}, u32[]{:S(2)}) collective-permute-start(bf16[1,256,1024]{1,2,0:T(8,128)(2,1)S(1)} %fusion.10), channel_id=1, source_target_pairs={{128,0},{256,128},{384,256},{129,1},{257,129},{385,257},{130,2},{2... | collective-permute-start | bytes 1572872 | tf_op jit(solution)/shard_map/ppermute | solution.py:10

commit v3 on v1

--- a/solution.py
+++ b/solution.py
@@ -1,7 +1,11 @@
 import jax
 import jax.numpy as jnp
 from jax import lax
+from jax.experimental import pallas as pl
+from jax.experimental.pallas import tpu as pltpu
 from jax.sharding import PartitionSpec as P
+
+LANE_BLOCK = 128
 
 
 def passed_along(block, axis, distance):
@@ -16,6 +20,94 @@
     width = col_count // axis_len
     chunks = partial_terms.reshape(row_count, axis_len, width).transpose(1, 0, 2)
     return jnp.sum(lax.all_to_all(chunks, axis, 0, 0, tiled=False), axis=0)
+
+
+def front_kernel(taps_ref, sig_ref, gy_ref, q_ref, k_ref, v_ref, kv_ref, gate_ref, xs_ref):
+    rows = q_ref.shape[0]
+    rim = sig_ref.shape[0] - rows
+    lags = rim + 1
+    xs_ref[pl.ds(0, rows + rim), :] = sig_ref[...].astype(jnp.float32)
+    for branch, out_ref in enumerate((q_ref, k_ref, v_ref)):
+        acc = None
+        for offset in range(lags):
+            term = taps_ref[pl.ds(branch * lags + offset, 1), :] * xs_ref[pl.ds(rim - offset, rows), :]
+            acc = term if acc is None else acc + term
+        out_ref[...] = acc.astype(jnp.bfloat16)
+    kv_ref[...] = (k_ref[...].astype(jnp.float32) * v_ref[...].astype(jnp.float32)).astype(
+        jnp.bfloat16
+    )
+    gate_ref[...] = (gy_ref[...].astype(jnp.float32) * q_ref[...].astype(jnp.float32)).astype(
+        jnp.bfloat16
+    )
+
+
+def short_front(taps, signal_pad, grad_out):
+    padded_rows, chan_count = signal_pad.shape
+    rows = grad_out.shape[0]
+    tap_rows = taps.shape[0]
+    row_spec = pl.BlockSpec((rows, LANE_BLOCK), lambda j: (0, j))
+    shape = jax.ShapeDtypeStruct((rows, chan_count), jnp.bfloat16)
+    return pl.pallas_call(
+        front_kernel,
+        grid=(chan_count // LANE_BLOCK,),
+        in_specs=[
+            pl.BlockSpec((tap_rows, LANE_BLOCK), lambda j: (0, j)),
+            pl.BlockSpec((padded_rows, LANE_BLOCK), lambda j: (0, j)),
+            row_spec,
+        ],
+        out_specs=[row_spec] * 5,
+        out_shape=[shape] * 5,
+        scratch_shapes=[pltpu.VMEM((padded_rows + 8, LANE_BLOCK), jnp.float32)],
+    )(taps, signal_pad, grad_out)
+
+
+def back_kernel(taps_ref, sig_ref, grads_ref, ig_ref, sp_ref, xs_ref, gs_ref):
+    rows = ig_ref.shape[0]
+    rim = sig_ref.shape[0] - rows
+    lags = rim + 1
+    branches = grads_ref.shape[0]
+    xs_ref[pl.ds(0, rows + rim), :] = sig_ref[...].astype(jnp.float32)
+    for branch in range(branches):
+        gs_ref[branch, pl.ds(0, rows + rim), :] = grads_ref[branch].astype(jnp.float32)
+    acc = None
+    for branch in range(branches):
+        for offset in range(lags):
+            term = taps_ref[pl.ds(branch * lags + offset, 1), :] * gs_ref[branch, pl.ds(offset, rows), :]
+            acc = term if acc is None else acc + term
+    ig_ref[...] = acc.astype(jnp.bfloat16)
+    for branch in range(branches):
+        grads_f = gs_ref[branch, pl.ds(0, rows), :]
+        for offset in range(lags):
+            prod = grads_f * xs_ref[pl.ds(rim - offset, rows), :]
+            sp_ref[pl.ds(branch * lags + offset, 1), :] = jnp.sum(prod, axis=0, keepdims=True)
+
+
+def short_back(taps, signal_pad, grads_pad):
+    padded_rows, chan_count = signal_pad.shape
+    branches = grads_pad.shape[0]
+    tap_rows = taps.shape[0]
+    rows = padded_rows - (tap_rows // branches - 1)
+    return pl.pallas_call(
+        back_kernel,
+        grid=(chan_count // LANE_BLOCK,),
+        in_specs=[
+            pl.BlockSpec((tap_rows, LANE_BLOCK), lambda j: (0, j)),
+            pl.BlockSpec((padded_rows, LANE_BLOCK), lambda j: (0, j)),
+            pl.BlockSpec((branches, padded_rows, LANE_BLOCK), lambda j: (0, 0, j)),
+        ],
+        out_specs=[
+            pl.BlockSpec((rows, LANE_BLOCK), lambda j: (0, j)),
+            pl.BlockSpec((tap_rows, LANE_BLOCK), lambda j: (0, j)),
+        ],
+        out_shape=[
+            jax.ShapeDtypeStruct((rows, chan_count), jnp.bfloat16),
+            jax.ShapeDtypeStruct((tap_rows, chan_count), jnp.float32),
+        ],
+        scratch_shapes=[
+            pltpu.VMEM((padded_rows + 8, LANE_BLOCK), jnp.float32),
+            pltpu.VMEM((branches, padded_rows + 8, LANE_BLOCK), jnp.float32),
+        ],
+    )(taps, signal_pad, grads_pad)
 
 
 def band_matrix(filter_taps, out_rows):
@@ -94,27 +186,14 @@
         (3, lag_count, group_count, group_width),
     ).reshape(3, lag_count, chan_count)
     medium_taps = medium_filter[0]
-    zero_rim = jnp.zeros((short_rim, chan_count), jnp.bfloat16)
-    features_local = short_features(jnp.concatenate([zero_rim, signal], 0), chan_short, seq_rows)
-    kv_local = (
-        features_local[1].astype(jnp.float32) * features_local[2].astype(jnp.float32)
-    ).astype(jnp.bfloat16)
-    signal_rim, kv_rim = passed_along(
-        (signal[seq_rows - short_rim :], kv_local[seq_rows - medium_rim :]), "ctx", 1
-    )
+    tap_table = chan_short.reshape(3 * lag_count, chan_count)
+    signal_rim = passed_along(signal[seq_rows - short_rim :], "ctx", 1)
     signal_pad = jnp.concatenate([signal_rim, signal], 0)
-    head_features = short_features(signal_pad[: 2 * short_rim], chan_short, short_rim)
-    features = jnp.concatenate([head_features, features_local[:, short_rim:]], 1)
-    query_in = features[0]
-    key_in = features[1]
-    value_in = features[2]
-    head_products = (
-        key_in[:short_rim].astype(jnp.float32) * value_in[:short_rim].astype(jnp.float32)
-    ).astype(jnp.bfloat16)
-    products = jnp.concatenate([head_products, kv_local[short_rim:]], 0)
+    query_in, key_in, value_in, products, gate_grad = short_front(tap_table, signal_pad, grad_out)
+    kv_rim, gate_rim = passed_along(products[seq_rows - medium_rim :], "ctx", 1), passed_along(
+        gate_grad[:medium_rim], "ctx", -1
+    )
     kv_pad = jnp.concatenate([kv_rim, products], 0)
-    gate_grad = (grad_out.astype(jnp.float32) * query_in.astype(jnp.float32)).astype(jnp.bfloat16)
-    gate_rim = passed_along(gate_grad[:medium_rim], "ctx", -1)
     gate_ext = jnp.concatenate([gate_grad, gate_rim], 0)
     mixed_out, back_out, taps_grad = medium_terms(medium_taps, kv_pad, gate_ext, 128)
     query_grad = (grad_out.astype(jnp.float32) * mixed_out).astype(jnp.bfloat16)
@@ -123,24 +202,8 @@
     feature_grads = jnp.stack([query_grad, key_grad, value_grad])
     feature_rim = passed_along(feature_grads[:, :short_rim], "ctx", -1)
     grads_pad = jnp.concatenate([feature_grads, feature_rim], 1)
-    running = jnp.zeros((seq_rows, chan_count), jnp.float32)
-    short_rows = []
-    for offset in range(lag_count):
-        running = running + jnp.sum(
-            chan_short[:, offset, None, :]
-            * grads_pad[:, offset : offset + seq_rows].astype(jnp.float32),
-            axis=0,
-        )
-        lag_start = short_rim - offset
-        short_rows.append(
-            jnp.sum(
-                feature_grads.astype(jnp.float32)
-                * signal_pad[None, lag_start : lag_start + seq_rows].astype(jnp.float32),
-                axis=1,
-            )
-        )
-    input_grad = running.astype(jnp.bfloat16)
-    short_grad = jnp.stack(short_rows, 1).reshape(3 * lag_count, group_count, group_width).sum(-1)
+    input_grad, short_terms = short_back(tap_table, signal_pad, grads_pad)
+    short_grad = short_terms.reshape(3 * lag_count, group_count, group_width).sum(-1)
     short_count = short_grad.shape[0]
     both_part = owned_sum(jnp.concatenate([short_grad, taps_grad], 0), "ctx")
     short_part = both_part[None, :short_count]

time: 204 us -> 133 us (0.65)
  the two profiles are of different devices: /device:TPU:1 before, /device:TPU:16 now
where the time goes in v3:
time: 133 us; the launch traced here: 132 us
  local copies, waits for them, and re-layouts  51.7 us (39%)
  starting transfers between devices  33 us (25%)
  waiting for transfers between devices  17.5 us (13%)
  Pallas kernels  13.1 us (10%)
  matrix products  8.62 us (6%)
  other arithmetic  7.27 us (5%)
    all_to_all x1, starting transfers between devices, owned_sum(): return jnp.sum(lax.all_to_all(chunks, axis, 0, 0, tiled=False), axis=0)  20.4 us
    reshape x1, local copies, waits for them, and re-layouts, band_matrix(): return tiled_rows.reshape(group_count, out_rows, span_len)  15.9 us
    all_to_all x1, waiting for transfers between devices, owned_sum(): return jnp.sum(lax.all_to_all(chunks, axis, 0, 0, tiled=False), axis=0)  12.9 us
    ppermute x5, starting transfers between devices, passed_along(): return lax.ppermute(block, axis, route)  12.7 us
    reshape x1, local copies, waits for them, and re-layouts, diagonal_sums(): cross_terms.reshape(group_count, out_rows * span_len)  9.23 us
    unnamed x17, local copies, waits for them, and re-layouts  8.12 us
    pallas_call x1, Pallas kernels, short_back(): pl.pallas_call(back_kernel, grid=(chan_count // LANE_BLOCK,), in_specs=[p...  7.13 us
    pallas_call x1, Pallas kernels, short_front(): pl.pallas_call(front_kernel, grid=(chan_count // LANE_BLOCK,), in_specs=[...  5.99 us
  transfers between devices with their start and end apart: 6, of which 2 were waited for; matrix products, arithmetic and copies ran while one was open for 31% of the time, Pallas kernels for 0%

profile of v3, /device:TPU:16, one launch (start us, length us, event | category | flops | bytes accessed | tf_op | source)
XLA Modules:
  0.0 132.2 jit_solution(3196972355108506965)
XLA Ops:
  0.6 0.0 copy-start.5
  0.6 0.7 slice_bitcast_fusion
  1.4 3.8 %collective-permute-start = (bf16[6,1024]{1,0:T(8,128)(2,1)S(1)}, bf16[6,1024]{1,0:T(8,128)(2,1)S(1)}, u32[]{:S(2)}, u32[]{:S(2)}) collective-permute-start(bf16[6,1024]{1,0:T(8,128)(2,1)S(1)} %slice_bitcast_fusion), channel_id=1, source_target_pairs={{0,4},{4,8},{8,12},{12,16},{16,20},{20,24},{24,28},{28,32},{32,36}... | collective-permute-start | bytes 36872 | tf_op jit(solution)/shard_map/ppermute | solution.py:14
  5.2 0.7 reshape.62
  5.9 0.2 broadcast_in_dim.15
  6.1 1.0 reshape_reshape.3.taps_ref
  7.2 0.0 collective-permute-done
  7.2 2.0 %pad_maximum_fusion.5.sig_ref = bf16[262,1024]{1,0:T(8,128)(2,1)} fusion(bf16[256,1024]{1,0:T(8,128)(2,1)} %bitcast.70, bf16[6,1024]{1,0:T(8,128)(2,1)S(1)} %collective-permute-done), kind=kLoop, calls=%fused_computation.14 | loop fusion | flops 1073152 | bytes 1073152 | tf_op jit(solution)/shard_map/concatenate | solution.py:191
  9.1 6.0 %shard_map.67 = (bf16[256,1024]{1,0:T(8,128)(2,1)}, bf16[256,1024]{1,0:T(8,128)(2,1)}, bf16[256,1024]{1,0:T(8,128)(2,1)}, bf16[256,1024]{1,0:T(8,128)(2,1)}, bf16[256,1024]{1,0:T(8,128)(2,1)}) custom-call(f32[21,1024]{1,0:T(8,128)} %reshape_reshape.3.taps_ref, bf16[262,1024]{1,0:T(8,128)(2,1)} %pad_maximum_fusion.5.sig_ref, bf16[256,1024]{1,0:T(8,128)(2,1)} %bitcast.69), custom_call_target="tpu_custom_call" | custom-call | tf_op jit(solution)/shard_map/pallas_call | solution.py:50
  15.1 1.0 slice.66
  16.1 1.3 collective-permute-start.2
  17.4 0.0 copy-done.5
  17.4 0.1 rev.16
  17.5 0.3 tile.4
  17.8 2.6 %copy.58 = bf16[8,8,128,256]{3,1,2,0:T(8,128)(2,1)S(1)} copy(bf16[8,8,128,256]{3,2,1,0:T(8,128)(2,1)S(1)} %bitcast.53) | data formatting | bytes 8388608
  20.4 2.2 %slice.74 = bf16[64,32640]{1,0:T(8,128)(2,1)} slice(bf16[64,32768]{1,0:T(8,128)(2,1)S(1)} %bitcast.54), slice={[0:64], [0:32640]} | slice | bytes 8355840 | tf_op jit(solution)/shard_map/slice | solution.py:118
  22.6 15.9 %reshape.53 = bf16[64,128,255]{2,1,0:T(8,128)(2,1)} reshape(bf16[64,32640]{1,0:T(8,128)(2,1)} %slice.74) | data formatting | bytes 8355840 | tf_op jit(solution)/shard_map/reshape | solution.py:119
  38.6 0.1 slice.58
  38.6 4.7 %collective-permute-start.1 = (bf16[127,1024]{1,0:T(8,128)(2,1)S(1)}, bf16[127,1024]{1,0:T(8,128)(2,1)S(1)}, u32[]{:S(2)}, u32[]{:S(2)}) collective-permute-start(bf16[127,1024]{1,0:T(8,128)(2,1)S(1)} %slice.58), channel_id=1, source_target_pairs={{0,4},{4,8},{8,12},{12,16},{16,20},{20,24},{24,28},{28,32},{32,36}... | collective-permute-start | bytes 780296 | tf_op jit(solution)/shard_map/ppermute | solution.py:14
  43.4 0.0 collective-permute-done.2
  43.4 0.1 fusion.8
  43.5 0.2 copy.48
  43.8 4.6 %collective-permute-done.1 = bf16[127,1024]{1,0:T(8,128)(2,1)S(1)} collective-permute-done((bf16[127,1024]{1,0:T(8,128)(2,1)S(1)}, bf16[127,1024]{1,0:T(8,128)(2,1)S(1)}, u32[]{:S(2)}, u32[]{:S(2)}) %collective-permute-start.1) | collective-permute-done | bytes 260128 | tf_op jit(solution)/shard_map/ppermute | solution.py:14
  48.4 0.2 pad_maximum_fusion.7
  48.5 0.2 copy.44
  48.8 0.2 copy.45
  49.0 0.2 copy.49
  49.2 0.2 pad_maximum_fusion.1
  49.4 2.1 %reverse = bf16[256,64,32]{0,2,1:T(8,128)(2,1)} reverse(bf16[256,64,32]{0,2,1:T(8,128)(2,1)S(1)} %bitcast.67), dimensions={0} | reverse | bytes 2097152
  51.5 4.5 %fusion = f32[64,128,255]{2,1,0:T(8,128)} fusion(bf16[255,64,16]{0,2,1:T(8,128)(2,1)S(1)} %bitcast.57, bf16[255,64,16]{0,2,1:T(8,128)(2,1)S(1)} %bitcast.55, bf16[255,64,16]{0,2,1:T(8,128)(2,1)S(1)} %bitcast.60, bf16[255,64,16]{0,2,1:T(8,128)(2,1)S(1)} %bitcast.62), kind=kOutput, calls=%fused_computation.12 | convolution fusion | flops 136830976 | bytes 10444800 | tf_op jit(solution)/shard_map/tgn,sgn->gts/dot_general | solution.py:162
  56.0 1.5 %fusion.1 = f32[64,32,128]{2,1,0:T(8,128)S(1)} fusion(bf16[64,128,255]{2,1,0:T(8,128)(2,1)S(1)} %copy-done, bf16[255,64,16]{0,2,1:T(8,128)(2,1)S(1)} %bitcast.58, bf16[255,64,16]{0,2,1:T(8,128)(2,1)S(1)} %bitcast.56), kind=kOutput, calls=%fused_computation.13 | convolution fusion | flops 135782400 | bytes 6270976 | tf_op jit(solution)/shard_map/gts,sgn->tgn/dot_general | solution.py:155
  57.5 2.6 %convolution_bitcast_fusion = f32[128,64,32]{0,2,1:T(8,128)} fusion(bf16[64,128,255]{2,1,0:T(8,128)(2,1)S(1)} %copy-done, bf16[256,64,32]{0,2,1:T(8,128)(2,1)S(1)} %copy-done.1), kind=kOutput, calls=%fused_computation.2 | convolution fusion | flops 133693440 | bytes 6275072 | tf_op jit(solution)/shard_map/gts,sgn->tgn/dot_general | solution.py:157
  60.1 0.5 copy.64
  60.6 0.8 reshape.55
  61.5 0.3 copy.47
  61.8 1.2 multiply_convert_fusion.2
  63.0 1.5 %rev.18 = f32[128,64,32]{0,2,1:T(8,128)S(1)} reverse(f32[128,64,32]{0,2,1:T(8,128)} %convolution_bitcast_fusion), dimensions={0} | reverse | bytes 2097152 | tf_op jit(solution)/shard_map/jit(_flip)/rev | solution.py:156
  64.5 0.0 copy-start.4
  64.5 0.5 copy.50
  65.0 0.1 copy.63
  65.1 0.3 copy.51
  65.4 0.1 copy-done.4
  65.5 1.3 %fusion.2 = (bf16[1,256,1024]{2,1,0:T(8,128)(2,1)S(1)}, bf16[1,256,1024]{2,1,0:T(8,128)(2,1)S(1)}) fusion(f32[256,1024]{1,0:T(8,128)S(1)} %copy.51, bf16[256,1024]{1,0:T(8,128)(2,1)} %get-tuple-element.11, bf16[256,1024]{1,0:T(8,128)(2,1)S(1)} %copy-done.4), kind=kLoop, calls=%fused_computation.15 | loop fusion | flops 1572864 | bytes 3145728 | tf_op jit(solution)/shard_map/stack | solution.py:202
  66.9 1.5 %collective-permute-start.3 = (bf16[3,6,1024]{2,1,0:T(8,128)(2,1)S(1)}, bf16[3,6,1024]{2,1,0:T(8,128)(2,1)S(1)}, u32[]{:S(2)}, u32[]{:S(2)}) collective-permute-start(bf16[3,6,1024]{2,1,0:T(8,128)(2,1)S(1)} %pad_maximum_fusion.9), channel_id=1, source_target_pairs={{4,0},{8,4},{12,8},{16,12},{20,16},{24,20},{28,24},{32,28},{36,32}... | collective-permute-start | bytes 110600 | tf_op jit(solution)/shard_map/ppermute | solution.py:14
  68.4 9.2 %reshape.59 = f32[64,32640]{1,0:T(8,128)} reshape(f32[64,128,255]{2,1,0:T(8,128)} %fusion) | data formatting | bytes 16711680 | tf_op jit(solution)/shard_map/reshape | solution.py:125
  77.6 4.0 %pad.5 = f32[64,32768]{1,0:T(8,128)S(1)} pad(f32[64,32640]{1,0:T(8,128)} %reshape.59, f32[]{:T(128)} %constant.1.clone.1), padding=0_0x0_128 | pad | bytes 16744452 | tf_op jit(solution)/shard_map/jit(_pad)/pad | solution.py:124
  81.7 2.5 %copy.60 = f32[8,8,128,256]{3,2,1,0:T(8,128)S(1)} copy(f32[8,8,128,256]{3,1,2,0:T(8,128)S(1)} %bitcast.51) | data formatting | bytes 16777216
  84.2 0.5 slice_reduce_fusion
  84.7 0.1 rev.19
  84.8 0.0 collective-permute-done.3
  84.8 1.4 %pad_maximum_fusion.grads_ref = bf16[3,262,1024]{2,1,0:T(8,128)(2,1)} fusion(bf16[3,6,1024]{2,1,0:T(8,128)(2,1)S(1)} %collective-permute-done.3, bf16[1,256,1024]{2,1,0:T(8,128)(2,1)S(1)} %get-tuple-element.16, bf16[1,256,1024]{2,1,0:T(8,128)(2,1)S(1)} %get-tuple-element.15, bf16[1,256,1024]{2,1,0:T(8,128)(2,1)S(1)} %multiply_convert_fusion.2), kind=kLoop, calls=%fused_computation.1 | loop fusion | flops 6438912 | bytes 3219456 | tf_op jit(solution)/shard_map/concatenate | solution.py:204
  86.1 7.1 %shard_map.68 = (bf16[256,1024]{1,0:T(8,128)(2,1)}, f32[21,1024]{1,0:T(8,128)}) custom-call(f32[21,1024]{1,0:T(8,128)} %reshape_reshape.3.taps_ref, bf16[262,1024]{1,0:T(8,128)(2,1)} %pad_maximum_fusion.5.sig_ref, bf16[3,262,1024]{2,1,0:T(8,128)(2,1)} %pad_maximum_fusion.grads_ref), custom_call_target="tpu_custom_call" | custom-call | tf_op jit(solution)/shard_map/pallas_call | solution.py:90
  93.3 1.1 reshape.58
  94.4 0.3 reduce_sum.27
  94.7 0.1 copy.53
  94.8 0.1 pad_maximum_fusion.8
  94.9 0.7 reshape.61
  95.5 20.4 %all-to-all-start = ((f32[32,149,2]{1,2,0:T(2,128)}), f32[32,149,2]{1,2,0:T(2,128)S(1)}, u32[]{:S(2)}, u32[]{:S(2)}) async-start(f32[32,149,2]{1,2,0:T(2,128)} %bitcast.19), calls=%async_computation | async-start | bytes 131072 | tf_op jit(solution)/shard_map/all_to_all | solution.py:22
  115.9 1.3 collective-permute-start.4
  117.2 12.9 %all-to-all-done = f32[32,149,2]{1,2,0:T(2,128)S(1)} async-done(((f32[32,149,2]{1,2,0:T(2,128)}), f32[32,149,2]{1,2,0:T(2,128)S(1)}, u32[]{:S(2)}, u32[]{:S(2)}) %all-to-all-start) | async-done | bytes 38176 | tf_op jit(solution)/shard_map/all_to_all | solution.py:22
  130.2 0.6 slice_bitcast_fusion.2
  130.7 0.6 slice_bitcast_fusion.1
  131.4 0.0 collective-permute-done.4
  131.4 0.8 copy.66
  (11 shorter events, 0.1 us)
Async XLA Ops:
  0.6 16.8 %copy-start.5 = (bf16[1,128,64]{1,2,0:T(8,128)(2,1)S(1)}, bf16[1,128,64]{1,2,0:T(8,128)(2,1)}, u32[]{:S(2)}) copy-start(bf16[1,128,64]{1,2,0:T(8,128)(2,1)} %param.7) | copy-start | bytes 49156
  1.4 5.8 %collective-permute-start = (bf16[6,1024]{1,0:T(8,128)(2,1)S(1)}, bf16[6,1024]{1,0:T(8,128)(2,1)S(1)}, u32[]{:S(2)}, u32[]{:S(2)}) collective-permute-start(bf16[6,1024]{1,0:T(8,128)(2,1)S(1)} %slice_bitcast_fusion), channel_id=1, source_target_pairs={{0,4},{4,8},{8,12},{12,16},{16,20},{20,24},{24,28},{28,32},{32,36}... | collective-permute-start | bytes 36872 | tf_op jit(solution)/shard_map/ppermute | solution.py:14
  16.1 27.3 %collective-permute-start.2 = (bf16[127,1024]{1,0:T(8,128)(2,1)S(1)}, bf16[127,1024]{1,0:T(8,128)(2,1)S(1)}, u32[]{:S(2)}, u32[]{:S(2)}) collective-permute-start(bf16[127,1024]{1,0:T(8,128)(2,1)S(1)} %slice.66), channel_id=1, source_target_pairs={{4,0},{8,4},{12,8},{16,12},{20,16},{24,20},{28,24},{32,28},{36,32}... | collective-permute-start | bytes 780296 | tf_op jit(solution)/shard_map/ppermute | solution.py:14
  22.6 16.0 %copy-start.2 = (bf16[256,1024]{1,0:T(8,128)(2,1)S(1)}, bf16[256,1024]{1,0:T(8,128)(2,1)}, u32[]{:S(2)}) copy-start(bf16[256,1024]{1,0:T(8,128)(2,1)} %get-tuple-element.9) | copy-start | bytes 1572868
  22.6 20.8 %copy-start.3 = (bf16[256,1024]{1,0:T(8,128)(2,1)S(1)}, bf16[256,1024]{1,0:T(8,128)(2,1)}, u32[]{:S(2)}) copy-start(bf16[256,1024]{1,0:T(8,128)(2,1)} %get-tuple-element.10) | copy-start | bytes 1572868
  38.6 9.7 %collective-permute-start.1 = (bf16[127,1024]{1,0:T(8,128)(2,1)S(1)}, bf16[127,1024]{1,0:T(8,128)(2,1)S(1)}, u32[]{:S(2)}, u32[]{:S(2)}) collective-permute-start(bf16[127,1024]{1,0:T(8,128)(2,1)S(1)} %slice.58), channel_id=1, source_target_pairs={{0,4},{4,8},{8,12},{12,16},{16,20},{20,24},{24,28},{28,32},{32,36}... | collective-permute-start | bytes 780296 | tf_op jit(solution)/shard_map/ppermute | solution.py:14
  51.5 4.5 %copy-start = (bf16[64,128,255]{2,1,0:T(8,128)(2,1)S(1)}, bf16[64,128,255]{2,1,0:T(8,128)(2,1)}, u32[]{:S(2)}) copy-start(bf16[64,128,255]{2,1,0:T(8,128)(2,1)} %reshape.53) | copy-start | bytes 12533764
  56.0 1.5 %copy-start.1 = (bf16[256,64,32]{0,2,1:T(8,128)(2,1)S(1)}, bf16[256,64,32]{0,2,1:T(8,128)(2,1)}, u32[]{:S(2)}) copy-start(bf16[256,64,32]{0,2,1:T(8,128)(2,1)} %reverse) | copy-start | bytes 3145732
  64.5 1.0 copy-start.4
  66.9 17.9 %collective-permute-start.3 = (bf16[3,6,1024]{2,1,0:T(8,128)(2,1)S(1)}, bf16[3,6,1024]{2,1,0:T(8,128)(2,1)S(1)}, u32[]{:S(2)}, u32[]{:S(2)}) collective-permute-start(bf16[3,6,1024]{2,1,0:T(8,128)(2,1)S(1)} %pad_maximum_fusion.9), channel_id=1, source_target_pairs={{4,0},{8,4},{12,8},{16,12},{20,16},{24,20},{28,24},{32,28},{36,32}... | collective-permute-start | bytes 110600 | tf_op jit(solution)/shard_map/ppermute | solution.py:14
  95.5 34.6 %all-to-all-start = ((f32[32,149,2]{1,2,0:T(2,128)}), f32[32,149,2]{1,2,0:T(2,128)S(1)}, u32[]{:S(2)}, u32[]{:S(2)}) async-start(f32[32,149,2]{1,2,0:T(2,128)} %bitcast.19), calls=%async_computation | async-start | bytes 131072 | tf_op jit(solution)/shard_map/all_to_all | solution.py:22
  115.9 15.4 %collective-permute-start.4 = (bf16[1,256,1024]{2,1,0:T(8,128)(2,1)}, bf16[1,256,1024]{2,1,0:T(8,128)(2,1)S(1)}, u32[]{:S(2)}, u32[]{:S(2)}) collective-permute-start(bf16[1,256,1024]{2,1,0:T(8,128)(2,1)} %bitcast.74), channel_id=1, source_target_pairs={{128,0},{256,128},{384,256},{129,1},{257,129},{385,257},{130,2},{2... | collective-permute-start | bytes 1572872 | tf_op jit(solution)/shard_map/ppermute | solution.py:14

commit v4 on v3

--- a/solution.py
+++ b/solution.py
@@ -110,33 +110,45 @@
     )(taps, signal_pad, grads_pad)
 
 
+def band_kernel(taps_ref, out_ref):
+    group_block, rows, span = out_ref.shape
+    for group in range(group_block):
+        row = jnp.broadcast_to(taps_ref[pl.ds(group, 1), :], (rows, span))
+        out_ref[group] = pltpu.roll(row, 0, 1, stride=1, stride_axis=0).astype(out_ref.dtype)
+
+
 def band_matrix(filter_taps, out_rows):
     tap_count, group_count = filter_taps.shape
-    leading = jnp.flip(filter_taps, 0).T
-    padded = jnp.concatenate([leading, jnp.zeros((group_count, out_rows), filter_taps.dtype)], 1)
-    span_len = out_rows + tap_count - 1
-    tiled_rows = jnp.tile(padded, (1, out_rows))[:, : out_rows * span_len]
-    return tiled_rows.reshape(group_count, out_rows, span_len)
-
-
-def diagonal_sums(cross_terms, tap_count):
-    group_count, out_rows, span_len = cross_terms.shape
-    flat_view = jnp.pad(
-        cross_terms.reshape(group_count, out_rows * span_len), ((0, 0), (0, out_rows))
-    )
-    skewed = flat_view.reshape(group_count, out_rows, span_len + 1)
-    return jnp.flip(jnp.sum(skewed[:, :, :tap_count], axis=1), 1)
-
-
-def short_features(padded, chan_short, out_rows):
-    lag_count = chan_short.shape[1]
-    running = jnp.zeros((3, out_rows, padded.shape[1]), jnp.float32)
-    for offset in range(lag_count):
-        first_row = lag_count - 1 - offset
-        running = running + chan_short[:, offset, None, :] * padded[
-            None, first_row : first_row + out_rows
-        ].astype(jnp.float32)
-    return running.astype(jnp.bfloat16)
+    span = out_rows + tap_count
+    leading = jnp.flip(filter_taps, 0).T.astype(jnp.float32)
+    padded = jnp.concatenate([leading, jnp.zeros((group_count, out_rows), jnp.float32)], 1)
+    group_block = 8
+    return pl.pallas_call(
+        band_kernel,
+        grid=(group_count // group_block,),
+        in_specs=[pl.BlockSpec((group_block, span), lambda j: (j, 0))],
+        out_specs=pl.BlockSpec((group_block, out_rows, span), lambda j: (j, 0, 0)),
+        out_shape=jax.ShapeDtypeStruct((group_count, out_rows, span), filter_taps.dtype),
+    )(padded)
+
+
+def diagonal_kernel(cross_ref, out_ref):
+    group_block, rows, span = cross_ref.shape
+    for group in range(group_block):
+        rolled = pltpu.roll(cross_ref[group], 0, 1, stride=1, stride_axis=0)
+        out_ref[pl.ds(group, 1), :] = jnp.sum(rolled[:, span - rows :], axis=0, keepdims=True)
+
+
+def diagonal_sums(cross_flipped):
+    group_count, rows, span = cross_flipped.shape
+    group_block = 8
+    return pl.pallas_call(
+        diagonal_kernel,
+        grid=(group_count // group_block,),
+        in_specs=[pl.BlockSpec((group_block, rows, span), lambda j: (j, 0, 0))],
+        out_specs=pl.BlockSpec((group_block, rows), lambda j: (j, 0)),
+        out_shape=jax.ShapeDtypeStruct((group_count, rows), jnp.float32),
+    )(cross_flipped)
 
 
 def medium_terms(medium_taps, kv_pad, gate_ext, row_block):
@@ -144,14 +156,17 @@
     seq_rows = gate_ext.shape[0] - tap_count + 1
     chan_count = kv_pad.shape[1]
     group_width = chan_count // group_count
-    span_len = row_block + tap_count - 1
+    span_len = row_block + tap_count
     block_count = seq_rows // row_block
     toeplitz = band_matrix(medium_taps, row_block)
-    kv_groups = kv_pad.reshape(-1, group_count, group_width)
-    gate_groups = gate_ext.reshape(-1, group_count, group_width)
+    zero_row = jnp.zeros((1, chan_count), kv_pad.dtype)
+    kv_groups = jnp.concatenate([kv_pad, zero_row], 0).reshape(-1, group_count, group_width)
+    gate_groups = jnp.concatenate([zero_row, gate_ext], 0).reshape(-1, group_count, group_width)
+    row_groups = gate_ext.reshape(-1, group_count, group_width)
     starts = [b * row_block for b in range(block_count)]
     kv_win = jnp.concatenate([kv_groups[b : b + span_len] for b in starts], axis=2)
     gate_win = jnp.concatenate([gate_groups[b : b + span_len] for b in starts], axis=2)
+    gate_rows = jnp.concatenate([row_groups[b : b + row_block] for b in starts], axis=2)
     mixed_out = jnp.einsum("gts,sgn->tgn", toeplitz, kv_win, preferred_element_type=jnp.float32)
     back_out = jnp.flip(
         jnp.einsum(
@@ -159,10 +174,10 @@
         ),
         0,
     )
-    cross_terms = jnp.einsum(
-        "tgn,sgn->gts", gate_win[:row_block], kv_win, preferred_element_type=jnp.float32
-    )
-    taps_grad = diagonal_sums(cross_terms, tap_count).T
+    cross_flipped = jnp.einsum(
+        "tgn,sgn->gts", gate_rows, jnp.flip(kv_win, 0), preferred_element_type=jnp.float32
+    )
+    taps_grad = diagonal_sums(cross_flipped).T
 
     def unblock(values_in):
         split = values_in.reshape(row_block, group_count, block_count, group_width)

time: 133 us -> 118 us (0.89)
  the two profiles are of different devices: /device:TPU:16 before, /device:TPU:8 now
where the time goes in v4:
time: 118 us; the launch traced here: 116 us
  starting transfers between devices  33.5 us (28%)
  Pallas kernels  26.4 us (22%)
  local copies, waits for them, and re-layouts  22 us (19%)
  waiting for transfers between devices  14.9 us (13%)
  matrix products  10.9 us (9%)
  other arithmetic  7.46 us (6%)
    all_to_all x1, starting transfers between devices, owned_sum(): return jnp.sum(lax.all_to_all(chunks, axis, 0, 0, tiled=False), axis=0)  20.4 us
    ppermute x5, starting transfers between devices, passed_along(): return lax.ppermute(block, axis, route)  13.1 us
    all_to_all x1, waiting for transfers between devices, owned_sum(): return jnp.sum(lax.all_to_all(chunks, axis, 0, 0, tiled=False), axis=0)  12.9 us
    pallas_call x1, Pallas kernels, diagonal_sums(): pl.pallas_call(diagonal_kernel, grid=(group_count // group_block,), in_sp...  7.68 us
    pallas_call x1, Pallas kernels, short_back(): pl.pallas_call(back_kernel, grid=(chan_count // LANE_BLOCK,), in_specs=[p...  7.13 us
    pallas_call x1, Pallas kernels, short_front(): pl.pallas_call(front_kernel, grid=(chan_count // LANE_BLOCK,), in_specs=[...  6 us
    pallas_call x1, Pallas kernels, band_matrix(): pl.pallas_call(band_kernel, grid=(group_count // group_block,), in_specs=...  5.57 us
    dot_general x1, matrix products, medium_terms(): jnp.einsum('gts,sgn->tgn', toeplitz, kv_win, preferred_element_type=jnp.f...  4.87 us
  transfers between devices with their start and end apart: 6, of which 2 were waited for; matrix products, arithmetic and copies ran while one was open for 13% of the time, Pallas kernels for 11%

profile of v4, /device:TPU:8, one launch (start us, length us, event | category | flops | bytes accessed | tf_op | source)
XLA Modules:
  0.0 116.0 jit_solution(14771698097739368834)
XLA Ops:
  0.6 0.7 slice_bitcast_fusion
  1.4 3.8 %collective-permute-start = (bf16[6,1024]{1,0:T(8,128)(2,1)S(1)}, bf16[6,1024]{1,0:T(8,128)(2,1)S(1)}, u32[]{:S(2)}, u32[]{:S(2)}) collective-permute-start(bf16[6,1024]{1,0:T(8,128)(2,1)S(1)} %slice_bitcast_fusion), channel_id=1, source_target_pairs={{0,4},{4,8},{8,12},{12,16},{16,20},{20,24},{24,28},{28,32},{32,36}... | collective-permute-start | bytes 36872 | tf_op jit(solution)/shard_map/ppermute | solution.py:14
  5.2 0.7 reshape.49
  5.9 0.2 broadcast_in_dim.16
  6.1 1.0 reshape_reshape.3.taps_ref
  7.1 0.8 rev.15
  7.9 0.0 collective-permute-done
  8.0 2.0 %pad_maximum_fusion.3.sig_ref = bf16[262,1024]{1,0:T(8,128)(2,1)} fusion(bf16[256,1024]{1,0:T(8,128)(2,1)} %bitcast.64, bf16[6,1024]{1,0:T(8,128)(2,1)S(1)} %collective-permute-done), kind=kLoop, calls=%fused_computation.9 | loop fusion | flops 1073152 | bytes 1073152 | tf_op jit(solution)/shard_map/concatenate | solution.py:206
  10.0 6.0 %shard_map.67 = (bf16[256,1024]{1,0:T(8,128)(2,1)}, bf16[256,1024]{1,0:T(8,128)(2,1)}, bf16[256,1024]{1,0:T(8,128)(2,1)}, bf16[256,1024]{1,0:T(8,128)(2,1)}, bf16[256,1024]{1,0:T(8,128)(2,1)}) custom-call(f32[21,1024]{1,0:T(8,128)} %reshape_reshape.3.taps_ref, bf16[262,1024]{1,0:T(8,128)(2,1)} %pad_maximum_fusion.3.sig_ref, bf16[256,1024]{1,0:T(8,128)(2,1)} %bitcast.59), custom_call_target="tpu_custom_call" | custom-call | tf_op jit(solution)/shard_map/pallas_call | solution.py:50
  16.0 1.0 slice.72
  16.9 1.3 %collective-permute-start.2 = (bf16[127,1024]{1,0:T(8,128)(2,1)S(1)}, bf16[127,1024]{1,0:T(8,128)(2,1)S(1)}, u32[]{:S(2)}, u32[]{:S(2)}) collective-permute-start(bf16[127,1024]{1,0:T(8,128)(2,1)S(1)} %slice.72), channel_id=1, source_target_pairs={{4,0},{8,4},{12,8},{16,12},{20,16},{24,20},{28,24},{32,28},{36,32}... | collective-permute-start | bytes 780296 | tf_op jit(solution)/shard_map/ppermute | solution.py:14
  18.2 0.6 pad_convert_fusion.taps_ref
  18.9 5.6 %shard_map.68 = bf16[64,128,256]{2,1,0:T(8,128)(2,1)} custom-call(f32[64,256]{1,0:T(8,128)} %pad_convert_fusion.taps_ref), custom_call_target="tpu_custom_call" | custom-call | tf_op jit(solution)/shard_map/pallas_call | solution.py:126
  24.4 0.0 copy-done.3
  24.4 0.8 slice.65
  25.2 5.3 %collective-permute-start.1 = (bf16[127,1024]{1,0:T(8,128)(2,1)}, bf16[127,1024]{1,0:T(8,128)(2,1)}, u32[]{:S(2)}, u32[]{:S(2)}) collective-permute-start(bf16[127,1024]{1,0:T(8,128)(2,1)} %slice.65), channel_id=1, source_target_pairs={{0,4},{4,8},{8,12},{12,16},{16,20},{20,24},{24,28},{28,32},{32,36}... | collective-permute-start | bytes 780296 | tf_op jit(solution)/shard_map/ppermute | solution.py:14
  30.5 0.0 copy-done.1
  30.5 0.2 copy.35
  30.7 0.8 copy.36
  31.5 0.0 collective-permute-done.2
  31.5 0.2 pad_slice_fusion
  31.8 0.2 copy.30
  32.0 0.2 copy.31
  32.2 0.1 pad_maximum_fusion.2
  32.3 0.9 rev.16
  33.3 2.0 %collective-permute-done.1 = bf16[127,1024]{1,0:T(8,128)(2,1)} collective-permute-done((bf16[127,1024]{1,0:T(8,128)(2,1)}, bf16[127,1024]{1,0:T(8,128)(2,1)}, u32[]{:S(2)}, u32[]{:S(2)}) %collective-permute-start.1) | collective-permute-done | bytes 260128 | tf_op jit(solution)/shard_map/ppermute | solution.py:14
  35.2 1.1 pad_maximum_fusion.5
  36.4 0.2 copy.26
  36.6 0.2 copy.27
  36.8 1.1 pad_maximum_fusion.1
  37.9 4.9 %fusion.7 = f32[64,32,128]{2,1,0:T(8,128)} fusion(bf16[64,128,256]{2,1,0:T(8,128)(2,1)} %shard_map.68, bf16[256,64,16]{0,2,1:T(8,128)(2,1)S(1)} %bitcast.53, bf16[256,64,16]{0,2,1:T(8,128)(2,1)S(1)} %bitcast.51), kind=kOutput, calls=%fused_computation.28 | convolution fusion | flops 136314880 | bytes 6291456 | tf_op jit(solution)/shard_map/gts,sgn->tgn/dot_general | solution.py:170
  42.8 1.5 %convolution_bitcast_fusion = f32[128,64,32]{0,2,1:T(8,128)S(1)} fusion(bf16[256,64,32]{0,2,1:T(8,128)(2,1)S(1)} %rev.16, bf16[64,128,256]{2,1,0:T(8,128)(2,1)S(1)} %copy-done), kind=kOutput, calls=%fused_computation.1 | convolution fusion | flops 134217728 | bytes 6291456 | tf_op jit(solution)/shard_map/gts,sgn->tgn/dot_general | solution.py:172
  44.3 0.5 rev.17
  44.8 0.5 copy.32
  45.4 0.1 copy.41
  45.5 0.3 copy.33
  45.8 1.8 %copy.42 = f32[128,64,2,16]{0,2,3,1:T(2,128)S(1)} copy(f32[128,64,2,16]{0,3,2,1:T(8,128)} %bitcast.58) | data formatting | bytes 2097152 | tf_op jit(solution)/shard_map/reshape | solution.py:183
  47.6 0.0 copy-start.2
  47.6 1.8 %reshape.44 = f32[1,256,1024]{1,2,0:T(8,128)} reshape(f32[2,128,64,16]{1,0,3,2:T(2,128)S(1)} %bitcast.57) | data formatting | bytes 2097152 | tf_op jit(solution)/shard_map/reshape | solution.py:184
  49.4 1.6 %copy.29 = f32[1,256,1024]{2,1,0:T(8,128)S(1)} copy(f32[1,256,1024]{1,2,0:T(8,128)} %reshape.44) | data formatting | bytes 2097152 | tf_op jit(solution)/shard_map/reshape | solution.py:184
  51.0 0.1 multiply_convert_fusion.2
  51.1 0.9 copy-done.5
  52.0 0.2 copy-done.6
  52.2 0.3 fusion
  52.5 1.4 %collective-permute-start.3 = (bf16[3,6,1024]{2,1,0:T(8,128)(2,1)S(1)}, bf16[3,6,1024]{2,1,0:T(8,128)(2,1)S(1)}, u32[]{:S(2)}, u32[]{:S(2)}) collective-permute-start(bf16[3,6,1024]{2,1,0:T(8,128)(2,1)S(1)} %pad_maximum_fusion.7), channel_id=1, source_target_pairs={{4,0},{8,4},{12,8},{16,12},{20,16},{24,20},{28,24},{32,28},{36,32}... | collective-permute-start | bytes 110600 | tf_op jit(solution)/shard_map/ppermute | solution.py:14
  53.9 2.5 %rev.18 = bf16[256,64,32]{0,2,1:T(8,128)(2,1)S(1)} reverse(bf16[256,64,32]{0,2,1:T(8,128)(2,1)} %pad_maximum_fusion.1), dimensions={0} | reverse | bytes 2097152 | tf_op jit(solution)/shard_map/jit(_flip)/rev | solution.py:178
  56.4 0.0 copy-done.4
  56.4 4.5 %fusion.2.cross_ref = f32[64,128,256]{2,1,0:T(8,128)} fusion(bf16[256,64,32]{0,2,1:T(8,128)(2,1)S(1)} %rev.18, bf16[128,64,16]{0,2,1:T(8,128)(2,1)S(1)} %bitcast.63, bf16[128,64,16]{0,2,1:T(8,128)(2,1)S(1)} %bitcast.62), kind=kOutput, calls=%fused_computation.16 | convolution fusion | flops 135266304 | bytes 9961472 | tf_op jit(solution)/shard_map/tgn,sgn->gts/dot_general | solution.py:177
  60.9 7.7 %shard_map.70 = f32[64,128]{1,0:T(8,128)} custom-call(f32[64,128,256]{2,1,0:T(8,128)} %fusion.2.cross_ref), custom_call_target="tpu_custom_call" | custom-call | tf_op jit(solution)/shard_map/pallas_call | solution.py:145
  68.6 0.0 collective-permute-done.3
  68.6 1.4 %pad_maximum_fusion.grads_ref = bf16[3,262,1024]{2,1,0:T(8,128)(2,1)} fusion(bf16[3,6,1024]{2,1,0:T(8,128)(2,1)S(1)} %collective-permute-done.3, bf16[1,256,1024]{2,1,0:T(8,128)(2,1)S(1)} %get-tuple-element.16, bf16[1,256,1024]{2,1,0:T(8,128)(2,1)S(1)} %get-tuple-element.15, bf16[1,256,1024]{2,1,0:T(8,128)(2,1)S(1)} %multiply_convert_fusion.2), kind=kLoop, calls=%fused_computation | loop fusion | flops 6438912 | bytes 3219456 | tf_op jit(solution)/shard_map/concatenate | solution.py:219
  70.0 7.1 %shard_map.69 = (bf16[256,1024]{1,0:T(8,128)(2,1)}, f32[21,1024]{1,0:T(8,128)}) custom-call(f32[21,1024]{1,0:T(8,128)} %reshape_reshape.3.taps_ref, bf16[262,1024]{1,0:T(8,128)(2,1)} %pad_maximum_fusion.3.sig_ref, bf16[3,262,1024]{2,1,0:T(8,128)(2,1)} %pad_maximum_fusion.grads_ref), custom_call_target="tpu_custom_call" | custom-call | tf_op jit(solution)/shard_map/pallas_call | solution.py:90
  77.1 1.1 reshape.47
  78.3 0.3 reduce_sum.18
  78.5 0.1 copy.37
  78.6 0.1 pad_maximum_fusion.6
  78.7 0.7 reshape.48
  79.4 20.4 %all-to-all-start = ((f32[32,149,2]{1,2,0:T(2,128)}), f32[32,149,2]{1,2,0:T(2,128)S(1)}, u32[]{:S(2)}, u32[]{:S(2)}) async-start(f32[32,149,2]{1,2,0:T(2,128)} %bitcast.21), calls=%async_computation | async-start | bytes 131072 | tf_op jit(solution)/shard_map/all_to_all | solution.py:22
  99.8 1.3 %collective-permute-start.4 = (bf16[1,256,1024]{2,1,0:T(8,128)(2,1)}, bf16[1,256,1024]{2,1,0:T(8,128)(2,1)S(1)}, u32[]{:S(2)}, u32[]{:S(2)}) collective-permute-start(bf16[1,256,1024]{2,1,0:T(8,128)(2,1)} %bitcast.68), channel_id=1, source_target_pairs={{128,0},{256,128},{384,256},{129,1},{257,129},{385,257},{130,2},{2... | collective-permute-start | bytes 1572872 | tf_op jit(solution)/shard_map/ppermute | solution.py:14
  101.0 12.9 %all-to-all-done = f32[32,149,2]{1,2,0:T(2,128)S(1)} async-done(((f32[32,149,2]{1,2,0:T(2,128)}), f32[32,149,2]{1,2,0:T(2,128)S(1)}, u32[]{:S(2)}, u32[]{:S(2)}) %all-to-all-start) | async-done | bytes 38176 | tf_op jit(solution)/shard_map/all_to_all | solution.py:22
  114.0 0.6 slice_bitcast_fusion.1
  114.6 0.6 slice_bitcast_fusion.2
  115.2 0.0 collective-permute-done.4
  115.2 0.8 copy.44
  (13 shorter events, 0.1 us)
Async XLA Ops:
  1.4 6.6 %collective-permute-start = (bf16[6,1024]{1,0:T(8,128)(2,1)S(1)}, bf16[6,1024]{1,0:T(8,128)(2,1)S(1)}, u32[]{:S(2)}, u32[]{:S(2)}) collective-permute-start(bf16[6,1024]{1,0:T(8,128)(2,1)S(1)} %slice_bitcast_fusion), channel_id=1, source_target_pairs={{0,4},{4,8},{8,12},{12,16},{16,20},{20,24},{24,28},{28,32},{32,36}... | collective-permute-start | bytes 36872 | tf_op jit(solution)/shard_map/ppermute | solution.py:14
  16.9 14.6 %collective-permute-start.2 = (bf16[127,1024]{1,0:T(8,128)(2,1)S(1)}, bf16[127,1024]{1,0:T(8,128)(2,1)S(1)}, u32[]{:S(2)}, u32[]{:S(2)}) collective-permute-start(bf16[127,1024]{1,0:T(8,128)(2,1)S(1)} %slice.72), channel_id=1, source_target_pairs={{4,0},{8,4},{12,8},{16,12},{20,16},{24,20},{28,24},{32,28},{36,32}... | collective-permute-start | bytes 780296 | tf_op jit(solution)/shard_map/ppermute | solution.py:14
  18.9 5.6 %copy-start.3 = (bf16[256,1024]{1,0:T(8,128)(2,1)S(1)}, bf16[256,1024]{1,0:T(8,128)(2,1)}, u32[]{:S(2)}) copy-start(bf16[256,1024]{1,0:T(8,128)(2,1)} %get-tuple-element.9) | copy-start | bytes 1572868
  18.9 11.6 %copy-start.1 = (bf16[256,1024]{1,0:T(8,128)(2,1)S(1)}, bf16[256,1024]{1,0:T(8,128)(2,1)}, u32[]{:S(2)}) copy-start(bf16[256,1024]{1,0:T(8,128)(2,1)} %get-tuple-element.10) | copy-start | bytes 1572868
  25.2 10.0 %collective-permute-start.1 = (bf16[127,1024]{1,0:T(8,128)(2,1)}, bf16[127,1024]{1,0:T(8,128)(2,1)}, u32[]{:S(2)}, u32[]{:S(2)}) collective-permute-start(bf16[127,1024]{1,0:T(8,128)(2,1)} %slice.65), channel_id=1, source_target_pairs={{0,4},{4,8},{8,12},{12,16},{16,20},{20,24},{24,28},{28,32},{32,36}... | collective-permute-start | bytes 780296 | tf_op jit(solution)/shard_map/ppermute | solution.py:14
  37.9 4.9 %copy-start = (bf16[64,128,256]{2,1,0:T(8,128)(2,1)S(1)}, bf16[64,128,256]{2,1,0:T(8,128)(2,1)}, u32[]{:S(2)}) copy-start(bf16[64,128,256]{2,1,0:T(8,128)(2,1)} %shard_map.68) | copy-start | bytes 12582916
  47.6 3.4 %copy-start.2 = (bf16[1,256,1024]{2,1,0:T(8,128)(2,1)S(1)}, bf16[1,256,1024]{2,1,0:T(8,128)(2,1)}, u32[]{:S(2)}) copy-start(bf16[1,256,1024]{2,1,0:T(8,128)(2,1)} %param.5) | copy-start | bytes 1572868
  51.0 1.0 copy-start.5
  51.0 1.2 %copy-start.6 = (bf16[256,1024]{1,0:T(8,128)(2,1)S(1)}, bf16[256,1024]{1,0:T(8,128)(2,1)}, u32[]{:S(2)}) copy-start(bf16[256,1024]{1,0:T(8,128)(2,1)} %get-tuple-element.11) | copy-start | bytes 1572868
  52.5 3.9 %copy-start.4 = (bf16[128,1024]{0,1:T(8,128)(2,1)S(1)}, bf16[128,1024]{0,1:T(8,128)(2,1)}, u32[]{:S(2)}) copy-start(bf16[128,1024]{0,1:T(8,128)(2,1)} %copy.36) | copy-start | bytes 786436
  52.5 16.1 %collective-permute-start.3 = (bf16[3,6,1024]{2,1,0:T(8,128)(2,1)S(1)}, bf16[3,6,1024]{2,1,0:T(8,128)(2,1)S(1)}, u32[]{:S(2)}, u32[]{:S(2)}) collective-permute-start(bf16[3,6,1024]{2,1,0:T(8,128)(2,1)S(1)} %pad_maximum_fusion.7), channel_id=1, source_target_pairs={{4,0},{8,4},{12,8},{16,12},{20,16},{24,20},{28,24},{32,28},{36,32}... | collective-permute-start | bytes 110600 | tf_op jit(solution)/shard_map/ppermute | solution.py:14
  70.0 8.6 %copy-start.7 = (f32[64,128]{1,0:T(8,128)S(1)}, f32[64,128]{1,0:T(8,128)}, u32[]{:S(2)}) copy-start(f32[64,128]{1,0:T(8,128)} %shard_map.70) | copy-start | bytes 98308
  79.4 34.6 %all-to-all-start = ((f32[32,149,2]{1,2,0:T(2,128)}), f32[32,149,2]{1,2,0:T(2,128)S(1)}, u32[]{:S(2)}, u32[]{:S(2)}) async-start(f32[32,149,2]{1,2,0:T(2,128)} %bitcast.21), calls=%async_computation | async-start | bytes 131072 | tf_op jit(solution)/shard_map/all_to_all | solution.py:22
  99.8 15.5 %collective-permute-start.4 = (bf16[1,256,1024]{2,1,0:T(8,128)(2,1)}, bf16[1,256,1024]{2,1,0:T(8,128)(2,1)S(1)}, u32[]{:S(2)}, u32[]{:S(2)}) collective-permute-start(bf16[1,256,1024]{2,1,0:T(8,128)(2,1)} %bitcast.68), channel_id=1, source_target_pairs={{128,0},{256,128},{384,256},{129,1},{257,129},{385,257},{130,2},{2... | collective-permute-start | bytes 1572872 | tf_op jit(solution)/shard_map/ppermute | solution.py:14

commit v5 on v3

--- a/solution.py
+++ b/solution.py
@@ -110,33 +110,36 @@
     )(taps, signal_pad, grads_pad)
 
 
-def band_matrix(filter_taps, out_rows):
-    tap_count, group_count = filter_taps.shape
-    leading = jnp.flip(filter_taps, 0).T
-    padded = jnp.concatenate([leading, jnp.zeros((group_count, out_rows), filter_taps.dtype)], 1)
-    span_len = out_rows + tap_count - 1
-    tiled_rows = jnp.tile(padded, (1, out_rows))[:, : out_rows * span_len]
-    return tiled_rows.reshape(group_count, out_rows, span_len)
-
-
-def diagonal_sums(cross_terms, tap_count):
-    group_count, out_rows, span_len = cross_terms.shape
-    flat_view = jnp.pad(
-        cross_terms.reshape(group_count, out_rows * span_len), ((0, 0), (0, out_rows))
-    )
-    skewed = flat_view.reshape(group_count, out_rows, span_len + 1)
-    return jnp.flip(jnp.sum(skewed[:, :, :tap_count], axis=1), 1)
-
-
-def short_features(padded, chan_short, out_rows):
-    lag_count = chan_short.shape[1]
-    running = jnp.zeros((3, out_rows, padded.shape[1]), jnp.float32)
-    for offset in range(lag_count):
-        first_row = lag_count - 1 - offset
-        running = running + chan_short[:, offset, None, :] * padded[
-            None, first_row : first_row + out_rows
-        ].astype(jnp.float32)
-    return running.astype(jnp.bfloat16)
+def medium_kernel(fwd_ref, bwd_ref, kv_ref, kvf_ref, gate_ref, mixed_ref, back_ref, taps_ref):
+    group_block, span = fwd_ref.shape
+    rows = taps_ref.shape[1]
+    block_count = mixed_ref.shape[0] // rows
+    lanes = mixed_ref.shape[1]
+    group_width = lanes // group_block
+    lane_group = lax.broadcasted_iota(jnp.int32, (1, lanes), 1) // group_width
+    mixed_ref[...] = jnp.zeros(mixed_ref.shape, mixed_ref.dtype)
+    back_ref[...] = jnp.zeros(back_ref.shape, back_ref.dtype)
+    for group in range(group_block):
+        in_group = lane_group == group
+        fwd = jnp.broadcast_to(fwd_ref[pl.ds(group, 1), :], (rows, span))
+        bwd = jnp.broadcast_to(bwd_ref[pl.ds(group, 1), :], (rows, span))
+        fwd_band = pltpu.roll(fwd, 0, 1, stride=1, stride_axis=0).astype(jnp.bfloat16)
+        bwd_band = pltpu.roll(bwd, 0, 1, stride=1, stride_axis=0).astype(jnp.bfloat16)
+        cross = None
+        for blk in range(block_count):
+            out_rows = pl.ds(blk * rows, rows)
+            mixed = jnp.dot(fwd_band, kv_ref[pl.ds(blk * rows, span), :], preferred_element_type=jnp.float32)
+            mixed_ref[out_rows, :] = jnp.where(in_group, mixed, mixed_ref[out_rows, :])
+            back = jnp.dot(bwd_band, gate_ref[pl.ds(blk * rows, span), :], preferred_element_type=jnp.float32)
+            back_ref[out_rows, :] = jnp.where(in_group, back, back_ref[out_rows, :])
+            gate_rows = jnp.where(in_group, gate_ref[out_rows, :], jnp.zeros((), gate_ref.dtype))
+            flipped = kvf_ref[pl.ds((block_count - 1 - blk) * rows, span), :]
+            part = lax.dot_general(
+                gate_rows, flipped, (((1,), (1,)), ((), ())), preferred_element_type=jnp.float32
+            )
+            cross = part if cross is None else cross + part
+        rolled = pltpu.roll(cross, 0, 1, stride=1, stride_axis=0)
+        taps_ref[pl.ds(group, 1), :] = jnp.sum(rolled[:, span - rows :], axis=0, keepdims=True)
 
 
 def medium_terms(medium_taps, kv_pad, gate_ext, row_block):
@@ -144,31 +147,30 @@
     seq_rows = gate_ext.shape[0] - tap_count + 1
     chan_count = kv_pad.shape[1]
     group_width = chan_count // group_count
-    span_len = row_block + tap_count - 1
-    block_count = seq_rows // row_block
-    toeplitz = band_matrix(medium_taps, row_block)
-    kv_groups = kv_pad.reshape(-1, group_count, group_width)
-    gate_groups = gate_ext.reshape(-1, group_count, group_width)
-    starts = [b * row_block for b in range(block_count)]
-    kv_win = jnp.concatenate([kv_groups[b : b + span_len] for b in starts], axis=2)
-    gate_win = jnp.concatenate([gate_groups[b : b + span_len] for b in starts], axis=2)
-    mixed_out = jnp.einsum("gts,sgn->tgn", toeplitz, kv_win, preferred_element_type=jnp.float32)
-    back_out = jnp.flip(
-        jnp.einsum(
-            "gts,sgn->tgn", toeplitz, jnp.flip(gate_win, 0), preferred_element_type=jnp.float32
-        ),
-        0,
-    )
-    cross_terms = jnp.einsum(
-        "tgn,sgn->gts", gate_win[:row_block], kv_win, preferred_element_type=jnp.float32
-    )
-    taps_grad = diagonal_sums(cross_terms, tap_count).T
-
-    def unblock(values_in):
-        split = values_in.reshape(row_block, group_count, block_count, group_width)
-        return split.transpose(2, 0, 1, 3).reshape(seq_rows, chan_count)
-
-    return unblock(mixed_out), unblock(back_out), taps_grad
+    span = row_block + tap_count
+    group_block = LANE_BLOCK // group_width
+    zero_taps = jnp.zeros((group_count, span - tap_count), jnp.float32)
+    fwd_taps = jnp.concatenate([jnp.flip(medium_taps, 0).T.astype(jnp.float32), zero_taps], 1)
+    bwd_taps = jnp.concatenate([medium_taps.T.astype(jnp.float32), zero_taps], 1)
+    zero_row = jnp.zeros((1, chan_count), kv_pad.dtype)
+    kv_full = jnp.concatenate([kv_pad, zero_row], 0)
+    gate_full = jnp.concatenate([gate_ext, zero_row], 0)
+    padded_rows = kv_full.shape[0]
+    taps_spec = pl.BlockSpec((group_block, span), lambda j: (j, 0))
+    full_spec = pl.BlockSpec((padded_rows, LANE_BLOCK), lambda j: (0, j))
+    out_spec = pl.BlockSpec((seq_rows, LANE_BLOCK), lambda j: (0, j))
+    mixed_out, back_out, taps_grad = pl.pallas_call(
+        medium_kernel,
+        grid=(chan_count // LANE_BLOCK,),
+        in_specs=[taps_spec, taps_spec, full_spec, full_spec, full_spec],
+        out_specs=[out_spec, out_spec, pl.BlockSpec((group_block, tap_count), lambda j: (j, 0))],
+        out_shape=[
+            jax.ShapeDtypeStruct((seq_rows, chan_count), jnp.float32),
+            jax.ShapeDtypeStruct((seq_rows, chan_count), jnp.float32),
+            jax.ShapeDtypeStruct((group_count, tap_count), jnp.float32),
+        ],
+    )(fwd_taps, bwd_taps, kv_full, jnp.flip(kv_full, 0), gate_full)
+    return mixed_out, back_out, taps_grad.T
 
 
 def per_device(inputs, upstream, short_filter, medium_filter):

time: 133 us -> 104 us (0.78)
  the two profiles are of different devices: /device:TPU:16 before, /device:TPU:24 now
where the time goes in v5:
time: 104 us; the launch traced here: 103 us
  starting transfers between devices  31 us (30%)
  Pallas kernels  24.1 us (23%)
  waiting for transfers between devices  21.7 us (21%)
  local copies, waits for them, and re-layouts  16.7 us (16%)
  other arithmetic  8.44 us (8%)
    all_to_all x1, starting transfers between devices, owned_sum(): return jnp.sum(lax.all_to_all(chunks, axis, 0, 0, tiled=False), axis=0)  18.7 us
    all_to_all x1, waiting for transfers between devices, owned_sum(): return jnp.sum(lax.all_to_all(chunks, axis, 0, 0, tiled=False), axis=0)  12.8 us
    ppermute x5, starting transfers between devices, passed_along(): return lax.ppermute(block, axis, route)  12.2 us
    pallas_call x1, Pallas kernels, medium_terms(): pl.pallas_call(medium_kernel, grid=(chan_count // LANE_BLOCK,), in_specs=...  11 us
    ppermute x5, waiting for transfers between devices, passed_along(): return lax.ppermute(block, axis, route)  8.88 us
    rev x1, local copies, waits for them, and re-layouts, medium_terms(): jnp.flip(kv_full, 0)  7.86 us
    pallas_call x1, Pallas kernels, short_back(): pl.pallas_call(back_kernel, grid=(chan_count // LANE_BLOCK,), in_specs=[p...  7.12 us
    pallas_call x1, Pallas kernels, short_front(): pl.pallas_call(front_kernel, grid=(chan_count // LANE_BLOCK,), in_specs=[...  6.01 us
  transfers between devices with their start and end apart: 6, of which 4 were waited for; matrix products, arithmetic and copies ran while one was open for 4% of the time, Pallas kernels for 0%

profile of v5, /device:TPU:24, one launch (start us, length us, event | category | flops | bytes accessed | tf_op | source)
XLA Modules:
  0.0 102.7 jit_solution(9536450679969252973)
XLA Ops:
  0.6 0.0 copy-start.2
  0.6 0.8 slice_bitcast_fusion
  1.4 3.8 %collective-permute-start = (bf16[6,1024]{1,0:T(8,128)(2,1)S(1)}, bf16[6,1024]{1,0:T(8,128)(2,1)S(1)}, u32[]{:S(2)}, u32[]{:S(2)}) collective-permute-start(bf16[6,1024]{1,0:T(8,128)(2,1)S(1)} %slice_bitcast_fusion), channel_id=1, source_target_pairs={{0,4},{4,8},{8,12},{12,16},{16,20},{20,24},{24,28},{28,32},{32,36}... | collective-permute-start | bytes 36872 | tf_op jit(solution)/shard_map/ppermute | solution.py:14
  5.2 0.7 reshape.23
  5.9 0.2 broadcast_in_dim.18
  6.2 1.0 reshape_reshape.3.taps_ref
  7.2 0.0 collective-permute-done
  7.2 0.0 copy-done.2
  7.2 0.0 copy-start.5
  7.2 1.0 pad_maximum_fusion.1.sig_ref
  8.2 6.0 %shard_map.67 = (bf16[256,1024]{1,0:T(8,128)(2,1)}, bf16[256,1024]{1,0:T(8,128)(2,1)}, bf16[256,1024]{1,0:T(8,128)(2,1)}, bf16[256,1024]{1,0:T(8,128)(2,1)}, bf16[256,1024]{1,0:T(8,128)(2,1)}) custom-call(f32[21,1024]{1,0:T(8,128)} %reshape_reshape.3.taps_ref, bf16[262,1024]{1,0:T(8,128)(2,1)} %pad_maximum_fusion.1.sig_ref, bf16[256,1024]{1,0:T(8,128)(2,1)} %bitcast.27), custom_call_target="tpu_custom_call" | custom-call | tf_op jit(solution)/shard_map/pallas_call | solution.py:50
  14.2 1.0 slice.23
  15.2 1.0 slice.24
  16.2 1.3 %collective-permute-start.2 = (bf16[127,1024]{1,0:T(8,128)(2,1)S(1)}, bf16[127,1024]{1,0:T(8,128)(2,1)S(1)}, u32[]{:S(2)}, u32[]{:S(2)}) collective-permute-start(bf16[127,1024]{1,0:T(8,128)(2,1)S(1)} %slice.24), channel_id=1, source_target_pairs={{4,0},{8,4},{12,8},{16,12},{20,16},{24,20},{28,24},{32,28},{36,32}... | collective-permute-start | bytes 780296 | tf_op jit(solution)/shard_map/ppermute | solution.py:14
  17.5 4.6 %collective-permute-start.1 = (bf16[127,1024]{1,0:T(8,128)(2,1)S(1)}, bf16[127,1024]{1,0:T(8,128)(2,1)S(1)}, u32[]{:S(2)}, u32[]{:S(2)}) collective-permute-start(bf16[127,1024]{1,0:T(8,128)(2,1)S(1)} %slice.23), channel_id=1, source_target_pairs={{0,4},{4,8},{8,12},{12,16},{16,20},{20,24},{24,28},{28,32},{32,36}... | collective-permute-start | bytes 780296 | tf_op jit(solution)/shard_map/ppermute | solution.py:14
  22.0 0.0 copy-done.5
  22.0 0.1 rev.8
  22.1 0.1 pad.18.clone
  22.2 0.6 pad_convert_fusion.1.fwd_ref
  22.8 0.6 pad_convert_fusion.bwd_ref
  23.5 2.5 %collective-permute-done.2 = bf16[127,1024]{1,0:T(8,128)(2,1)S(1)} collective-permute-done((bf16[127,1024]{1,0:T(8,128)(2,1)S(1)}, bf16[127,1024]{1,0:T(8,128)(2,1)S(1)}, u32[]{:S(2)}, u32[]{:S(2)}) %collective-permute-start.2) | collective-permute-done | bytes 260128 | tf_op jit(solution)/shard_map/ppermute | solution.py:14
  26.0 1.2 %collective-permute-done.1 = bf16[127,1024]{1,0:T(8,128)(2,1)S(1)} collective-permute-done((bf16[127,1024]{1,0:T(8,128)(2,1)S(1)}, bf16[127,1024]{1,0:T(8,128)(2,1)S(1)}, u32[]{:S(2)}, u32[]{:S(2)}) %collective-permute-start.1) | collective-permute-done | bytes 260128 | tf_op jit(solution)/shard_map/ppermute | solution.py:14
  27.2 2.5 %maximum_maximum_fusion.1 = (bf16[384,1024]{1,0:T(8,128)(2,1)}, bf16[384,1024]{1,0:T(8,128)(2,1)S(1)}) fusion(bf16[127,1024]{1,0:T(8,128)(2,1)S(1)} %collective-permute-done.2, bf16[256,1024]{1,0:T(8,128)(2,1)} %get-tuple-element.13, bf16[384]{0:T(512)(128)(2,1)S(1)} %pad.18.clone, bf16[256,1024]{1,0:T(8,128)(2,1)} %get-tuple-element.12, ...), kind=kLoop, calls=%fused_computation.5 | loop fusion | flops 4325376 | bytes 3142400 | tf_op jit(solution)/shard_map/concatenate | solution.py:157
  29.7 0.0 copy-start
  29.7 7.9 %rev.9.kvf_ref = bf16[384,1024]{1,0:T(8,128)(2,1)} reverse(bf16[384,1024]{1,0:T(8,128)(2,1)S(1)} %get-tuple-element.24.kv_ref), dimensions={0} | reverse | bytes 1572864 | tf_op jit(solution)/shard_map/jit(_flip)/rev | solution.py:172
  37.5 0.0 copy-start.1
  37.5 0.0 copy-start.3
  37.5 0.0 copy-start.4
  37.5 0.0 copy-done
  37.6 11.0 %shard_map.68 = (f32[256,1024]{1,0:T(8,128)}, f32[256,1024]{1,0:T(8,128)}, f32[64,128]{1,0:T(8,128)}) custom-call(f32[64,256]{1,0:T(8,128)} %pad_convert_fusion.1.fwd_ref, f32[64,256]{1,0:T(8,128)} %pad_convert_fusion.bwd_ref, bf16[384,1024]{1,0:T(8,128)(2,1)} %copy-done, bf16[384,1024]{1,0:T(8,128)(2,1)} %rev.9.kvf_ref, ...), custom_call_target="tpu_custom_call" | custom-call | tf_op jit(solution)/shard_map/pallas_call | solution.py:162
  48.5 0.0 copy-done.1
  48.5 0.0 copy-done.3
  48.5 0.0 copy-done.4
  48.5 2.0 %fusion.1 = (bf16[1,256,1024]{2,1,0:T(8,128)(2,1)S(1)}, bf16[1,256,1024]{2,1,0:T(8,128)(2,1)S(1)}, bf16[1,256,1024]{2,1,0:T(8,128)(2,1)S(1)}) fusion(f32[256,1024]{1,0:T(8,128)} %get-tuple-element.15, bf16[256,1024]{1,0:T(8,128)(2,1)S(1)} %copy-done.4, bf16[256,1024]{1,0:T(8,128)(2,1)S(1)} %copy-done.3, f32[256,1024]{1,0:T(8,128)} %get-tuple-element.14, ...), kind=kLoop, calls=%fused_computation.8 | loop fusion | flops 2359296 | bytes 5242880 | tf_op jit(solution)/shard_map/stack | solution.py:204
  50.6 1.3 %collective-permute-start.3 = (bf16[3,6,1024]{2,1,0:T(8,128)(2,1)S(1)}, bf16[3,6,1024]{2,1,0:T(8,128)(2,1)S(1)}, u32[]{:S(2)}, u32[]{:S(2)}) collective-permute-start(bf16[3,6,1024]{2,1,0:T(8,128)(2,1)S(1)} %pad_maximum_fusion.3), channel_id=1, source_target_pairs={{4,0},{8,4},{12,8},{16,12},{20,16},{24,20},{28,24},{32,28},{36,32}... | collective-permute-start | bytes 110600 | tf_op jit(solution)/shard_map/ppermute | solution.py:14
  51.9 5.2 %collective-permute-done.3 = bf16[3,6,1024]{2,1,0:T(8,128)(2,1)S(1)} collective-permute-done((bf16[3,6,1024]{2,1,0:T(8,128)(2,1)S(1)}, bf16[3,6,1024]{2,1,0:T(8,128)(2,1)S(1)}, u32[]{:S(2)}, u32[]{:S(2)}) %collective-permute-start.3) | collective-permute-done | bytes 36896 | tf_op jit(solution)/shard_map/ppermute | solution.py:14
  57.0 1.3 %pad_maximum_fusion.grads_ref = bf16[3,262,1024]{2,1,0:T(8,128)(2,1)} fusion(bf16[3,6,1024]{2,1,0:T(8,128)(2,1)S(1)} %collective-permute-done.3, bf16[1,256,1024]{2,1,0:T(8,128)(2,1)S(1)} %get-tuple-element.22, bf16[1,256,1024]{2,1,0:T(8,128)(2,1)S(1)} %get-tuple-element.21, bf16[1,256,1024]{2,1,0:T(8,128)(2,1)S(1)} %get-tuple-element.25), kind=kLoop, calls=%fused_computation | loop fusion | flops 6438912 | bytes 3219456 | tf_op jit(solution)/shard_map/concatenate | solution.py:206
  58.4 0.0 copy-start.6
  58.4 7.1 %shard_map.69 = (bf16[256,1024]{1,0:T(8,128)(2,1)}, f32[21,1024]{1,0:T(8,128)}) custom-call(f32[21,1024]{1,0:T(8,128)} %reshape_reshape.3.taps_ref, bf16[262,1024]{1,0:T(8,128)(2,1)} %pad_maximum_fusion.1.sig_ref, bf16[3,262,1024]{2,1,0:T(8,128)(2,1)} %pad_maximum_fusion.grads_ref), custom_call_target="tpu_custom_call" | custom-call | tf_op jit(solution)/shard_map/pallas_call | solution.py:90
  65.5 0.0 copy-start.7
  65.5 1.2 %reshape.21 = f32[21,64,16]{2,1,0:T(8,128)S(1)} reshape(f32[21,1024]{1,0:T(8,128)} %get-tuple-element.19) | data formatting | bytes 172032 | tf_op jit(solution)/shard_map/reshape | solution.py:208
  66.7 0.3 reduce_sum.18
  66.9 0.1 copy.7
  67.0 0.0 copy-done.6
  67.0 0.1 pad_maximum_fusion.2
  67.1 0.7 reshape.22
  67.8 18.7 %all-to-all-start = ((f32[32,149,2]{1,2,0:T(2,128)}), f32[32,149,2]{1,2,0:T(2,128)S(1)}, u32[]{:S(2)}, u32[]{:S(2)}) async-start(f32[32,149,2]{1,2,0:T(2,128)} %bitcast.11), calls=%async_computation | async-start | bytes 131072 | tf_op jit(solution)/shard_map/all_to_all | solution.py:22
  86.5 0.0 copy-done.7
  86.5 1.3 %collective-permute-start.4 = (bf16[1,256,1024]{2,1,0:T(8,128)(2,1)S(1)}, bf16[1,256,1024]{2,1,0:T(8,128)(2,1)S(1)}, u32[]{:S(2)}, u32[]{:S(2)}) collective-permute-start(bf16[1,256,1024]{2,1,0:T(8,128)(2,1)S(1)} %bitcast.33), channel_id=1, source_target_pairs={{128,0},{256,128},{384,256},{129,1},{257,129},{385,257},{130,2},{2... | collective-permute-start | bytes 1572872 | tf_op jit(solution)/shard_map/ppermute | solution.py:14
  87.8 12.8 %all-to-all-done = f32[32,149,2]{1,2,0:T(2,128)S(1)} async-done(((f32[32,149,2]{1,2,0:T(2,128)}), f32[32,149,2]{1,2,0:T(2,128)S(1)}, u32[]{:S(2)}, u32[]{:S(2)}) %all-to-all-start) | async-done | bytes 38176 | tf_op jit(solution)/shard_map/all_to_all | solution.py:22
  100.7 0.6 slice_bitcast_fusion.1
  101.4 0.6 slice_bitcast_fusion.2
  101.9 0.0 collective-permute-done.4
  101.9 0.8 copy.9
  (2 shorter events, 0.1 us)
Async XLA Ops:
  0.6 6.6 %copy-start.2 = (bf16[1,256,1024]{2,1,0:T(8,128)(2,1)S(1)}, bf16[1,256,1024]{2,1,0:T(8,128)(2,1)}, u32[]{:S(2)}) copy-start(bf16[1,256,1024]{2,1,0:T(8,128)(2,1)} %param.4) | copy-start | bytes 1572868
  1.4 5.8 %collective-permute-start = (bf16[6,1024]{1,0:T(8,128)(2,1)S(1)}, bf16[6,1024]{1,0:T(8,128)(2,1)S(1)}, u32[]{:S(2)}, u32[]{:S(2)}) collective-permute-start(bf16[6,1024]{1,0:T(8,128)(2,1)S(1)} %slice_bitcast_fusion), channel_id=1, source_target_pairs={{0,4},{4,8},{8,12},{12,16},{16,20},{20,24},{24,28},{28,32},{32,36}... | collective-permute-start | bytes 36872 | tf_op jit(solution)/shard_map/ppermute | solution.py:14
  7.2 14.8 %copy-start.5 = (bf16[1,128,64]{1,2,0:T(8,128)(2,1)S(1)}, bf16[1,128,64]{1,2,0:T(8,128)(2,1)}, u32[]{:S(2)}) copy-start(bf16[1,128,64]{1,2,0:T(8,128)(2,1)} %param.7) | copy-start | bytes 49156
  16.2 9.8 %collective-permute-start.2 = (bf16[127,1024]{1,0:T(8,128)(2,1)S(1)}, bf16[127,1024]{1,0:T(8,128)(2,1)S(1)}, u32[]{:S(2)}, u32[]{:S(2)}) collective-permute-start(bf16[127,1024]{1,0:T(8,128)(2,1)S(1)} %slice.24), channel_id=1, source_target_pairs={{4,0},{8,4},{12,8},{16,12},{20,16},{24,20},{28,24},{32,28},{36,32}... | collective-permute-start | bytes 780296 | tf_op jit(solution)/shard_map/ppermute | solution.py:14
  17.5 9.7 %collective-permute-start.1 = (bf16[127,1024]{1,0:T(8,128)(2,1)S(1)}, bf16[127,1024]{1,0:T(8,128)(2,1)S(1)}, u32[]{:S(2)}, u32[]{:S(2)}) collective-permute-start(bf16[127,1024]{1,0:T(8,128)(2,1)S(1)} %slice.23), channel_id=1, source_target_pairs={{0,4},{4,8},{8,12},{12,16},{16,20},{20,24},{24,28},{28,32},{32,36}... | collective-permute-start | bytes 780296 | tf_op jit(solution)/shard_map/ppermute | solution.py:14
  29.7 7.9 %copy-start = (bf16[384,1024]{1,0:T(8,128)(2,1)}, bf16[384,1024]{1,0:T(8,128)(2,1)S(1)}, u32[]{:S(2)}) copy-start(bf16[384,1024]{1,0:T(8,128)(2,1)S(1)} %get-tuple-element.24.kv_ref) | copy-start | bytes 2359300
  37.5 11.0 %copy-start.1 = (bf16[1,256,1024]{2,1,0:T(8,128)(2,1)S(1)}, bf16[1,256,1024]{2,1,0:T(8,128)(2,1)}, u32[]{:S(2)}) copy-start(bf16[1,256,1024]{2,1,0:T(8,128)(2,1)} %param.5) | copy-start | bytes 1572868
  37.5 11.0 %copy-start.3 = (bf16[256,1024]{1,0:T(8,128)(2,1)S(1)}, bf16[256,1024]{1,0:T(8,128)(2,1)}, u32[]{:S(2)}) copy-start(bf16[256,1024]{1,0:T(8,128)(2,1)} %get-tuple-element.17) | copy-start | bytes 1572868
  37.5 11.0 %copy-start.4 = (bf16[256,1024]{1,0:T(8,128)(2,1)S(1)}, bf16[256,1024]{1,0:T(8,128)(2,1)}, u32[]{:S(2)}) copy-start(bf16[256,1024]{1,0:T(8,128)(2,1)} %get-tuple-element.16) | copy-start | bytes 1572868
  50.6 6.5 %collective-permute-start.3 = (bf16[3,6,1024]{2,1,0:T(8,128)(2,1)S(1)}, bf16[3,6,1024]{2,1,0:T(8,128)(2,1)S(1)}, u32[]{:S(2)}, u32[]{:S(2)}) collective-permute-start(bf16[3,6,1024]{2,1,0:T(8,128)(2,1)S(1)} %pad_maximum_fusion.3), channel_id=1, source_target_pairs={{4,0},{8,4},{12,8},{16,12},{20,16},{24,20},{28,24},{32,28},{36,32}... | collective-permute-start | bytes 110600 | tf_op jit(solution)/shard_map/ppermute | solution.py:14
  58.4 8.7 %copy-start.6 = (f32[64,128]{1,0:T(8,128)S(1)}, f32[64,128]{1,0:T(8,128)}, u32[]{:S(2)}) copy-start(f32[64,128]{1,0:T(8,128)} %get-tuple-element.20) | copy-start | bytes 98308
  65.5 21.1 %copy-start.7 = (bf16[256,1024]{1,0:T(8,128)(2,1)S(1)}, bf16[256,1024]{1,0:T(8,128)(2,1)}, u32[]{:S(2)}) copy-start(bf16[256,1024]{1,0:T(8,128)(2,1)} %get-tuple-element.18) | copy-start | bytes 1572868
  67.8 32.9 %all-to-all-start = ((f32[32,149,2]{1,2,0:T(2,128)}), f32[32,149,2]{1,2,0:T(2,128)S(1)}, u32[]{:S(2)}, u32[]{:S(2)}) async-start(f32[32,149,2]{1,2,0:T(2,128)} %bitcast.11), calls=%async_computation | async-start | bytes 131072 | tf_op jit(solution)/shard_map/all_to_all | solution.py:22
  86.5 15.4 %collective-permute-start.4 = (bf16[1,256,1024]{2,1,0:T(8,128)(2,1)S(1)}, bf16[1,256,1024]{2,1,0:T(8,128)(2,1)S(1)}, u32[]{:S(2)}, u32[]{:S(2)}) collective-permute-start(bf16[1,256,1024]{2,1,0:T(8,128)(2,1)S(1)} %bitcast.33), channel_id=1, source_target_pairs={{128,0},{256,128},{384,256},{129,1},{257,129},{385,257},{130,2},{2... | collective-permute-start | bytes 1572872 | tf_op jit(solution)/shard_map/ppermute | solution.py:14

commit v6 on v5

--- a/solution.py
+++ b/solution.py
@@ -110,8 +110,15 @@
     )(taps, signal_pad, grads_pad)
 
 
-def medium_kernel(fwd_ref, bwd_ref, kv_ref, kvf_ref, gate_ref, mixed_ref, back_ref, taps_ref):
+def medium_kernel(fwd_ref, bwd_ref, kv_ref, gate_ref, mixed_ref, back_ref, taps_ref):
     group_block, span = fwd_ref.shape
+    padded_rows = kv_ref.shape[0]
+    row_id = lax.broadcasted_iota(jnp.int32, (padded_rows, padded_rows), 0)
+    col_id = lax.broadcasted_iota(jnp.int32, (padded_rows, padded_rows), 1)
+    reversal = (row_id + col_id == padded_rows - 1).astype(kv_ref.dtype)
+    kv_flipped = jnp.dot(reversal, kv_ref[...], preferred_element_type=jnp.float32).astype(
+        kv_ref.dtype
+    )
     rows = taps_ref.shape[1]
     block_count = mixed_ref.shape[0] // rows
     lanes = mixed_ref.shape[1]
@@ -133,7 +140,8 @@
             back = jnp.dot(bwd_band, gate_ref[pl.ds(blk * rows, span), :], preferred_element_type=jnp.float32)
             back_ref[out_rows, :] = jnp.where(in_group, back, back_ref[out_rows, :])
             gate_rows = jnp.where(in_group, gate_ref[out_rows, :], jnp.zeros((), gate_ref.dtype))
-            flipped = kvf_ref[pl.ds((block_count - 1 - blk) * rows, span), :]
+            flip_start = (block_count - 1 - blk) * rows
+            flipped = kv_flipped[flip_start : flip_start + span]
             part = lax.dot_general(
                 gate_rows, flipped, (((1,), (1,)), ((), ())), preferred_element_type=jnp.float32
             )
@@ -162,14 +170,14 @@
     mixed_out, back_out, taps_grad = pl.pallas_call(
         medium_kernel,
         grid=(chan_count // LANE_BLOCK,),
-        in_specs=[taps_spec, taps_spec, full_spec, full_spec, full_spec],
+        in_specs=[taps_spec, taps_spec, full_spec, full_spec],
         out_specs=[out_spec, out_spec, pl.BlockSpec((group_block, tap_count), lambda j: (j, 0))],
         out_shape=[
             jax.ShapeDtypeStruct((seq_rows, chan_count), jnp.float32),
             jax.ShapeDtypeStruct((seq_rows, chan_count), jnp.float32),
             jax.ShapeDtypeStruct((group_count, tap_count), jnp.float32),
         ],
-    )(fwd_taps, bwd_taps, kv_full, jnp.flip(kv_full, 0), gate_full)
+    )(fwd_taps, bwd_taps, kv_full, gate_full)
     return mixed_out, back_out, taps_grad.T
 
 

time: 104 us -> 96.8 us (0.931)
  the two profiles are of different devices: /device:TPU:24 before, /device:TPU:8 now
where the time goes in v6:
time: 96.8 us; the launch traced here: 95.8 us
  starting transfers between devices  31 us (32%)
  Pallas kernels  24.8 us (26%)
  waiting for transfers between devices  21.7 us (22%)
  local copies, waits for them, and re-layouts  8.85 us (9%)
  other arithmetic  8.71 us (9%)
    all_to_all x1, starting transfers between devices, owned_sum(): return jnp.sum(lax.all_to_all(chunks, axis, 0, 0, tiled=False), axis=0)  18.7 us
    all_to_all x1, waiting for transfers between devices, owned_sum(): return jnp.sum(lax.all_to_all(chunks, axis, 0, 0, tiled=False), axis=0)  12.8 us
    ppermute x5, starting transfers between devices, passed_along(): return lax.ppermute(block, axis, route)  12.2 us
    pallas_call x1, Pallas kernels, medium_terms(): pl.pallas_call(medium_kernel, grid=(chan_count // LANE_BLOCK,), in_specs=...  11.7 us
    ppermute x5, waiting for transfers between devices, passed_along(): return lax.ppermute(block, axis, route)  8.85 us
    pallas_call x1, Pallas kernels, short_back(): pl.pallas_call(back_kernel, grid=(chan_count // LANE_BLOCK,), in_specs=[p...  7.12 us
    pallas_call x1, Pallas kernels, short_front(): pl.pallas_call(front_kernel, grid=(chan_count // LANE_BLOCK,), in_specs=[...  5.99 us
    concatenate x1, other arithmetic, medium_terms(): gate_full = jnp.concatenate([gate_ext, zero_row], 0)  2.76 us
  transfers between devices with their start and end apart: 6, of which 4 were waited for; matrix products, arithmetic and copies ran while one was open for 5% of the time, Pallas kernels for 0%

profile of v6, /device:TPU:8, one launch (start us, length us, event | category | flops | bytes accessed | tf_op | source)
XLA Modules:
  0.0 95.8 jit_solution(18095515433287299572)
XLA Ops:
  0.6 0.0 copy-start.1
  0.6 0.8 slice_bitcast_fusion
  1.4 3.8 %collective-permute-start = (bf16[6,1024]{1,0:T(8,128)(2,1)S(1)}, bf16[6,1024]{1,0:T(8,128)(2,1)S(1)}, u32[]{:S(2)}, u32[]{:S(2)}) collective-permute-start(bf16[6,1024]{1,0:T(8,128)(2,1)S(1)} %slice_bitcast_fusion), channel_id=1, source_target_pairs={{0,4},{4,8},{8,12},{12,16},{16,20},{20,24},{24,28},{28,32},{32,36}... | collective-permute-start | bytes 36872 | tf_op jit(solution)/shard_map/ppermute | solution.py:14
  5.2 0.7 reshape.23
  5.9 0.2 broadcast_in_dim.18
  6.2 1.0 %reshape_reshape.3.taps_ref = f32[21,1024]{1,0:T(8,128)} reshape(f32[3,7,64,16]{3,2,1,0:T(8,128)S(1)} %broadcast_in_dim.18) | data formatting | bytes 172032 | tf_op jit(solution)/shard_map/reshape;reshape | solution.py:199
  7.2 0.0 collective-permute-done
  7.2 0.0 copy-done.1
  7.2 0.0 copy-start.4
  7.2 0.9 pad_maximum_fusion.1.sig_ref
  8.1 6.0 %shard_map.67 = (bf16[256,1024]{1,0:T(8,128)(2,1)}, bf16[256,1024]{1,0:T(8,128)(2,1)}, bf16[256,1024]{1,0:T(8,128)(2,1)}, bf16[256,1024]{1,0:T(8,128)(2,1)}, bf16[256,1024]{1,0:T(8,128)(2,1)}) custom-call(f32[21,1024]{1,0:T(8,128)} %reshape_reshape.3.taps_ref, bf16[262,1024]{1,0:T(8,128)(2,1)} %pad_maximum_fusion.1.sig_ref, bf16[256,1024]{1,0:T(8,128)(2,1)} %bitcast.27), custom_call_target="tpu_custom_call" | custom-call | tf_op jit(solution)/shard_map/pallas_call | solution.py:50
  14.1 1.0 %slice.23 = bf16[127,1024]{1,0:T(8,128)(2,1)S(1)} slice(bf16[256,1024]{1,0:T(8,128)(2,1)} %get-tuple-element.12), slice={[129:256], [0:1024]} | slice | bytes 520192 | tf_op jit(solution)/shard_map/slice | solution.py:203
  15.1 1.0 %slice.24 = bf16[127,1024]{1,0:T(8,128)(2,1)S(1)} slice(bf16[256,1024]{1,0:T(8,128)(2,1)} %get-tuple-element.13), slice={[0:127], [0:1024]} | slice | bytes 520192 | tf_op jit(solution)/shard_map/slice | solution.py:204
  16.1 1.3 %collective-permute-start.2 = (bf16[127,1024]{1,0:T(8,128)(2,1)S(1)}, bf16[127,1024]{1,0:T(8,128)(2,1)S(1)}, u32[]{:S(2)}, u32[]{:S(2)}) collective-permute-start(bf16[127,1024]{1,0:T(8,128)(2,1)S(1)} %slice.24), channel_id=1, source_target_pairs={{4,0},{8,4},{12,8},{16,12},{20,16},{24,20},{28,24},{32,28},{36,32}... | collective-permute-start | bytes 780296 | tf_op jit(solution)/shard_map/ppermute | solution.py:14
  17.4 4.6 %collective-permute-start.1 = (bf16[127,1024]{1,0:T(8,128)(2,1)S(1)}, bf16[127,1024]{1,0:T(8,128)(2,1)S(1)}, u32[]{:S(2)}, u32[]{:S(2)}) collective-permute-start(bf16[127,1024]{1,0:T(8,128)(2,1)S(1)} %slice.23), channel_id=1, source_target_pairs={{0,4},{4,8},{8,12},{12,16},{16,20},{20,24},{24,28},{28,32},{32,36}... | collective-permute-start | bytes 780296 | tf_op jit(solution)/shard_map/ppermute | solution.py:14
  22.0 0.0 copy-done.4
  22.0 0.1 rev.4
  22.1 0.1 pad.18.clone
  22.2 0.6 pad_convert_fusion.1.fwd_ref
  22.8 0.6 pad_convert_fusion.bwd_ref
  23.4 2.5 %collective-permute-done.2 = bf16[127,1024]{1,0:T(8,128)(2,1)S(1)} collective-permute-done((bf16[127,1024]{1,0:T(8,128)(2,1)S(1)}, bf16[127,1024]{1,0:T(8,128)(2,1)S(1)}, u32[]{:S(2)}, u32[]{:S(2)}) %collective-permute-start.2) | collective-permute-done | bytes 260128 | tf_op jit(solution)/shard_map/ppermute | solution.py:14
  26.0 1.2 %collective-permute-done.1 = bf16[127,1024]{1,0:T(8,128)(2,1)S(1)} collective-permute-done((bf16[127,1024]{1,0:T(8,128)(2,1)S(1)}, bf16[127,1024]{1,0:T(8,128)(2,1)S(1)}, u32[]{:S(2)}, u32[]{:S(2)}) %collective-permute-start.1) | collective-permute-done | bytes 260128 | tf_op jit(solution)/shard_map/ppermute | solution.py:14
  27.1 2.8 %maximum_maximum_fusion.1 = (bf16[384,1024]{1,0:T(8,128)(2,1)}, bf16[384,1024]{1,0:T(8,128)(2,1)}) fusion(bf16[127,1024]{1,0:T(8,128)(2,1)S(1)} %collective-permute-done.2, bf16[256,1024]{1,0:T(8,128)(2,1)} %get-tuple-element.13, bf16[384]{0:T(512)(128)(2,1)S(1)} %pad.18.clone, bf16[256,1024]{1,0:T(8,128)(2,1)} %get-tuple-element.12, ...), kind=kLoop, calls=%fused_computation.5 | loop fusion | flops 4325376 | bytes 3142400 | tf_op jit(solution)/shard_map/concatenate | solution.py:165
  29.9 0.0 copy-start
  29.9 0.0 copy-start.2
  29.9 0.0 copy-start.3
  29.9 11.7 %shard_map.68 = (f32[256,1024]{1,0:T(8,128)}, f32[256,1024]{1,0:T(8,128)}, f32[64,128]{1,0:T(8,128)}) custom-call(f32[64,256]{1,0:T(8,128)} %pad_convert_fusion.1.fwd_ref, f32[64,256]{1,0:T(8,128)} %pad_convert_fusion.bwd_ref, bf16[384,1024]{1,0:T(8,128)(2,1)} %get-tuple-element.24.kv_ref, bf16[384,1024]{1,0:T(8,128)(2,1)} %get-tuple-element.23.gate_ref), custom_call_target="tpu_custom_call" | custom-call | tf_op jit(solution)/shard_map/pallas_call | solution.py:170
  41.6 0.0 copy-done
  41.6 0.0 copy-done.2
  41.6 0.0 copy-done.3
  41.6 2.0 %fusion.1 = (bf16[1,256,1024]{2,1,0:T(8,128)(2,1)S(1)}, bf16[1,256,1024]{2,1,0:T(8,128)(2,1)S(1)}, bf16[1,256,1024]{2,1,0:T(8,128)(2,1)S(1)}) fusion(f32[256,1024]{1,0:T(8,128)} %get-tuple-element.15, bf16[256,1024]{1,0:T(8,128)(2,1)S(1)} %copy-done.3, bf16[256,1024]{1,0:T(8,128)(2,1)S(1)} %copy-done.2, f32[256,1024]{1,0:T(8,128)} %get-tuple-element.14, ...), kind=kLoop, calls=%fused_computation.8 | loop fusion | flops 2359296 | bytes 5242880 | tf_op jit(solution)/shard_map/stack | solution.py:212
  43.7 1.3 %collective-permute-start.3 = (bf16[3,6,1024]{2,1,0:T(8,128)(2,1)S(1)}, bf16[3,6,1024]{2,1,0:T(8,128)(2,1)S(1)}, u32[]{:S(2)}, u32[]{:S(2)}) collective-permute-start(bf16[3,6,1024]{2,1,0:T(8,128)(2,1)S(1)} %pad_maximum_fusion.3), channel_id=1, source_target_pairs={{4,0},{8,4},{12,8},{16,12},{20,16},{24,20},{28,24},{32,28},{36,32}... | collective-permute-start | bytes 110600 | tf_op jit(solution)/shard_map/ppermute | solution.py:14
  45.0 5.2 %collective-permute-done.3 = bf16[3,6,1024]{2,1,0:T(8,128)(2,1)S(1)} collective-permute-done((bf16[3,6,1024]{2,1,0:T(8,128)(2,1)S(1)}, bf16[3,6,1024]{2,1,0:T(8,128)(2,1)S(1)}, u32[]{:S(2)}, u32[]{:S(2)}) %collective-permute-start.3) | collective-permute-done | bytes 36896 | tf_op jit(solution)/shard_map/ppermute | solution.py:14
  50.1 1.3 %pad_maximum_fusion.grads_ref = bf16[3,262,1024]{2,1,0:T(8,128)(2,1)} fusion(bf16[3,6,1024]{2,1,0:T(8,128)(2,1)S(1)} %collective-permute-done.3, bf16[1,256,1024]{2,1,0:T(8,128)(2,1)S(1)} %get-tuple-element.22, bf16[1,256,1024]{2,1,0:T(8,128)(2,1)S(1)} %get-tuple-element.21, bf16[1,256,1024]{2,1,0:T(8,128)(2,1)S(1)} %get-tuple-element.25), kind=kLoop, calls=%fused_computation | loop fusion | flops 6438912 | bytes 3219456 | tf_op jit(solution)/shard_map/concatenate | solution.py:214
  51.5 0.0 copy-start.5
  51.5 7.1 %shard_map.69 = (bf16[256,1024]{1,0:T(8,128)(2,1)}, f32[21,1024]{1,0:T(8,128)}) custom-call(f32[21,1024]{1,0:T(8,128)} %reshape_reshape.3.taps_ref, bf16[262,1024]{1,0:T(8,128)(2,1)} %pad_maximum_fusion.1.sig_ref, bf16[3,262,1024]{2,1,0:T(8,128)(2,1)} %pad_maximum_fusion.grads_ref), custom_call_target="tpu_custom_call" | custom-call | tf_op jit(solution)/shard_map/pallas_call | solution.py:90
  58.6 0.0 copy-start.6
  58.6 1.2 %reshape.21 = f32[21,64,16]{2,1,0:T(8,128)S(1)} reshape(f32[21,1024]{1,0:T(8,128)} %get-tuple-element.19) | data formatting | bytes 172032 | tf_op jit(solution)/shard_map/reshape | solution.py:216
  59.8 0.3 reduce_sum.18
  60.0 0.1 copy.7
  60.1 0.0 copy-done.5
  60.1 0.1 pad_maximum_fusion.2
  60.2 0.7 reshape.22
  60.9 18.7 %all-to-all-start = ((f32[32,149,2]{1,2,0:T(2,128)}), f32[32,149,2]{1,2,0:T(2,128)S(1)}, u32[]{:S(2)}, u32[]{:S(2)}) async-start(f32[32,149,2]{1,2,0:T(2,128)} %bitcast.11), calls=%async_computation | async-start | bytes 131072 | tf_op jit(solution)/shard_map/all_to_all | solution.py:22
  79.6 0.0 copy-done.6
  79.7 1.3 %collective-permute-start.4 = (bf16[1,256,1024]{2,1,0:T(8,128)(2,1)S(1)}, bf16[1,256,1024]{2,1,0:T(8,128)(2,1)S(1)}, u32[]{:S(2)}, u32[]{:S(2)}) collective-permute-start(bf16[1,256,1024]{2,1,0:T(8,128)(2,1)S(1)} %bitcast.33), channel_id=1, source_target_pairs={{128,0},{256,128},{384,256},{129,1},{257,129},{385,257},{130,2},{2... | collective-permute-start | bytes 1572872 | tf_op jit(solution)/shard_map/ppermute | solution.py:14
  81.0 12.8 %all-to-all-done = f32[32,149,2]{1,2,0:T(2,128)S(1)} async-done(((f32[32,149,2]{1,2,0:T(2,128)}), f32[32,149,2]{1,2,0:T(2,128)S(1)}, u32[]{:S(2)}, u32[]{:S(2)}) %all-to-all-start) | async-done | bytes 38176 | tf_op jit(solution)/shard_map/all_to_all | solution.py:22
  93.8 0.6 slice_bitcast_fusion.1
  94.5 0.6 slice_bitcast_fusion.2
  95.0 0.0 collective-permute-done.4
  95.0 0.8 copy.9
  (2 shorter events, 0.1 us)
Async XLA Ops:
  0.6 6.6 %copy-start.1 = (bf16[1,256,1024]{2,1,0:T(8,128)(2,1)S(1)}, bf16[1,256,1024]{2,1,0:T(8,128)(2,1)}, u32[]{:S(2)}) copy-start(bf16[1,256,1024]{2,1,0:T(8,128)(2,1)} %param.4) | copy-start | bytes 1572868
  1.4 5.8 %collective-permute-start = (bf16[6,1024]{1,0:T(8,128)(2,1)S(1)}, bf16[6,1024]{1,0:T(8,128)(2,1)S(1)}, u32[]{:S(2)}, u32[]{:S(2)}) collective-permute-start(bf16[6,1024]{1,0:T(8,128)(2,1)S(1)} %slice_bitcast_fusion), channel_id=1, source_target_pairs={{0,4},{4,8},{8,12},{12,16},{16,20},{20,24},{24,28},{28,32},{32,36}... | collective-permute-start | bytes 36872 | tf_op jit(solution)/shard_map/ppermute | solution.py:14
  7.2 14.8 %copy-start.4 = (bf16[1,128,64]{1,2,0:T(8,128)(2,1)S(1)}, bf16[1,128,64]{1,2,0:T(8,128)(2,1)}, u32[]{:S(2)}) copy-start(bf16[1,128,64]{1,2,0:T(8,128)(2,1)} %param.7) | copy-start | bytes 49156
  16.1 9.8 %collective-permute-start.2 = (bf16[127,1024]{1,0:T(8,128)(2,1)S(1)}, bf16[127,1024]{1,0:T(8,128)(2,1)S(1)}, u32[]{:S(2)}, u32[]{:S(2)}) collective-permute-start(bf16[127,1024]{1,0:T(8,128)(2,1)S(1)} %slice.24), channel_id=1, source_target_pairs={{4,0},{8,4},{12,8},{16,12},{20,16},{24,20},{28,24},{32,28},{36,32}... | collective-permute-start | bytes 780296 | tf_op jit(solution)/shard_map/ppermute | solution.py:14
  17.4 9.7 %collective-permute-start.1 = (bf16[127,1024]{1,0:T(8,128)(2,1)S(1)}, bf16[127,1024]{1,0:T(8,128)(2,1)S(1)}, u32[]{:S(2)}, u32[]{:S(2)}) collective-permute-start(bf16[127,1024]{1,0:T(8,128)(2,1)S(1)} %slice.23), channel_id=1, source_target_pairs={{0,4},{4,8},{8,12},{12,16},{16,20},{20,24},{24,28},{28,32},{32,36}... | collective-permute-start | bytes 780296 | tf_op jit(solution)/shard_map/ppermute | solution.py:14
  29.9 11.7 %copy-start = (bf16[1,256,1024]{2,1,0:T(8,128)(2,1)S(1)}, bf16[1,256,1024]{2,1,0:T(8,128)(2,1)}, u32[]{:S(2)}) copy-start(bf16[1,256,1024]{2,1,0:T(8,128)(2,1)} %param.5) | copy-start | bytes 1572868
  29.9 11.7 %copy-start.2 = (bf16[256,1024]{1,0:T(8,128)(2,1)S(1)}, bf16[256,1024]{1,0:T(8,128)(2,1)}, u32[]{:S(2)}) copy-start(bf16[256,1024]{1,0:T(8,128)(2,1)} %get-tuple-element.17) | copy-start | bytes 1572868
  29.9 11.7 %copy-start.3 = (bf16[256,1024]{1,0:T(8,128)(2,1)S(1)}, bf16[256,1024]{1,0:T(8,128)(2,1)}, u32[]{:S(2)}) copy-start(bf16[256,1024]{1,0:T(8,128)(2,1)} %get-tuple-element.16) | copy-start | bytes 1572868
  43.7 6.5 %collective-permute-start.3 = (bf16[3,6,1024]{2,1,0:T(8,128)(2,1)S(1)}, bf16[3,6,1024]{2,1,0:T(8,128)(2,1)S(1)}, u32[]{:S(2)}, u32[]{:S(2)}) collective-permute-start(bf16[3,6,1024]{2,1,0:T(8,128)(2,1)S(1)} %pad_maximum_fusion.3), channel_id=1, source_target_pairs={{4,0},{8,4},{12,8},{16,12},{20,16},{24,20},{28,24},{32,28},{36,32}... | collective-permute-start | bytes 110600 | tf_op jit(solution)/shard_map/ppermute | solution.py:14
  51.5 8.7 %copy-start.5 = (f32[64,128]{1,0:T(8,128)S(1)}, f32[64,128]{1,0:T(8,128)}, u32[]{:S(2)}) copy-start(f32[64,128]{1,0:T(8,128)} %get-tuple-element.20) | copy-start | bytes 98308
  58.6 21.1 %copy-start.6 = (bf16[256,1024]{1,0:T(8,128)(2,1)S(1)}, bf16[256,1024]{1,0:T(8,128)(2,1)}, u32[]{:S(2)}) copy-start(bf16[256,1024]{1,0:T(8,128)(2,1)} %get-tuple-element.18) | copy-start | bytes 1572868
  60.9 32.9 %all-to-all-start = ((f32[32,149,2]{1,2,0:T(2,128)}), f32[32,149,2]{1,2,0:T(2,128)S(1)}, u32[]{:S(2)}, u32[]{:S(2)}) async-start(f32[32,149,2]{1,2,0:T(2,128)} %bitcast.11), calls=%async_computation | async-start | bytes 131072 | tf_op jit(solution)/shard_map/all_to_all | solution.py:22
  79.7 15.4 %collective-permute-start.4 = (bf16[1,256,1024]{2,1,0:T(8,128)(2,1)S(1)}, bf16[1,256,1024]{2,1,0:T(8,128)(2,1)S(1)}, u32[]{:S(2)}, u32[]{:S(2)}) collective-permute-start(bf16[1,256,1024]{2,1,0:T(8,128)(2,1)S(1)} %bitcast.33), channel_id=1, source_target_pairs={{128,0},{256,128},{384,256},{129,1},{257,129},{385,257},{130,2},{2... | collective-permute-start | bytes 1572872 | tf_op jit(solution)/shard_map/ppermute | solution.py:14

commit v7 on v5

v7 whole, which is shorter than its diff:
```python
import jax
import jax.numpy as jnp
from jax import lax
from jax.experimental import pallas as pl
from jax.experimental.pallas import tpu as pltpu
from jax.sharding import PartitionSpec as P

LANE_BLOCK = 128


def passed_along(block, axis, distance):
    devices = range(lax.axis_size(axis))
    route = [(i - distance, i) for i in devices if i - distance in devices]
    return lax.ppermute(block, axis, route)


def owned_sum(partial_terms, axis):
    axis_len = lax.axis_size(axis)
    row_count, col_count = partial_terms.shape
    width = col_count // axis_len
    chunks = partial_terms.reshape(row_count, axis_len, width).transpose(1, 0, 2)
    return jnp.sum(lax.all_to_all(chunks, axis, 0, 0, tiled=False), axis=0)


def front_kernel(taps_ref, sig_ref, gy_ref, q_ref, k_ref, v_ref, kv_ref, gate_ref, xs_ref):
    rows = q_ref.shape[0]
    rim = sig_ref.shape[0] - rows
    lags = rim + 1
    xs_ref[pl.ds(0, rows + rim), :] = sig_ref[...].astype(jnp.float32)
    for branch, out_ref in enumerate((q_ref, k_ref, v_ref)):
        acc = None
        for offset in range(lags):
            term = taps_ref[pl.ds(branch * lags + offset, 1), :] * xs_ref[pl.ds(rim - offset, rows), :]
            acc = term if acc is None else acc + term
        out_ref[...] = acc.astype(jnp.bfloat16)
    kv_ref[...] = (k_ref[...].astype(jnp.float32) * v_ref[...].astype(jnp.float32)).astype(
        jnp.bfloat16
    )
    gate_ref[...] = (gy_ref[...].astype(jnp.float32) * q_ref[...].astype(jnp.float32)).astype(
        jnp.bfloat16
    )


def short_front(taps, signal_pad, grad_out):
    padded_rows, chan_count = signal_pad.shape
    rows = grad_out.shape[0]
    tap_rows = taps.shape[0]
    row_spec = pl.BlockSpec((rows, LANE_BLOCK), lambda j: (0, j))
    shape = jax.ShapeDtypeStruct((rows, chan_count), jnp.bfloat16)
    return pl.pallas_call(
        front_kernel,
        grid=(chan_count // LANE_BLOCK,),
        in_specs=[
            pl.BlockSpec((tap_rows, LANE_BLOCK), lambda j: (0, j)),
            pl.BlockSpec((padded_rows, LANE_BLOCK), lambda j: (0, j)),
            row_spec,
        ],
        out_specs=[row_spec] * 5,
        out_shape=[shape] * 5,
        scratch_shapes=[pltpu.VMEM((padded_rows + 8, LANE_BLOCK), jnp.float32)],
    )(taps, signal_pad, grad_out)


def input_grad_kernel(taps_ref, grads_ref, rim_ref, ig_ref, gs_ref):
    branches, rows, lanes = grads_ref.shape
    rim = rim_ref.shape[1]
    lags = rim + 1
    for branch in range(branches):
        gs_ref[branch, pl.ds(0, rows), :] = grads_ref[branch].astype(jnp.float32)
        gs_ref[branch, pl.ds(rows, rim), :] = rim_ref[branch].astype(jnp.float32)
    acc = None
    for branch in range(branches):
        for offset in range(lags):
            term = taps_ref[pl.ds(branch * lags + offset, 1), :] * gs_ref[branch, pl.ds(offset, rows), :]
            acc = term if acc is None else acc + term
    ig_ref[...] = acc.astype(jnp.bfloat16)


def short_partial_kernel(sig_ref, grads_ref, sp_ref, xs_ref):
    branches, rows, lanes = grads_ref.shape
    rim = sig_ref.shape[0] - rows
    lags = rim + 1
    xs_ref[pl.ds(0, rows + rim), :] = sig_ref[...].astype(jnp.float32)
    for branch in range(branches):
        grads_f = grads_ref[branch].astype(jnp.float32)
        for offset in range(lags):
            prod = grads_f * xs_ref[pl.ds(rim - offset, rows), :]
            sp_ref[pl.ds(branch * lags + offset, 1), :] = jnp.sum(prod, axis=0, keepdims=True)


def short_partials(signal_pad, feature_grads):
    padded_rows, chan_count = signal_pad.shape
    branches, rows, _ = feature_grads.shape
    tap_rows = branches * (padded_rows - rows + 1)
    return pl.pallas_call(
        short_partial_kernel,
        grid=(chan_count // LANE_BLOCK,),
        in_specs=[
            pl.BlockSpec((padded_rows, LANE_BLOCK), lambda j: (0, j)),
            pl.BlockSpec((branches, rows, LANE_BLOCK), lambda j: (0, 0, j)),
        ],
        out_specs=pl.BlockSpec((tap_rows, LANE_BLOCK), lambda j: (0, j)),
        out_shape=jax.ShapeDtypeStruct((tap_rows, chan_count), jnp.float32),
        scratch_shapes=[pltpu.VMEM((padded_rows + 8, LANE_BLOCK), jnp.float32)],
    )(signal_pad, feature_grads)


def input_grads(taps, feature_grads, feature_rim):
    branches, rows, chan_count = feature_grads.shape
    rim = feature_rim.shape[1]
    return pl.pallas_call(
        input_grad_kernel,
        grid=(chan_count // LANE_BLOCK,),
        in_specs=[
            pl.BlockSpec((taps.shape[0], LANE_BLOCK), lambda j: (0, j)),
            pl.BlockSpec((branches, rows, LANE_BLOCK), lambda j: (0, 0, j)),
            pl.BlockSpec((branches, rim, LANE_BLOCK), lambda j: (0, 0, j)),
        ],
        out_specs=pl.BlockSpec((rows, LANE_BLOCK), lambda j: (0, j)),
        out_shape=jax.ShapeDtypeStruct((rows, chan_count), jnp.bfloat16),
        scratch_shapes=[pltpu.VMEM((branches, rows + rim + 2, LANE_BLOCK), jnp.float32)],
    )(taps, feature_grads, feature_rim)


def medium_kernel(
    fwd_ref, bwd_ref, kv_rim_ref, prod_ref, gate_ref, gate_rim_ref, gy_ref, key_ref, value_ref,
    grads_ref, taps_ref, kv_s, gate_s, mixed_s, back_s,
):
    group_block, span = fwd_ref.shape
    rows = taps_ref.shape[1]
    seq_rows, lanes = gy_ref.shape
    block_count = seq_rows // rows
    rim = kv_rim_ref.shape[0]
    padded_rows = kv_s.shape[0]
    kv_s[pl.ds(0, rim), :] = kv_rim_ref[...].astype(jnp.float32)
    kv_s[pl.ds(rim, seq_rows), :] = prod_ref[...].astype(jnp.float32)
    kv_s[pl.ds(rim + seq_rows, padded_rows - rim - seq_rows), :] = jnp.zeros(
        (padded_rows - rim - seq_rows, lanes), jnp.float32
    )
    gate_s[pl.ds(0, seq_rows), :] = gate_ref[...].astype(jnp.float32)
    gate_s[pl.ds(seq_rows, rim), :] = gate_rim_ref[...].astype(jnp.float32)
    gate_s[pl.ds(rim + seq_rows, padded_rows - rim - seq_rows), :] = jnp.zeros(
        (padded_rows - rim - seq_rows, lanes), jnp.float32
    )
    kv_all = kv_s[...].astype(jnp.bfloat16)
    gate_all = gate_s[...].astype(jnp.bfloat16)
    row_id = lax.broadcasted_iota(jnp.int32, (padded_rows, padded_rows), 0)
    col_id = lax.broadcasted_iota(jnp.int32, (padded_rows, padded_rows), 1)
    reversal = (row_id + col_id == padded_rows - 1).astype(jnp.bfloat16)
    kv_flipped = jnp.dot(reversal, kv_all, preferred_element_type=jnp.float32).astype(jnp.bfloat16)
    group_width = lanes // group_block
    lane_group = lax.broadcasted_iota(jnp.int32, (1, lanes), 1) // group_width
    mixed_s[...] = jnp.zeros(mixed_s.shape, mixed_s.dtype)
    back_s[...] = jnp.zeros(back_s.shape, back_s.dtype)
    for group in range(group_block):
        in_group = lane_group == group
        fwd = jnp.broadcast_to(fwd_ref[pl.ds(group, 1), :], (rows, span))
        bwd = jnp.broadcast_to(bwd_ref[pl.ds(group, 1), :], (rows, span))
        fwd_band = pltpu.roll(fwd, 0, 1, stride=1, stride_axis=0).astype(jnp.bfloat16)
        bwd_band = pltpu.roll(bwd, 0, 1, stride=1, stride_axis=0).astype(jnp.bfloat16)
        cross = None
        for blk in range(block_count):
            start = blk * rows
            out_rows = pl.ds(start, rows)
            mixed = jnp.dot(fwd_band, kv_all[start : start + span], preferred_element_type=jnp.float32)
            mixed_s[out_rows, :] = jnp.where(in_group, mixed, mixed_s[out_rows, :])
            back = jnp.dot(bwd_band, gate_all[start : start + span], preferred_element_type=jnp.float32)
            back_s[out_rows, :] = jnp.where(in_group, back, back_s[out_rows, :])
            gate_rows = jnp.where(in_group, gate_all[start : start + rows], jnp.zeros((), jnp.bfloat16))
            flip_start = (block_count - 1 - blk) * rows
            part = lax.dot_general(
                gate_rows,
                kv_flipped[flip_start : flip_start + span],
                (((1,), (1,)), ((), ())),
                preferred_element_type=jnp.float32,
            )
            cross = part if cross is None else cross + part
        rolled = pltpu.roll(cross, 0, 1, stride=1, stride_axis=0)
        taps_ref[pl.ds(group, 1), :] = jnp.sum(rolled[:, span - rows :], axis=0, keepdims=True)
    back_all = back_s[...]
    grads_ref[0] = (gy_ref[...].astype(jnp.float32) * mixed_s[...]).astype(jnp.bfloat16)
    grads_ref[1] = (back_all * value_ref[...].astype(jnp.float32)).astype(jnp.bfloat16)
    grads_ref[2] = (back_all * key_ref[...].astype(jnp.float32)).astype(jnp.bfloat16)


def medium_terms(medium_taps, kv_rim, products, gate_grad, gate_rim, grad_out, key_in, value_in):
    tap_count, group_count = medium_taps.shape
    seq_rows, chan_count = products.shape
    group_width = chan_count // group_count
    row_block = tap_count
    span = row_block + tap_count
    padded_rows = seq_rows + tap_count
    group_block = LANE_BLOCK // group_width
    zero_taps = jnp.zeros((group_count, span - tap_count), jnp.float32)
    fwd_taps = jnp.concatenate([jnp.flip(medium_taps, 0).T.astype(jnp.float32), zero_taps], 1)
    bwd_taps = jnp.concatenate([medium_taps.T.astype(jnp.float32), zero_taps], 1)
    taps_spec = pl.BlockSpec((group_block, span), lambda j: (j, 0))
    rim_spec = pl.BlockSpec((kv_rim.shape[0], LANE_BLOCK), lambda j: (0, j))
    row_spec = pl.BlockSpec((seq_rows, LANE_BLOCK), lambda j: (0, j))
    grads, taps_grad = pl.pallas_call(
        medium_kernel,
        grid=(chan_count // LANE_BLOCK,),
        in_specs=[taps_spec, taps_spec, rim_spec, row_spec, row_spec, rim_spec, row_spec, row_spec, row_spec],
        out_specs=[
            pl.BlockSpec((3, seq_rows, LANE_BLOCK), lambda j: (0, 0, j)),
            pl.BlockSpec((group_block, tap_count), lambda j: (j, 0)),
        ],
        out_shape=[
            jax.ShapeDtypeStruct((3, seq_rows, chan_count), jnp.bfloat16),
            jax.ShapeDtypeStruct((group_count, tap_count), jnp.float32),
        ],
        scratch_shapes=[
            pltpu.VMEM((padded_rows, LANE_BLOCK), jnp.float32),
            pltpu.VMEM((padded_rows, LANE_BLOCK), jnp.float32),
            pltpu.VMEM((seq_rows, LANE_BLOCK), jnp.float32),
            pltpu.VMEM((seq_rows, LANE_BLOCK), jnp.float32),
        ],
    )(fwd_taps, bwd_taps, kv_rim, products, gate_grad, gate_rim, grad_out, key_in, value_in)
    return grads, taps_grad.T


def per_device(inputs, upstream, short_filter, medium_filter):
    signal = inputs[0]
    grad_out = upstream[0]
    seq_rows, chan_count = signal.shape
    tap_count = medium_filter.shape[1]
    group_count = medium_filter.shape[2]
    lag_count = short_filter.shape[1] // 3
    group_width = chan_count // group_count
    short_rim = lag_count - 1
    medium_rim = tap_count - 1
    chan_short = jnp.broadcast_to(
        short_filter[0].astype(jnp.float32).reshape(3, lag_count, group_count, 1),
        (3, lag_count, group_count, group_width),
    ).reshape(3, lag_count, chan_count)
    medium_taps = medium_filter[0]
    tap_table = chan_short.reshape(3 * lag_count, chan_count)
    signal_rim = passed_along(signal[seq_rows - short_rim :], "ctx", 1)
    signal_pad = jnp.concatenate([signal_rim, signal], 0)
    query_in, key_in, value_in, products, gate_grad = short_front(tap_table, signal_pad, grad_out)
    kv_rim, gate_rim = passed_along(products[seq_rows - medium_rim :], "ctx", 1), passed_along(
        gate_grad[:medium_rim], "ctx", -1
    )
    feature_grads, taps_grad = medium_terms(
        medium_taps, kv_rim, products, gate_grad, gate_rim, grad_out, key_in, value_in
    )
    feature_rim = passed_along(feature_grads[:, :short_rim], "ctx", -1)
    short_terms = short_partials(signal_pad, feature_grads)
    input_grad = input_grads(tap_table, feature_grads, feature_rim)
    short_grad = short_terms.reshape(3 * lag_count, group_count, group_width).sum(-1)
    short_count = short_grad.shape[0]
    both_part = owned_sum(jnp.concatenate([short_grad, taps_grad], 0), "ctx")
    short_part = both_part[None, :short_count]
    medium_part = both_part[None, short_count:]
    incoming = passed_along(input_grad[None], "section", -1)
    return (incoming, short_part, medium_part)


def solution(mesh):
    in_specs = (
        P("section", "ctx", "dp"),
        P("section", "ctx", "dp"),
        P("section", None, "dp"),
        P("section", None, "dp"),
    )
    out_specs = (
        P("section", "ctx", "dp"),
        P("section", None, ("dp", "ctx")),
        P("section", None, ("dp", "ctx")),
    )
    return jax.shard_map(
        per_device, mesh=mesh, in_specs=in_specs, out_specs=out_specs, check_vma=False
    )
```

time: 104 us -> 95.6 us (0.919)
  the two profiles are of different devices: /device:TPU:24 before, /device:TPU:1 now
where the time goes in v7:
time: 95.6 us; the launch traced here: 94.5 us
  starting transfers between devices  36.3 us (38%)
  Pallas kernels  30 us (31%)
  waiting for transfers between devices  14.6 us (15%)
  local copies, waits for them, and re-layouts  10.8 us (11%)
  other arithmetic  1.98 us (2%)
    all_to_all x1, starting transfers between devices, owned_sum(): return jnp.sum(lax.all_to_all(chunks, axis, 0, 0, tiled=False), axis=0)  20 us
    ppermute x5, starting transfers between devices, passed_along(): return lax.ppermute(block, axis, route)  16.3 us
    ppermute x5, waiting for transfers between devices, passed_along(): return lax.ppermute(block, axis, route)  14.6 us
    pallas_call x1, Pallas kernels, medium_terms(): pl.pallas_call(medium_kernel, grid=(chan_count // LANE_BLOCK,), in_specs=...  11.9 us
    pallas_call x1, Pallas kernels, short_partials(): pl.pallas_call(short_partial_kernel, grid=(chan_count // LANE_BLOCK,), in...  6.09 us
    pallas_call x1, Pallas kernels, input_grads(): pl.pallas_call(input_grad_kernel, grid=(chan_count // LANE_BLOCK,), in_sp...  6.03 us
    pallas_call x1, Pallas kernels, short_front(): pl.pallas_call(front_kernel, grid=(chan_count // LANE_BLOCK,), in_specs=[...  6.01 us
    unnamed x13, local copies, waits for them, and re-layouts  2.12 us
  transfers between devices with their start and end apart: 6, of which 4 were waited for; matrix products, arithmetic and copies ran while one was open for 5% of the time, Pallas kernels for 6%

profile of v7, /device:TPU:1, one launch (start us, length us, event | category | flops | bytes accessed | tf_op | source)
XLA Modules:
  0.0 94.5 jit_solution(7709561242476883952)
XLA Ops:
  0.6 0.0 copy-start
  0.6 0.8 slice_bitcast_fusion
  1.4 4.4 %collective-permute-start = (bf16[6,1024]{1,0:T(8,128)(2,1)S(1)}, bf16[6,1024]{1,0:T(8,128)(2,1)S(1)}, u32[]{:S(2)}, u32[]{:S(2)}) collective-permute-start(bf16[6,1024]{1,0:T(8,128)(2,1)S(1)} %slice_bitcast_fusion), channel_id=1, source_target_pairs={{0,4},{4,8},{8,12},{12,16},{16,20},{20,24},{24,28},{28,32},{32,36}... | collective-permute-start | bytes 36872 | tf_op jit(solution)/shard_map/ppermute | solution.py:14
  5.8 0.7 reshape.23
  6.5 0.2 broadcast_in_dim.15
  6.7 1.0 %reshape_reshape.3.taps_ref = f32[21,1024]{1,0:T(8,128)} reshape(f32[3,7,64,16]{3,2,1,0:T(8,128)S(1)} %broadcast_in_dim.15) | data formatting | bytes 172032 | tf_op jit(solution)/shard_map/reshape;reshape | solution.py:237
  7.8 0.0 collective-permute-done
  7.8 0.0 copy-done
  7.8 0.9 pad_maximum_fusion.sig_ref
  8.7 0.0 copy-start.3
  8.7 6.0 %shard_map.67 = (bf16[256,1024]{1,0:T(8,128)(2,1)}, bf16[256,1024]{1,0:T(8,128)(2,1)}, bf16[256,1024]{1,0:T(8,128)(2,1)}, bf16[256,1024]{1,0:T(8,128)(2,1)}, bf16[256,1024]{1,0:T(8,128)(2,1)}) custom-call(f32[21,1024]{1,0:T(8,128)} %reshape_reshape.3.taps_ref, bf16[262,1024]{1,0:T(8,128)(2,1)} %pad_maximum_fusion.sig_ref, bf16[256,1024]{1,0:T(8,128)(2,1)} %bitcast.19), custom_call_target="tpu_custom_call" | custom-call | tf_op jit(solution)/shard_map/pallas_call | solution.py:50
  14.7 1.0 %slice.23 = bf16[127,1024]{1,0:T(8,128)(2,1)S(1)} slice(bf16[256,1024]{1,0:T(8,128)(2,1)} %get-tuple-element.9.prod_ref), slice={[129:256], [0:1024]} | slice | bytes 520192 | tf_op jit(solution)/shard_map/slice | solution.py:241
  15.7 1.0 %slice.24 = bf16[127,1024]{1,0:T(8,128)(2,1)S(1)} slice(bf16[256,1024]{1,0:T(8,128)(2,1)} %get-tuple-element.10.gate_ref), slice={[0:127], [0:1024]} | slice | bytes 520192 | tf_op jit(solution)/shard_map/slice | solution.py:242
  16.7 1.3 %collective-permute-start.2 = (bf16[127,1024]{1,0:T(8,128)(2,1)S(1)}, bf16[127,1024]{1,0:T(8,128)(2,1)S(1)}, u32[]{:S(2)}, u32[]{:S(2)}) collective-permute-start(bf16[127,1024]{1,0:T(8,128)(2,1)S(1)} %slice.24), channel_id=1, source_target_pairs={{4,0},{8,4},{12,8},{16,12},{20,16},{24,20},{28,24},{32,28},{36,32}... | collective-permute-start | bytes 780296 | tf_op jit(solution)/shard_map/ppermute | solution.py:14
  18.0 4.2 %collective-permute-start.1 = (bf16[127,1024]{1,0:T(8,128)(2,1)S(1)}, bf16[127,1024]{1,0:T(8,128)(2,1)S(1)}, u32[]{:S(2)}, u32[]{:S(2)}) collective-permute-start(bf16[127,1024]{1,0:T(8,128)(2,1)S(1)} %slice.23), channel_id=1, source_target_pairs={{0,4},{4,8},{8,12},{12,16},{16,20},{20,24},{24,28},{28,32},{32,36}... | collective-permute-start | bytes 780296 | tf_op jit(solution)/shard_map/ppermute | solution.py:14
  22.2 0.0 copy-done.3
  22.2 0.1 rev.4
  22.3 0.7 pad_convert_fusion
  23.0 1.0 %collective-permute-done.2.gate_rim_ref = bf16[127,1024]{1,0:T(8,128)(2,1)S(1)} collective-permute-done((bf16[127,1024]{1,0:T(8,128)(2,1)S(1)}, bf16[127,1024]{1,0:T(8,128)(2,1)S(1)}, u32[]{:S(2)}, u32[]{:S(2)}) %collective-permute-start.2) | collective-permute-done | bytes 260128 | tf_op jit(solution)/shard_map/ppermute | solution.py:14
  24.0 0.0 copy-start.1
  24.0 1.5 %collective-permute-done.1.kv_rim_ref = bf16[127,1024]{1,0:T(8,128)(2,1)S(1)} collective-permute-done((bf16[127,1024]{1,0:T(8,128)(2,1)S(1)}, bf16[127,1024]{1,0:T(8,128)(2,1)S(1)}, u32[]{:S(2)}, u32[]{:S(2)}) %collective-permute-start.1) | collective-permute-done | bytes 260128 | tf_op jit(solution)/shard_map/ppermute | solution.py:14
  25.5 0.0 copy-start.2
  25.5 0.0 copy-done.1
  25.5 0.7 copy-done.2
  26.2 11.9 %shard_map.68 = (bf16[3,256,1024]{2,1,0:T(8,128)(2,1)}, f32[64,128]{1,0:T(8,128)}) custom-call(f32[64,256]{1,0:T(8,128)} %get-tuple-element.16.fwd_ref, f32[64,256]{1,0:T(8,128)} %get-tuple-element.15.bwd_ref, bf16[127,1024]{1,0:T(8,128)(2,1)} %copy-done.2, bf16[256,1024]{1,0:T(8,128)(2,1)} %get-tuple-element.9.prod_ref, ...), custom_call_target="tpu_custom_call" | custom-call | tf_op jit(solution)/shard_map/pallas_call | solution.py:200
  38.1 6.1 %shard_map.70 = f32[21,1024]{1,0:T(8,128)} custom-call(bf16[262,1024]{1,0:T(8,128)(2,1)} %pad_maximum_fusion.sig_ref, bf16[3,256,1024]{2,1,0:T(8,128)(2,1)} %get-tuple-element.13.grads_ref), custom_call_target="tpu_custom_call" | custom-call | tf_op jit(solution)/shard_map/pallas_call | solution.py:95
  44.2 0.0 copy-start.5
  44.2 1.1 %reshape.21 = f32[21,64,16]{2,1,0:T(8,128)S(1)} reshape(f32[21,1024]{1,0:T(8,128)} %shard_map.70) | data formatting | bytes 172032 | tf_op jit(solution)/shard_map/reshape | solution.py:250
  45.3 0.3 reduce_sum.18
  45.6 0.1 copy.7
  45.7 0.0 copy-done.5
  45.7 0.1 pad_maximum_fusion.1
  45.8 0.7 reshape.22
  46.4 20.0 %all-to-all-start = ((f32[32,149,2]{1,2,0:T(2,128)}), f32[32,149,2]{1,2,0:T(2,128)S(1)}, u32[]{:S(2)}, u32[]{:S(2)}) async-start(f32[32,149,2]{1,2,0:T(2,128)} %bitcast.8), calls=%async_computation | async-start | bytes 131072 | tf_op jit(solution)/shard_map/all_to_all | solution.py:22
  66.4 0.8 slice.25
  67.2 1.3 %collective-permute-start.3 = (bf16[3,6,1024]{2,1,0:T(8,128)(2,1)S(1)}, bf16[3,6,1024]{2,1,0:T(8,128)(2,1)S(1)}, u32[]{:S(2)}, u32[]{:S(2)}) collective-permute-start(bf16[3,6,1024]{2,1,0:T(8,128)(2,1)S(1)} %slice.25), channel_id=1, source_target_pairs={{4,0},{8,4},{12,8},{16,12},{20,16},{24,20},{28,24},{32,28},{36,32}... | collective-permute-start | bytes 110600 | tf_op jit(solution)/shard_map/ppermute | solution.py:14
  68.5 3.9 %collective-permute-done.3.rim_ref = bf16[3,6,1024]{2,1,0:T(8,128)(2,1)S(1)} collective-permute-done((bf16[3,6,1024]{2,1,0:T(8,128)(2,1)S(1)}, bf16[3,6,1024]{2,1,0:T(8,128)(2,1)S(1)}, u32[]{:S(2)}, u32[]{:S(2)}) %collective-permute-start.3) | collective-permute-done | bytes 36896 | tf_op jit(solution)/shard_map/ppermute | solution.py:14
  72.5 0.0 copy-start.4
  72.5 0.6 copy-done.4
  73.1 6.0 %shard_map.69 = bf16[256,1024]{1,0:T(8,128)(2,1)} custom-call(f32[21,1024]{1,0:T(8,128)} %reshape_reshape.3.taps_ref, bf16[3,256,1024]{2,1,0:T(8,128)(2,1)} %get-tuple-element.13.grads_ref, bf16[3,6,1024]{2,1,0:T(8,128)(2,1)} %copy-done.4), custom_call_target="tpu_custom_call" | custom-call | tf_op jit(solution)/shard_map/pallas_call | solution.py:111
  79.1 5.2 %collective-permute-start.4 = (bf16[1,256,1024]{2,1,0:T(8,128)(2,1)}, bf16[1,256,1024]{2,1,0:T(8,128)(2,1)S(1)}, u32[]{:S(2)}, u32[]{:S(2)}) collective-permute-start(bf16[1,256,1024]{2,1,0:T(8,128)(2,1)} %bitcast.22), channel_id=1, source_target_pairs={{128,0},{256,128},{384,256},{129,1},{257,129},{385,257},{130,2},{2... | collective-permute-start | bytes 1572872 | tf_op jit(solution)/shard_map/ppermute | solution.py:14
  84.3 0.0 all-to-all-done
  84.3 0.6 slice_bitcast_fusion.1
  85.0 0.6 slice_bitcast_fusion.2
  85.5 8.1 %collective-permute-done.4 = bf16[1,256,1024]{2,1,0:T(8,128)(2,1)S(1)} collective-permute-done((bf16[1,256,1024]{2,1,0:T(8,128)(2,1)}, bf16[1,256,1024]{2,1,0:T(8,128)(2,1)S(1)}, u32[]{:S(2)}, u32[]{:S(2)}) %collective-permute-start.4) | collective-permute-done | bytes 524320 | tf_op jit(solution)/shard_map/ppermute | solution.py:14
  93.7 0.8 copy.9
  (1 shorter events, 0.0 us)
Async XLA Ops:
  0.6 7.1 %copy-start = (bf16[1,256,1024]{2,1,0:T(8,128)(2,1)S(1)}, bf16[1,256,1024]{2,1,0:T(8,128)(2,1)}, u32[]{:S(2)}) copy-start(bf16[1,256,1024]{2,1,0:T(8,128)(2,1)} %param.4) | copy-start | bytes 1572868
  1.4 6.3 %collective-permute-start = (bf16[6,1024]{1,0:T(8,128)(2,1)S(1)}, bf16[6,1024]{1,0:T(8,128)(2,1)S(1)}, u32[]{:S(2)}, u32[]{:S(2)}) collective-permute-start(bf16[6,1024]{1,0:T(8,128)(2,1)S(1)} %slice_bitcast_fusion), channel_id=1, source_target_pairs={{0,4},{4,8},{8,12},{12,16},{16,20},{20,24},{24,28},{28,32},{32,36}... | collective-permute-start | bytes 36872 | tf_op jit(solution)/shard_map/ppermute | solution.py:14
  8.7 13.5 %copy-start.3 = (bf16[1,128,64]{1,2,0:T(8,128)(2,1)S(1)}, bf16[1,128,64]{1,2,0:T(8,128)(2,1)}, u32[]{:S(2)}) copy-start(bf16[1,128,64]{1,2,0:T(8,128)(2,1)} %param.7) | copy-start | bytes 49156
  16.7 7.3 %collective-permute-start.2 = (bf16[127,1024]{1,0:T(8,128)(2,1)S(1)}, bf16[127,1024]{1,0:T(8,128)(2,1)S(1)}, u32[]{:S(2)}, u32[]{:S(2)}) collective-permute-start(bf16[127,1024]{1,0:T(8,128)(2,1)S(1)} %slice.24), channel_id=1, source_target_pairs={{4,0},{8,4},{12,8},{16,12},{20,16},{24,20},{28,24},{32,28},{36,32}... | collective-permute-start | bytes 780296 | tf_op jit(solution)/shard_map/ppermute | solution.py:14
  18.0 7.5 %collective-permute-start.1 = (bf16[127,1024]{1,0:T(8,128)(2,1)S(1)}, bf16[127,1024]{1,0:T(8,128)(2,1)S(1)}, u32[]{:S(2)}, u32[]{:S(2)}) collective-permute-start(bf16[127,1024]{1,0:T(8,128)(2,1)S(1)} %slice.23), channel_id=1, source_target_pairs={{0,4},{4,8},{8,12},{12,16},{16,20},{20,24},{24,28},{28,32},{32,36}... | collective-permute-start | bytes 780296 | tf_op jit(solution)/shard_map/ppermute | solution.py:14
  24.0 1.5 %copy-start.1 = (bf16[127,1024]{1,0:T(8,128)(2,1)}, bf16[127,1024]{1,0:T(8,128)(2,1)S(1)}, u32[]{:S(2)}) copy-start(bf16[127,1024]{1,0:T(8,128)(2,1)S(1)} %collective-permute-done.2.gate_rim_ref) | copy-start | bytes 780292
  25.5 0.7 copy-start.2
  44.2 1.5 %copy-start.5 = (f32[64,128]{1,0:T(8,128)S(1)}, f32[64,128]{1,0:T(8,128)}, u32[]{:S(2)}) copy-start(f32[64,128]{1,0:T(8,128)} %get-tuple-element.14) | copy-start | bytes 98308
  46.4 37.8 %all-to-all-start = ((f32[32,149,2]{1,2,0:T(2,128)}), f32[32,149,2]{1,2,0:T(2,128)S(1)}, u32[]{:S(2)}, u32[]{:S(2)}) async-start(f32[32,149,2]{1,2,0:T(2,128)} %bitcast.8), calls=%async_computation | async-start | bytes 131072 | tf_op jit(solution)/shard_map/all_to_all | solution.py:22
  67.2 5.2 %collective-permute-start.3 = (bf16[3,6,1024]{2,1,0:T(8,128)(2,1)S(1)}, bf16[3,6,1024]{2,1,0:T(8,128)(2,1)S(1)}, u32[]{:S(2)}, u32[]{:S(2)}) collective-permute-start(bf16[3,6,1024]{2,1,0:T(8,128)(2,1)S(1)} %slice.25), channel_id=1, source_target_pairs={{4,0},{8,4},{12,8},{16,12},{20,16},{24,20},{28,24},{32,28},{36,32}... | collective-permute-start | bytes 110600 | tf_op jit(solution)/shard_map/ppermute | solution.py:14
  72.5 0.6 copy-start.4
  79.1 14.6 %collective-permute-start.4 = (bf16[1,256,1024]{2,1,0:T(8,128)(2,1)}, bf16[1,256,1024]{2,1,0:T(8,128)(2,1)S(1)}, u32[]{:S(2)}, u32[]{:S(2)}) collective-permute-start(bf16[1,256,1024]{2,1,0:T(8,128)(2,1)} %bitcast.22), channel_id=1, source_target_pairs={{128,0},{256,128},{384,256},{129,1},{257,129},{385,257},{130,2},{2... | collective-permute-start | bytes 1572872 | tf_op jit(solution)/shard_map/ppermute | solution.py:14

commit v8 on v7

--- a/solution.py
+++ b/solution.py
@@ -249,7 +249,9 @@
     input_grad = input_grads(tap_table, feature_grads, feature_rim)
     short_grad = short_terms.reshape(3 * lag_count, group_count, group_width).sum(-1)
     short_count = short_grad.shape[0]
-    both_part = owned_sum(jnp.concatenate([short_grad, taps_grad], 0), "ctx")
+    local_terms = jnp.concatenate([short_grad, taps_grad], 0)
+    input_grad, local_terms = lax.optimization_barrier((input_grad, local_terms))
+    both_part = owned_sum(local_terms, "ctx")
     short_part = both_part[None, :short_count]
     medium_part = both_part[None, short_count:]
     incoming = passed_along(input_grad[None], "section", -1)

time: 95.6 us -> 96.5 us (level)
  the two profiles are of different devices: /device:TPU:1 before, /device:TPU:16 now
where the time goes in v8:
time: 96.5 us; the launch traced here: 95.4 us
  starting transfers between devices  31 us (32%)
  Pallas kernels  30 us (31%)
  waiting for transfers between devices  20.8 us (22%)
  local copies, waits for them, and re-layouts  10.8 us (11%)
  other arithmetic  1.98 us (2%)
    all_to_all x1, starting transfers between devices, owned_sum(): return jnp.sum(lax.all_to_all(chunks, axis, 0, 0, tiled=False), axis=0)  18.7 us
    all_to_all x1, waiting for transfers between devices, owned_sum(): return jnp.sum(lax.all_to_all(chunks, axis, 0, 0, tiled=False), axis=0)  12.8 us
    ppermute x5, starting transfers between devices, passed_along(): return lax.ppermute(block, axis, route)  12.2 us
    pallas_call x1, Pallas kernels, medium_terms(): pl.pallas_call(medium_kernel, grid=(chan_count // LANE_BLOCK,), in_specs=...  11.9 us
    ppermute x5, waiting for transfers between devices, passed_along(): return lax.ppermute(block, axis, route)  7.96 us
    pallas_call x1, Pallas kernels, short_partials(): pl.pallas_call(short_partial_kernel, grid=(chan_count // LANE_BLOCK,), in...  6.09 us
    pallas_call x1, Pallas kernels, input_grads(): pl.pallas_call(input_grad_kernel, grid=(chan_count // LANE_BLOCK,), in_sp...  6.03 us
    pallas_call x1, Pallas kernels, short_front(): pl.pallas_call(front_kernel, grid=(chan_count // LANE_BLOCK,), in_specs=[...  6.01 us
  transfers between devices with their start and end apart: 6, of which 4 were waited for; matrix products, arithmetic and copies ran while one was open for 6% of the time, Pallas kernels for 0%

profile of v8, /device:TPU:16, one launch (start us, length us, event | category | flops | bytes accessed | tf_op | source)
XLA Modules:
  0.0 95.4 jit_solution(8988137409445356867)
XLA Ops:
  0.6 0.0 copy-start
  0.6 0.8 slice_bitcast_fusion
  1.4 3.8 %collective-permute-start = (bf16[6,1024]{1,0:T(8,128)(2,1)S(1)}, bf16[6,1024]{1,0:T(8,128)(2,1)S(1)}, u32[]{:S(2)}, u32[]{:S(2)}) collective-permute-start(bf16[6,1024]{1,0:T(8,128)(2,1)S(1)} %slice_bitcast_fusion), channel_id=1, source_target_pairs={{0,4},{4,8},{8,12},{12,16},{16,20},{20,24},{24,28},{28,32},{32,36}... | collective-permute-start | bytes 36872 | tf_op jit(solution)/shard_map/ppermute | solution.py:14
  5.2 0.7 reshape.23
  5.9 0.2 broadcast_in_dim.15
  6.2 1.0 %reshape_reshape.3.taps_ref = f32[21,1024]{1,0:T(8,128)} reshape(f32[3,7,64,16]{3,2,1,0:T(8,128)S(1)} %broadcast_in_dim.15) | data formatting | bytes 172032 | tf_op jit(solution)/shard_map/reshape;reshape | solution.py:237
  7.2 0.0 collective-permute-done
  7.2 0.0 copy-done
  7.2 0.9 pad_maximum_fusion.sig_ref
  8.1 0.0 copy-start.3
  8.1 6.0 %shard_map.67 = (bf16[256,1024]{1,0:T(8,128)(2,1)}, bf16[256,1024]{1,0:T(8,128)(2,1)}, bf16[256,1024]{1,0:T(8,128)(2,1)}, bf16[256,1024]{1,0:T(8,128)(2,1)}, bf16[256,1024]{1,0:T(8,128)(2,1)}) custom-call(f32[21,1024]{1,0:T(8,128)} %reshape_reshape.3.taps_ref, bf16[262,1024]{1,0:T(8,128)(2,1)} %pad_maximum_fusion.sig_ref, bf16[256,1024]{1,0:T(8,128)(2,1)} %bitcast.19), custom_call_target="tpu_custom_call" | custom-call | tf_op jit(solution)/shard_map/pallas_call | solution.py:50
  14.2 1.0 %slice.23 = bf16[127,1024]{1,0:T(8,128)(2,1)S(1)} slice(bf16[256,1024]{1,0:T(8,128)(2,1)} %get-tuple-element.11.prod_ref), slice={[129:256], [0:1024]} | slice | bytes 520192 | tf_op jit(solution)/shard_map/slice | solution.py:241
  15.2 1.0 %slice.24 = bf16[127,1024]{1,0:T(8,128)(2,1)S(1)} slice(bf16[256,1024]{1,0:T(8,128)(2,1)} %get-tuple-element.12.gate_ref), slice={[0:127], [0:1024]} | slice | bytes 520192 | tf_op jit(solution)/shard_map/slice | solution.py:242
  16.1 1.3 %collective-permute-start.2 = (bf16[127,1024]{1,0:T(8,128)(2,1)S(1)}, bf16[127,1024]{1,0:T(8,128)(2,1)S(1)}, u32[]{:S(2)}, u32[]{:S(2)}) collective-permute-start(bf16[127,1024]{1,0:T(8,128)(2,1)S(1)} %slice.24), channel_id=1, source_target_pairs={{4,0},{8,4},{12,8},{16,12},{20,16},{24,20},{28,24},{32,28},{36,32}... | collective-permute-start | bytes 780296 | tf_op jit(solution)/shard_map/ppermute | solution.py:14
  17.4 4.6 %collective-permute-start.1 = (bf16[127,1024]{1,0:T(8,128)(2,1)S(1)}, bf16[127,1024]{1,0:T(8,128)(2,1)S(1)}, u32[]{:S(2)}, u32[]{:S(2)}) collective-permute-start(bf16[127,1024]{1,0:T(8,128)(2,1)S(1)} %slice.23), channel_id=1, source_target_pairs={{0,4},{4,8},{8,12},{12,16},{16,20},{20,24},{24,28},{28,32},{32,36}... | collective-permute-start | bytes 780296 | tf_op jit(solution)/shard_map/ppermute | solution.py:14
  22.0 0.0 copy-done.3
  22.0 0.1 rev.4
  22.1 0.7 pad_convert_fusion
  22.8 3.2 %collective-permute-done.2.gate_rim_ref = bf16[127,1024]{1,0:T(8,128)(2,1)S(1)} collective-permute-done((bf16[127,1024]{1,0:T(8,128)(2,1)S(1)}, bf16[127,1024]{1,0:T(8,128)(2,1)S(1)}, u32[]{:S(2)}, u32[]{:S(2)}) %collective-permute-start.2) | collective-permute-done | bytes 260128 | tf_op jit(solution)/shard_map/ppermute | solution.py:14
  26.0 0.0 copy-start.1
  26.0 1.2 %collective-permute-done.1.kv_rim_ref = bf16[127,1024]{1,0:T(8,128)(2,1)S(1)} collective-permute-done((bf16[127,1024]{1,0:T(8,128)(2,1)S(1)}, bf16[127,1024]{1,0:T(8,128)(2,1)S(1)}, u32[]{:S(2)}, u32[]{:S(2)}) %collective-permute-start.1) | collective-permute-done | bytes 260128 | tf_op jit(solution)/shard_map/ppermute | solution.py:14
  27.2 0.0 copy-start.2
  27.2 0.0 copy-done.1
  27.2 0.7 copy-done.2
  27.9 11.9 %shard_map.68 = (bf16[3,256,1024]{2,1,0:T(8,128)(2,1)}, f32[64,128]{1,0:T(8,128)}) custom-call(f32[64,256]{1,0:T(8,128)} %get-tuple-element.20.fwd_ref, f32[64,256]{1,0:T(8,128)} %get-tuple-element.19.bwd_ref, bf16[127,1024]{1,0:T(8,128)(2,1)} %copy-done.2, bf16[256,1024]{1,0:T(8,128)(2,1)} %get-tuple-element.11.prod_ref, ...), custom_call_target="tpu_custom_call" | custom-call | tf_op jit(solution)/shard_map/pallas_call | solution.py:200
  39.8 6.1 %shard_map.70 = f32[21,1024]{1,0:T(8,128)} custom-call(bf16[262,1024]{1,0:T(8,128)(2,1)} %pad_maximum_fusion.sig_ref, bf16[3,256,1024]{2,1,0:T(8,128)(2,1)} %get-tuple-element.15.grads_ref), custom_call_target="tpu_custom_call" | custom-call | tf_op jit(solution)/shard_map/pallas_call | solution.py:95
  45.9 0.0 copy-start.5
  45.9 0.8 slice.25
  46.7 1.3 %collective-permute-start.3 = (bf16[3,6,1024]{2,1,0:T(8,128)(2,1)S(1)}, bf16[3,6,1024]{2,1,0:T(8,128)(2,1)S(1)}, u32[]{:S(2)}, u32[]{:S(2)}) collective-permute-start(bf16[3,6,1024]{2,1,0:T(8,128)(2,1)S(1)} %slice.25), channel_id=1, source_target_pairs={{4,0},{8,4},{12,8},{16,12},{20,16},{24,20},{28,24},{32,28},{36,32}... | collective-permute-start | bytes 110600 | tf_op jit(solution)/shard_map/ppermute | solution.py:14
  48.0 1.1 %reshape.21 = f32[21,64,16]{2,1,0:T(8,128)S(1)} reshape(f32[21,1024]{1,0:T(8,128)} %shard_map.70) | data formatting | bytes 172032 | tf_op jit(solution)/shard_map/reshape | solution.py:250
  49.1 0.3 reduce_sum.18
  49.4 0.1 copy.7
  49.5 0.0 copy-done.5
  49.5 0.1 pad_maximum_fusion.1
  49.6 3.6 %collective-permute-done.3.rim_ref = bf16[3,6,1024]{2,1,0:T(8,128)(2,1)S(1)} collective-permute-done((bf16[3,6,1024]{2,1,0:T(8,128)(2,1)S(1)}, bf16[3,6,1024]{2,1,0:T(8,128)(2,1)S(1)}, u32[]{:S(2)}, u32[]{:S(2)}) %collective-permute-start.3) | collective-permute-done | bytes 36896 | tf_op jit(solution)/shard_map/ppermute | solution.py:14
  53.1 0.0 copy-start.4
  53.1 0.6 copy-done.4
  53.7 6.0 %shard_map.69 = bf16[256,1024]{1,0:T(8,128)(2,1)} custom-call(f32[21,1024]{1,0:T(8,128)} %reshape_reshape.3.taps_ref, bf16[3,256,1024]{2,1,0:T(8,128)(2,1)} %get-tuple-element.15.grads_ref, bf16[3,6,1024]{2,1,0:T(8,128)(2,1)} %copy-done.4), custom_call_target="tpu_custom_call" | custom-call | tf_op jit(solution)/shard_map/pallas_call | solution.py:111
  59.8 0.7 reshape.22
  60.4 18.7 %all-to-all-start = ((f32[32,149,2]{1,2,0:T(2,128)}), f32[32,149,2]{1,2,0:T(2,128)S(1)}, u32[]{:S(2)}, u32[]{:S(2)}) async-start(f32[32,149,2]{1,2,0:T(2,128)} %bitcast.8), calls=%async_computation | async-start | bytes 131072 | tf_op jit(solution)/shard_map/all_to_all | solution.py:22
  79.2 1.3 %collective-permute-start.4 = (bf16[1,256,1024]{2,1,0:T(8,128)(2,1)}, bf16[1,256,1024]{2,1,0:T(8,128)(2,1)S(1)}, u32[]{:S(2)}, u32[]{:S(2)}) collective-permute-start(bf16[1,256,1024]{2,1,0:T(8,128)(2,1)} %bitcast.22), channel_id=1, source_target_pairs={{128,0},{256,128},{384,256},{129,1},{257,129},{385,257},{130,2},{2... | collective-permute-start | bytes 1572872 | tf_op jit(solution)/shard_map/ppermute | solution.py:14
  80.5 12.8 %all-to-all-done = f32[32,149,2]{1,2,0:T(2,128)S(1)} async-done(((f32[32,149,2]{1,2,0:T(2,128)}), f32[32,149,2]{1,2,0:T(2,128)S(1)}, u32[]{:S(2)}, u32[]{:S(2)}) %all-to-all-start) | async-done | bytes 38176 | tf_op jit(solution)/shard_map/all_to_all | solution.py:22
  93.4 0.6 slice_bitcast_fusion.1
  94.0 0.6 slice_bitcast_fusion.2
  94.6 0.0 collective-permute-done.4
  94.6 0.8 copy.9
  (1 shorter events, 0.0 us)
Async XLA Ops:
  0.6 6.6 %copy-start = (bf16[1,256,1024]{2,1,0:T(8,128)(2,1)S(1)}, bf16[1,256,1024]{2,1,0:T(8,128)(2,1)}, u32[]{:S(2)}) copy-start(bf16[1,256,1024]{2,1,0:T(8,128)(2,1)} %param.4) | copy-start | bytes 1572868
  1.4 5.8 %collective-permute-start = (bf16[6,1024]{1,0:T(8,128)(2,1)S(1)}, bf16[6,1024]{1,0:T(8,128)(2,1)S(1)}, u32[]{:S(2)}, u32[]{:S(2)}) collective-permute-start(bf16[6,1024]{1,0:T(8,128)(2,1)S(1)} %slice_bitcast_fusion), channel_id=1, source_target_pairs={{0,4},{4,8},{8,12},{12,16},{16,20},{20,24},{24,28},{28,32},{32,36}... | collective-permute-start | bytes 36872 | tf_op jit(solution)/shard_map/ppermute | solution.py:14
  8.1 13.9 %copy-start.3 = (bf16[1,128,64]{1,2,0:T(8,128)(2,1)S(1)}, bf16[1,128,64]{1,2,0:T(8,128)(2,1)}, u32[]{:S(2)}) copy-start(bf16[1,128,64]{1,2,0:T(8,128)(2,1)} %param.7) | copy-start | bytes 49156
  16.1 9.8 %collective-permute-start.2 = (bf16[127,1024]{1,0:T(8,128)(2,1)S(1)}, bf16[127,1024]{1,0:T(8,128)(2,1)S(1)}, u32[]{:S(2)}, u32[]{:S(2)}) collective-permute-start(bf16[127,1024]{1,0:T(8,128)(2,1)S(1)} %slice.24), channel_id=1, source_target_pairs={{4,0},{8,4},{12,8},{16,12},{20,16},{24,20},{28,24},{32,28},{36,32}... | collective-permute-start | bytes 780296 | tf_op jit(solution)/shard_map/ppermute | solution.py:14
  17.4 9.7 %collective-permute-start.1 = (bf16[127,1024]{1,0:T(8,128)(2,1)S(1)}, bf16[127,1024]{1,0:T(8,128)(2,1)S(1)}, u32[]{:S(2)}, u32[]{:S(2)}) collective-permute-start(bf16[127,1024]{1,0:T(8,128)(2,1)S(1)} %slice.23), channel_id=1, source_target_pairs={{0,4},{4,8},{8,12},{12,16},{16,20},{20,24},{24,28},{28,32},{32,36}... | collective-permute-start | bytes 780296 | tf_op jit(solution)/shard_map/ppermute | solution.py:14
  26.0 1.2 %copy-start.1 = (bf16[127,1024]{1,0:T(8,128)(2,1)}, bf16[127,1024]{1,0:T(8,128)(2,1)S(1)}, u32[]{:S(2)}) copy-start(bf16[127,1024]{1,0:T(8,128)(2,1)S(1)} %collective-permute-done.2.gate_rim_ref) | copy-start | bytes 780292
  27.2 0.7 copy-start.2
  45.9 3.6 %copy-start.5 = (f32[64,128]{1,0:T(8,128)S(1)}, f32[64,128]{1,0:T(8,128)}, u32[]{:S(2)}) copy-start(f32[64,128]{1,0:T(8,128)} %get-tuple-element.16) | copy-start | bytes 98308
  46.7 6.4 %collective-permute-start.3 = (bf16[3,6,1024]{2,1,0:T(8,128)(2,1)S(1)}, bf16[3,6,1024]{2,1,0:T(8,128)(2,1)S(1)}, u32[]{:S(2)}, u32[]{:S(2)}) collective-permute-start(bf16[3,6,1024]{2,1,0:T(8,128)(2,1)S(1)} %slice.25), channel_id=1, source_target_pairs={{4,0},{8,4},{12,8},{16,12},{20,16},{24,20},{28,24},{32,28},{36,32}... | collective-permute-start | bytes 110600 | tf_op jit(solution)/shard_map/ppermute | solution.py:14
  53.1 0.6 copy-start.4
  60.4 32.9 %all-to-all-start = ((f32[32,149,2]{1,2,0:T(2,128)}), f32[32,149,2]{1,2,0:T(2,128)S(1)}, u32[]{:S(2)}, u32[]{:S(2)}) async-start(f32[32,149,2]{1,2,0:T(2,128)} %bitcast.8), calls=%async_computation | async-start | bytes 131072 | tf_op jit(solution)/shard_map/all_to_all | solution.py:22
  79.2 15.4 %collective-permute-start.4 = (bf16[1,256,1024]{2,1,0:T(8,128)(2,1)}, bf16[1,256,1024]{2,1,0:T(8,128)(2,1)S(1)}, u32[]{:S(2)}, u32[]{:S(2)}) collective-permute-start(bf16[1,256,1024]{2,1,0:T(8,128)(2,1)} %bitcast.22), channel_id=1, source_target_pairs={{128,0},{256,128},{384,256},{129,1},{257,129},{385,257},{130,2},{2... | collective-permute-start | bytes 1572872 | tf_op jit(solution)/shard_map/ppermute | solution.py:14

commit v9 on v7

--- a/solution.py
+++ b/solution.py
@@ -235,12 +235,16 @@
     ).reshape(3, lag_count, chan_count)
     medium_taps = medium_filter[0]
     tap_table = chan_short.reshape(3 * lag_count, chan_count)
+    prev_rows = passed_along(signal[seq_rows - medium_rim - short_rim :], "ctx", 1)
+    next_rows, next_grad = passed_along(
+        (signal[:medium_rim], grad_out[:medium_rim]), "ctx", -1
+    )
     signal_rim = passed_along(signal[seq_rows - short_rim :], "ctx", 1)
     signal_pad = jnp.concatenate([signal_rim, signal], 0)
     query_in, key_in, value_in, products, gate_grad = short_front(tap_table, signal_pad, grad_out)
-    kv_rim, gate_rim = passed_along(products[seq_rows - medium_rim :], "ctx", 1), passed_along(
-        gate_grad[:medium_rim], "ctx", -1
-    )
+    kv_rim = short_front(tap_table, prev_rows, jnp.zeros_like(next_grad))[3]
+    next_pad = jnp.concatenate([signal[seq_rows - short_rim :], next_rows], 0)
+    gate_rim = short_front(tap_table, next_pad, next_grad)[4]
     feature_grads, taps_grad = medium_terms(
         medium_taps, kv_rim, products, gate_grad, gate_rim, grad_out, key_in, value_in
     )

time: 95.6 us -> 103 us (1.077)
  Pallas kernels: 30 us -> 40 us
  waiting for transfers between devices: 14.6 us -> 12 us
  starting transfers between devices: 36.3 us -> 34.8 us
    pallas_call x1 -> x3, Pallas kernels: 6.01 us -> 16 us  [short_front(): pl.pallas_call(front_kernel, grid=(chan_count // LANE_BLOCK,), in_specs=[...]
    all_to_all x1, starting transfers between devices: 20 us -> 17 us  [owned_sum(): return jnp.sum(lax.all_to_all(chunks, axis, 0, 0, tiled=False), axis=0)]
    ppermute x5 -> x6, waiting for transfers between devices: 14.6 us -> 12 us  [passed_along(): return lax.ppermute(block, axis, route)]
    ppermute x5 -> x6, starting transfers between devices: 16.3 us -> 17.8 us  [passed_along(): return lax.ppermute(block, axis, route)]
    unnamed x13 -> x15, local copies, waits for them, and re-layouts: 2.12 us -> 2.13 us
  transfers between devices with their start and end apart: 6 -> 7, of which waited for: 4 -> 2; matrix products, arithmetic and copies ran while one was open for 5% -> 8% of each run, Pallas kernels for 6% -> 17%
where the time goes in v9:
time: 103 us; the launch traced here: 101 us
  Pallas kernels  40 us (39%)
  starting transfers between devices  34.8 us (34%)
  waiting for transfers between devices  12 us (12%)
  local copies, waits for them, and re-layouts  10.9 us (11%)
  other arithmetic  2.77 us (3%)
    ppermute x6, starting transfers between devices, passed_along(): return lax.ppermute(block, axis, route)  17.8 us
    all_to_all x1, starting transfers between devices, owned_sum(): return jnp.sum(lax.all_to_all(chunks, axis, 0, 0, tiled=False), axis=0)  17 us
    pallas_call x3, Pallas kernels, short_front(): pl.pallas_call(front_kernel, grid=(chan_count // LANE_BLOCK,), in_specs=[...  16 us
    ppermute x6, waiting for transfers between devices, passed_along(): return lax.ppermute(block, axis, route)  12 us
    pallas_call x1, Pallas kernels, medium_terms(): pl.pallas_call(medium_kernel, grid=(chan_count // LANE_BLOCK,), in_specs=...  11.9 us
    pallas_call x1, Pallas kernels, short_partials(): pl.pallas_call(short_partial_kernel, grid=(chan_count // LANE_BLOCK,), in...  6.09 us
    pallas_call x1, Pallas kernels, input_grads(): pl.pallas_call(input_grad_kernel, grid=(chan_count // LANE_BLOCK,), in_sp...  6.03 us
    unnamed x15, local copies, waits for them, and re-layouts  2.13 us
  transfers between devices with their start and end apart: 7, of which 2 were waited for; matrix products, arithmetic and copies ran while one was open for 8% of the time, Pallas kernels for 17%

profile of v9, /device:TPU:1, one launch (start us, length us, event | category | flops | bytes accessed | tf_op | source)
XLA Modules:
  0.0 101.4 jit_solution(15241487591547585971)
XLA Ops:
  0.6 0.0 copy-start
  0.6 0.0 copy-start.3
  0.7 0.0 copy-start.6
  0.7 0.8 slice_bitcast_fusion.3
  1.4 4.4 %collective-permute-start.1 = (bf16[6,1024]{1,0:T(8,128)(2,1)S(1)}, bf16[6,1024]{1,0:T(8,128)(2,1)S(1)}, u32[]{:S(2)}, u32[]{:S(2)}) collective-permute-start(bf16[6,1024]{1,0:T(8,128)(2,1)S(1)} %slice_bitcast_fusion.3), channel_id=1, source_target_pairs={{0,4},{4,8},{8,12},{12,16},{16,20},{20,24},{24,28},{28,32},{32,36}... | collective-permute-start | bytes 36872 | tf_op jit(solution)/shard_map/ppermute | solution.py:14
  5.8 1.0 slice_bitcast_fusion.2
  6.8 1.3 %collective-permute-start.2 = (bf16[127,1024]{1,0:T(8,128)(2,1)S(1)}, bf16[127,1024]{1,0:T(8,128)(2,1)S(1)}, u32[]{:S(2)}, u32[]{:S(2)}) collective-permute-start(bf16[127,1024]{1,0:T(8,128)(2,1)S(1)} %slice_bitcast_fusion.2), channel_id=1, source_target_pairs={{4,0},{8,4},{12,8},{16,12},{20,16},{24,20},{28,24},{32,28},{36,32}... | collective-permute-start | bytes 780296 | tf_op jit(solution)/shard_map/ppermute | solution.py:14
  8.1 1.0 slice_bitcast_fusion.1
  9.1 1.3 %collective-permute-start.3 = (bf16[127,1024]{1,0:T(8,128)(2,1)S(1)}, bf16[127,1024]{1,0:T(8,128)(2,1)S(1)}, u32[]{:S(2)}, u32[]{:S(2)}) collective-permute-start(bf16[127,1024]{1,0:T(8,128)(2,1)S(1)} %slice_bitcast_fusion.1), channel_id=1, source_target_pairs={{4,0},{8,4},{12,8},{16,12},{20,16},{24,20},{28,24},{32,28},{36,32}... | collective-permute-start | bytes 780296 | tf_op jit(solution)/shard_map/ppermute | solution.py:14
  10.4 0.0 copy-done
  10.4 0.1 slice_bitcast_fusion
  10.4 4.8 %collective-permute-start = (bf16[133,1024]{1,0:T(8,128)(2,1)S(1)}, bf16[133,1024]{1,0:T(8,128)(2,1)S(1)}, u32[]{:S(2)}, u32[]{:S(2)}) collective-permute-start(bf16[133,1024]{1,0:T(8,128)(2,1)S(1)} %slice_bitcast_fusion), channel_id=1, source_target_pairs={{0,4},{4,8},{8,12},{12,16},{16,20},{20,24},{24,28},{28,32},{32,36}... | collective-permute-start | bytes 817160 | tf_op jit(solution)/shard_map/ppermute | solution.py:14
  15.3 0.0 copy-done.3
  15.3 0.1 rev.4
  15.4 0.7 pad_convert_fusion
  16.0 0.0 copy-done.6
  16.0 0.2 broadcast_in_dim.18
  16.3 1.0 reshape_reshape.3.taps_ref
  17.3 0.0 collective-permute-done.1
  17.3 0.9 pad_maximum_fusion.sig_ref
  18.2 6.0 %shard_map.68 = (bf16[256,1024]{1,0:T(8,128)(2,1)}, bf16[256,1024]{1,0:T(8,128)(2,1)}, bf16[256,1024]{1,0:T(8,128)(2,1)}, bf16[256,1024]{1,0:T(8,128)(2,1)}, bf16[256,1024]{1,0:T(8,128)(2,1)}) custom-call(f32[21,1024]{1,0:T(8,128)} %reshape_reshape.3.taps_ref, bf16[262,1024]{1,0:T(8,128)(2,1)} %pad_maximum_fusion.sig_ref, bf16[256,1024]{1,0:T(8,128)(2,1)} %bitcast.25), custom_call_target="tpu_custom_call" | custom-call | tf_op jit(solution)/shard_map/pallas_call | solution.py:50
  24.3 0.0 collective-permute-done.2
  24.3 0.8 pad_maximum_fusion.1.sig_ref
  25.0 0.0 collective-permute-done.3.gy_ref
  25.0 0.0 copy-start.2
  25.0 0.7 copy-done.2
  25.7 5.0 %shard_map.69 = (bf16[127,1024]{1,0:T(8,128)(2,1)}, bf16[127,1024]{1,0:T(8,128)(2,1)}, bf16[127,1024]{1,0:T(8,128)(2,1)}, bf16[127,1024]{1,0:T(8,128)(2,1)}, bf16[127,1024]{1,0:T(8,128)(2,1)}) custom-call(f32[21,1024]{1,0:T(8,128)} %reshape_reshape.3.taps_ref, bf16[133,1024]{1,0:T(8,128)(2,1)} %pad_maximum_fusion.1.sig_ref, bf16[127,1024]{1,0:T(8,128)(2,1)} %copy-done.2), custom_call_target="tpu_custom_call" | custom-call | tf_op jit(solution)/shard_map/pallas_call | solution.py:50
  30.7 0.0 collective-permute-done.sig_ref
  30.7 0.0 copy-start.1
  30.7 0.8 broadcast_in_dim.19.gy_ref
  31.5 0.0 copy-done.1
  31.5 5.0 %shard_map.67 = (bf16[127,1024]{1,0:T(8,128)(2,1)}, bf16[127,1024]{1,0:T(8,128)(2,1)}, bf16[127,1024]{1,0:T(8,128)(2,1)}, bf16[127,1024]{1,0:T(8,128)(2,1)}, bf16[127,1024]{1,0:T(8,128)(2,1)}) custom-call(f32[21,1024]{1,0:T(8,128)} %reshape_reshape.3.taps_ref, bf16[133,1024]{1,0:T(8,128)(2,1)} %copy-done.1, bf16[127,1024]{1,0:T(8,128)(2,1)} %broadcast_in_dim.19.gy_ref), custom_call_target="tpu_custom_call" | custom-call | tf_op jit(solution)/shard_map/pallas_call | solution.py:50
  36.5 11.9 %shard_map.70 = (bf16[3,256,1024]{2,1,0:T(8,128)(2,1)}, f32[64,128]{1,0:T(8,128)}) custom-call(f32[64,256]{1,0:T(8,128)} %get-tuple-element.20.fwd_ref, f32[64,256]{1,0:T(8,128)} %get-tuple-element.19.bwd_ref, bf16[127,1024]{1,0:T(8,128)(2,1)} %get-tuple-element.11.kv_rim_ref, bf16[256,1024]{1,0:T(8,128)(2,1)} %get-tuple-element.12.prod_ref, ...), custom_call_target="tpu_custom_call" | custom-call | tf_op jit(solution)/shard_map/pallas_call | solution.py:200
  48.4 6.1 %shard_map.72 = f32[21,1024]{1,0:T(8,128)} custom-call(bf16[262,1024]{1,0:T(8,128)(2,1)} %pad_maximum_fusion.sig_ref, bf16[3,256,1024]{2,1,0:T(8,128)(2,1)} %get-tuple-element.17.grads_ref), custom_call_target="tpu_custom_call" | custom-call | tf_op jit(solution)/shard_map/pallas_call | solution.py:95
  54.5 0.0 copy-start.5
  54.5 1.1 %reshape.24 = f32[21,64,16]{2,1,0:T(8,128)S(1)} reshape(f32[21,1024]{1,0:T(8,128)} %shard_map.72) | data formatting | bytes 172032 | tf_op jit(solution)/shard_map/reshape | solution.py:254
  55.7 0.3 reduce_sum.18
  55.9 0.1 copy.7
  56.0 0.0 copy-done.5
  56.0 0.1 pad_maximum_fusion.2
  56.1 0.7 reshape.25
  56.8 17.0 %all-to-all-start = ((f32[32,149,2]{1,2,0:T(2,128)}), f32[32,149,2]{1,2,0:T(2,128)S(1)}, u32[]{:S(2)}, u32[]{:S(2)}) async-start(f32[32,149,2]{1,2,0:T(2,128)} %bitcast.11), calls=%async_computation | async-start | bytes 131072 | tf_op jit(solution)/shard_map/all_to_all | solution.py:22
  73.8 0.8 slice.42
  74.6 1.3 %collective-permute-start.4 = (bf16[3,6,1024]{2,1,0:T(8,128)(2,1)S(1)}, bf16[3,6,1024]{2,1,0:T(8,128)(2,1)S(1)}, u32[]{:S(2)}, u32[]{:S(2)}) collective-permute-start(bf16[3,6,1024]{2,1,0:T(8,128)(2,1)S(1)} %slice.42), channel_id=1, source_target_pairs={{4,0},{8,4},{12,8},{16,12},{20,16},{24,20},{28,24},{32,28},{36,32}... | collective-permute-start | bytes 110600 | tf_op jit(solution)/shard_map/ppermute | solution.py:14
  75.9 3.9 %collective-permute-done.4.rim_ref = bf16[3,6,1024]{2,1,0:T(8,128)(2,1)S(1)} collective-permute-done((bf16[3,6,1024]{2,1,0:T(8,128)(2,1)S(1)}, bf16[3,6,1024]{2,1,0:T(8,128)(2,1)S(1)}, u32[]{:S(2)}, u32[]{:S(2)}) %collective-permute-start.4) | collective-permute-done | bytes 36896 | tf_op jit(solution)/shard_map/ppermute | solution.py:14
  79.8 0.0 copy-start.4
  79.8 0.6 copy-done.4
  80.4 6.0 %shard_map.71 = bf16[256,1024]{1,0:T(8,128)(2,1)} custom-call(f32[21,1024]{1,0:T(8,128)} %reshape_reshape.3.taps_ref, bf16[3,256,1024]{2,1,0:T(8,128)(2,1)} %get-tuple-element.17.grads_ref, bf16[3,6,1024]{2,1,0:T(8,128)(2,1)} %copy-done.4), custom_call_target="tpu_custom_call" | custom-call | tf_op jit(solution)/shard_map/pallas_call | solution.py:111
  86.4 4.8 %collective-permute-start.5 = (bf16[1,256,1024]{2,1,0:T(8,128)(2,1)}, bf16[1,256,1024]{2,1,0:T(8,128)(2,1)S(1)}, u32[]{:S(2)}, u32[]{:S(2)}) collective-permute-start(bf16[1,256,1024]{2,1,0:T(8,128)(2,1)} %bitcast.28), channel_id=1, source_target_pairs={{128,0},{256,128},{384,256},{129,1},{257,129},{385,257},{130,2},{2... | collective-permute-start | bytes 1572872 | tf_op jit(solution)/shard_map/ppermute | solution.py:14
  91.2 0.0 all-to-all-done
  91.2 0.6 slice_bitcast_fusion.4
  91.9 0.6 slice_bitcast_fusion.5
  92.4 8.1 %collective-permute-done.5 = bf16[1,256,1024]{2,1,0:T(8,128)(2,1)S(1)} collective-permute-done((bf16[1,256,1024]{2,1,0:T(8,128)(2,1)}, bf16[1,256,1024]{2,1,0:T(8,128)(2,1)S(1)}, u32[]{:S(2)}, u32[]{:S(2)}) %collective-permute-start.5) | collective-permute-done | bytes 524320 | tf_op jit(solution)/shard_map/ppermute | solution.py:14
  100.6 0.8 copy.9
  (2 shorter events, 0.1 us)
Async XLA Ops:
  0.6 9.7 %copy-start = (bf16[1,256,1024]{2,1,0:T(8,128)(2,1)S(1)}, bf16[1,256,1024]{2,1,0:T(8,128)(2,1)}, u32[]{:S(2)}) copy-start(bf16[1,256,1024]{2,1,0:T(8,128)(2,1)} %param.4) | copy-start | bytes 1572868
  0.6 14.6 %copy-start.3 = (bf16[1,128,64]{1,2,0:T(8,128)(2,1)S(1)}, bf16[1,128,64]{1,2,0:T(8,128)(2,1)}, u32[]{:S(2)}) copy-start(bf16[1,128,64]{1,2,0:T(8,128)(2,1)} %param.7) | copy-start | bytes 49156
  0.7 15.4 %copy-start.6 = (bf16[1,21,64]{2,1,0:T(8,128)(2,1)S(1)}, bf16[1,21,64]{2,1,0:T(8,128)(2,1)}, u32[]{:S(2)}) copy-start(bf16[1,21,64]{2,1,0:T(8,128)(2,1)} %param.6) | copy-start | bytes 8068
  1.4 15.9 %collective-permute-start.1 = (bf16[6,1024]{1,0:T(8,128)(2,1)S(1)}, bf16[6,1024]{1,0:T(8,128)(2,1)S(1)}, u32[]{:S(2)}, u32[]{:S(2)}) collective-permute-start(bf16[6,1024]{1,0:T(8,128)(2,1)S(1)} %slice_bitcast_fusion.3), channel_id=1, source_target_pairs={{0,4},{4,8},{8,12},{12,16},{16,20},{20,24},{24,28},{28,32},{32,36}... | collective-permute-start | bytes 36872 | tf_op jit(solution)/shard_map/ppermute | solution.py:14
  6.8 17.5 %collective-permute-start.2 = (bf16[127,1024]{1,0:T(8,128)(2,1)S(1)}, bf16[127,1024]{1,0:T(8,128)(2,1)S(1)}, u32[]{:S(2)}, u32[]{:S(2)}) collective-permute-start(bf16[127,1024]{1,0:T(8,128)(2,1)S(1)} %slice_bitcast_fusion.2), channel_id=1, source_target_pairs={{4,0},{8,4},{12,8},{16,12},{20,16},{24,20},{28,24},{32,28},{36,32}... | collective-permute-start | bytes 780296 | tf_op jit(solution)/shard_map/ppermute | solution.py:14
  9.1 16.0 %collective-permute-start.3 = (bf16[127,1024]{1,0:T(8,128)(2,1)S(1)}, bf16[127,1024]{1,0:T(8,128)(2,1)S(1)}, u32[]{:S(2)}, u32[]{:S(2)}) collective-permute-start(bf16[127,1024]{1,0:T(8,128)(2,1)S(1)} %slice_bitcast_fusion.1), channel_id=1, source_target_pairs={{4,0},{8,4},{12,8},{16,12},{20,16},{24,20},{28,24},{32,28},{36,32}... | collective-permute-start | bytes 780296 | tf_op jit(solution)/shard_map/ppermute | solution.py:14
  10.4 20.3 %collective-permute-start = (bf16[133,1024]{1,0:T(8,128)(2,1)S(1)}, bf16[133,1024]{1,0:T(8,128)(2,1)S(1)}, u32[]{:S(2)}, u32[]{:S(2)}) collective-permute-start(bf16[133,1024]{1,0:T(8,128)(2,1)S(1)} %slice_bitcast_fusion), channel_id=1, source_target_pairs={{0,4},{4,8},{8,12},{12,16},{16,20},{20,24},{24,28},{28,32},{32,36}... | collective-permute-start | bytes 817160 | tf_op jit(solution)/shard_map/ppermute | solution.py:14
  25.0 0.7 copy-start.2
  30.7 0.8 copy-start.1
  54.5 1.5 %copy-start.5 = (f32[64,128]{1,0:T(8,128)S(1)}, f32[64,128]{1,0:T(8,128)}, u32[]{:S(2)}) copy-start(f32[64,128]{1,0:T(8,128)} %get-tuple-element.18) | copy-start | bytes 98308
  56.8 34.4 %all-to-all-start = ((f32[32,149,2]{1,2,0:T(2,128)}), f32[32,149,2]{1,2,0:T(2,128)S(1)}, u32[]{:S(2)}, u32[]{:S(2)}) async-start(f32[32,149,2]{1,2,0:T(2,128)} %bitcast.11), calls=%async_computation | async-start | bytes 131072 | tf_op jit(solution)/shard_map/all_to_all | solution.py:22
  74.6 5.2 %collective-permute-start.4 = (bf16[3,6,1024]{2,1,0:T(8,128)(2,1)S(1)}, bf16[3,6,1024]{2,1,0:T(8,128)(2,1)S(1)}, u32[]{:S(2)}, u32[]{:S(2)}) collective-permute-start(bf16[3,6,1024]{2,1,0:T(8,128)(2,1)S(1)} %slice.42), channel_id=1, source_target_pairs={{4,0},{8,4},{12,8},{16,12},{20,16},{24,20},{28,24},{32,28},{36,32}... | collective-permute-start | bytes 110600 | tf_op jit(solution)/shard_map/ppermute | solution.py:14
  79.8 0.6 copy-start.4
  86.4 14.2 %collective-permute-start.5 = (bf16[1,256,1024]{2,1,0:T(8,128)(2,1)}, bf16[1,256,1024]{2,1,0:T(8,128)(2,1)S(1)}, u32[]{:S(2)}, u32[]{:S(2)}) collective-permute-start(bf16[1,256,1024]{2,1,0:T(8,128)(2,1)} %bitcast.28), channel_id=1, source_target_pairs={{128,0},{256,128},{384,256},{129,1},{257,129},{385,257},{130,2},{2... | collective-permute-start | bytes 1572872 | tf_op jit(solution)/shard_map/ppermute | solution.py:14

commit v10 on v7

--- a/solution.py
+++ b/solution.py
@@ -6,6 +6,7 @@
 from jax.sharding import PartitionSpec as P
 
 LANE_BLOCK = 128
+SHORT_BLOCK = 256
 
 
 def passed_along(block, axis, distance):
@@ -45,19 +46,19 @@
     padded_rows, chan_count = signal_pad.shape
     rows = grad_out.shape[0]
     tap_rows = taps.shape[0]
-    row_spec = pl.BlockSpec((rows, LANE_BLOCK), lambda j: (0, j))
+    row_spec = pl.BlockSpec((rows, SHORT_BLOCK), lambda j: (0, j))
     shape = jax.ShapeDtypeStruct((rows, chan_count), jnp.bfloat16)
     return pl.pallas_call(
         front_kernel,
-        grid=(chan_count // LANE_BLOCK,),
+        grid=(chan_count // SHORT_BLOCK,),
         in_specs=[
-            pl.BlockSpec((tap_rows, LANE_BLOCK), lambda j: (0, j)),
-            pl.BlockSpec((padded_rows, LANE_BLOCK), lambda j: (0, j)),
+            pl.BlockSpec((tap_rows, SHORT_BLOCK), lambda j: (0, j)),
+            pl.BlockSpec((padded_rows, SHORT_BLOCK), lambda j: (0, j)),
             row_spec,
         ],
         out_specs=[row_spec] * 5,
         out_shape=[shape] * 5,
-        scratch_shapes=[pltpu.VMEM((padded_rows + 8, LANE_BLOCK), jnp.float32)],
+        scratch_shapes=[pltpu.VMEM((padded_rows + 8, SHORT_BLOCK), jnp.float32)],
     )(taps, signal_pad, grad_out)
 
 
@@ -94,14 +95,14 @@
     tap_rows = branches * (padded_rows - rows + 1)
     return pl.pallas_call(
         short_partial_kernel,
-        grid=(chan_count // LANE_BLOCK,),
+        grid=(chan_count // SHORT_BLOCK,),
         in_specs=[
-            pl.BlockSpec((padded_rows, LANE_BLOCK), lambda j: (0, j)),
-            pl.BlockSpec((branches, rows, LANE_BLOCK), lambda j: (0, 0, j)),
-        ],
-        out_specs=pl.BlockSpec((tap_rows, LANE_BLOCK), lambda j: (0, j)),
+            pl.BlockSpec((padded_rows, SHORT_BLOCK), lambda j: (0, j)),
+            pl.BlockSpec((branches, rows, SHORT_BLOCK), lambda j: (0, 0, j)),
+        ],
+        out_specs=pl.BlockSpec((tap_rows, SHORT_BLOCK), lambda j: (0, j)),
         out_shape=jax.ShapeDtypeStruct((tap_rows, chan_count), jnp.float32),
-        scratch_shapes=[pltpu.VMEM((padded_rows + 8, LANE_BLOCK), jnp.float32)],
+        scratch_shapes=[pltpu.VMEM((padded_rows + 8, SHORT_BLOCK), jnp.float32)],
     )(signal_pad, feature_grads)
 
 
@@ -110,15 +111,15 @@
     rim = feature_rim.shape[1]
     return pl.pallas_call(
         input_grad_kernel,
-        grid=(chan_count // LANE_BLOCK,),
+        grid=(chan_count // SHORT_BLOCK,),
         in_specs=[
-            pl.BlockSpec((taps.shape[0], LANE_BLOCK), lambda j: (0, j)),
-            pl.BlockSpec((branches, rows, LANE_BLOCK), lambda j: (0, 0, j)),
-            pl.BlockSpec((branches, rim, LANE_BLOCK), lambda j: (0, 0, j)),
-        ],
-        out_specs=pl.BlockSpec((rows, LANE_BLOCK), lambda j: (0, j)),
+            pl.BlockSpec((taps.shape[0], SHORT_BLOCK), lambda j: (0, j)),
+            pl.BlockSpec((branches, rows, SHORT_BLOCK), lambda j: (0, 0, j)),
+            pl.BlockSpec((branches, rim, SHORT_BLOCK), lambda j: (0, 0, j)),
+        ],
+        out_specs=pl.BlockSpec((rows, SHORT_BLOCK), lambda j: (0, j)),
         out_shape=jax.ShapeDtypeStruct((rows, chan_count), jnp.bfloat16),
-        scratch_shapes=[pltpu.VMEM((branches, rows + rim + 2, LANE_BLOCK), jnp.float32)],
+        scratch_shapes=[pltpu.VMEM((branches, rows + rim + 2, SHORT_BLOCK), jnp.float32)],
     )(taps, feature_grads, feature_rim)
 
 

time: 95.6 us -> 94.3 us (0.986)
  no operation moved by 1% of the time
where the time goes in v10:
time: 94.3 us; the launch traced here: 93.6 us
  starting transfers between devices  36.3 us (38%)
  Pallas kernels  29.1 us (31%)
  waiting for transfers between devices  14.6 us (15%)
  local copies, waits for them, and re-layouts  10.8 us (11%)
  other arithmetic  1.98 us (2%)
    all_to_all x1, starting transfers between devices, owned_sum(): return jnp.sum(lax.all_to_all(chunks, axis, 0, 0, tiled=False), axis=0)  20 us
    ppermute x5, starting transfers between devices, passed_along(): return lax.ppermute(block, axis, route)  16.3 us
    ppermute x5, waiting for transfers between devices, passed_along(): return lax.ppermute(block, axis, route)  14.6 us
    pallas_call x1, Pallas kernels, medium_terms(): pl.pallas_call(medium_kernel, grid=(chan_count // LANE_BLOCK,), in_specs=...  11.9 us
    pallas_call x1, Pallas kernels, short_front(): pl.pallas_call(front_kernel, grid=(chan_count // SHORT_BLOCK,), in_specs=...  6.19 us
    pallas_call x1, Pallas kernels, input_grads(): pl.pallas_call(input_grad_kernel, grid=(chan_count // SHORT_BLOCK,), in_s...  5.73 us
    pallas_call x1, Pallas kernels, short_partials(): pl.pallas_call(short_partial_kernel, grid=(chan_count // SHORT_BLOCK,), i...  5.3 us
    unnamed x13, local copies, waits for them, and re-layouts  2.12 us
  transfers between devices with their start and end apart: 6, of which 4 were waited for; matrix products, arithmetic and copies ran while one was open for 5% of the time, Pallas kernels for 6%

profile of v10, /device:TPU:1, one launch (start us, length us, event | category | flops | bytes accessed | tf_op | source)
XLA Modules:
  0.0 93.6 jit_solution(7763235253553049081)
XLA Ops:
  0.6 0.0 copy-start
  0.6 0.8 slice_bitcast_fusion
  1.4 4.4 %collective-permute-start = (bf16[6,1024]{1,0:T(8,128)(2,1)S(1)}, bf16[6,1024]{1,0:T(8,128)(2,1)S(1)}, u32[]{:S(2)}, u32[]{:S(2)}) collective-permute-start(bf16[6,1024]{1,0:T(8,128)(2,1)S(1)} %slice_bitcast_fusion), channel_id=1, source_target_pairs={{0,4},{4,8},{8,12},{12,16},{16,20},{20,24},{24,28},{28,32},{32,36}... | collective-permute-start | bytes 36872 | tf_op jit(solution)/shard_map/ppermute | solution.py:15
  5.8 0.7 reshape.23
  6.5 0.2 broadcast_in_dim.15
  6.7 1.0 %reshape_reshape.3.taps_ref = f32[21,1024]{1,0:T(8,128)} reshape(f32[3,7,64,16]{3,2,1,0:T(8,128)S(1)} %broadcast_in_dim.15) | data formatting | bytes 172032 | tf_op jit(solution)/shard_map/reshape;reshape | solution.py:238
  7.8 0.0 collective-permute-done
  7.8 0.0 copy-done
  7.8 0.9 pad_maximum_fusion.sig_ref
  8.7 0.0 copy-start.3
  8.7 6.2 %shard_map.67 = (bf16[256,1024]{1,0:T(8,128)(2,1)}, bf16[256,1024]{1,0:T(8,128)(2,1)}, bf16[256,1024]{1,0:T(8,128)(2,1)}, bf16[256,1024]{1,0:T(8,128)(2,1)}, bf16[256,1024]{1,0:T(8,128)(2,1)}) custom-call(f32[21,1024]{1,0:T(8,128)} %reshape_reshape.3.taps_ref, bf16[262,1024]{1,0:T(8,128)(2,1)} %pad_maximum_fusion.sig_ref, bf16[256,1024]{1,0:T(8,128)(2,1)} %bitcast.19), custom_call_target="tpu_custom_call" | custom-call | tf_op jit(solution)/shard_map/pallas_call | solution.py:51
  14.9 1.0 %slice.23 = bf16[127,1024]{1,0:T(8,128)(2,1)S(1)} slice(bf16[256,1024]{1,0:T(8,128)(2,1)} %get-tuple-element.9.prod_ref), slice={[129:256], [0:1024]} | slice | bytes 520192 | tf_op jit(solution)/shard_map/slice | solution.py:242
  15.9 1.0 %slice.24 = bf16[127,1024]{1,0:T(8,128)(2,1)S(1)} slice(bf16[256,1024]{1,0:T(8,128)(2,1)} %get-tuple-element.10.gate_ref), slice={[0:127], [0:1024]} | slice | bytes 520192 | tf_op jit(solution)/shard_map/slice | solution.py:243
  16.9 1.3 %collective-permute-start.2 = (bf16[127,1024]{1,0:T(8,128)(2,1)S(1)}, bf16[127,1024]{1,0:T(8,128)(2,1)S(1)}, u32[]{:S(2)}, u32[]{:S(2)}) collective-permute-start(bf16[127,1024]{1,0:T(8,128)(2,1)S(1)} %slice.24), channel_id=1, source_target_pairs={{4,0},{8,4},{12,8},{16,12},{20,16},{24,20},{28,24},{32,28},{36,32}... | collective-permute-start | bytes 780296 | tf_op jit(solution)/shard_map/ppermute | solution.py:15
  18.2 4.2 %collective-permute-start.1 = (bf16[127,1024]{1,0:T(8,128)(2,1)S(1)}, bf16[127,1024]{1,0:T(8,128)(2,1)S(1)}, u32[]{:S(2)}, u32[]{:S(2)}) collective-permute-start(bf16[127,1024]{1,0:T(8,128)(2,1)S(1)} %slice.23), channel_id=1, source_target_pairs={{0,4},{4,8},{8,12},{12,16},{16,20},{20,24},{24,28},{28,32},{32,36}... | collective-permute-start | bytes 780296 | tf_op jit(solution)/shard_map/ppermute | solution.py:15
  22.4 0.0 copy-done.3
  22.4 0.1 rev.4
  22.5 0.7 pad_convert_fusion
  23.1 1.0 %collective-permute-done.2.gate_rim_ref = bf16[127,1024]{1,0:T(8,128)(2,1)S(1)} collective-permute-done((bf16[127,1024]{1,0:T(8,128)(2,1)S(1)}, bf16[127,1024]{1,0:T(8,128)(2,1)S(1)}, u32[]{:S(2)}, u32[]{:S(2)}) %collective-permute-start.2) | collective-permute-done | bytes 260128 | tf_op jit(solution)/shard_map/ppermute | solution.py:15
  24.2 0.0 copy-start.1
  24.2 1.5 %collective-permute-done.1.kv_rim_ref = bf16[127,1024]{1,0:T(8,128)(2,1)S(1)} collective-permute-done((bf16[127,1024]{1,0:T(8,128)(2,1)S(1)}, bf16[127,1024]{1,0:T(8,128)(2,1)S(1)}, u32[]{:S(2)}, u32[]{:S(2)}) %collective-permute-start.1) | collective-permute-done | bytes 260128 | tf_op jit(solution)/shard_map/ppermute | solution.py:15
  25.7 0.0 copy-start.2
  25.7 0.0 copy-done.1
  25.7 0.7 copy-done.2
  26.4 11.9 %shard_map.68 = (bf16[3,256,1024]{2,1,0:T(8,128)(2,1)}, f32[64,128]{1,0:T(8,128)}) custom-call(f32[64,256]{1,0:T(8,128)} %get-tuple-element.16.fwd_ref, f32[64,256]{1,0:T(8,128)} %get-tuple-element.15.bwd_ref, bf16[127,1024]{1,0:T(8,128)(2,1)} %copy-done.2, bf16[256,1024]{1,0:T(8,128)(2,1)} %get-tuple-element.9.prod_ref, ...), custom_call_target="tpu_custom_call" | custom-call | tf_op jit(solution)/shard_map/pallas_call | solution.py:201
  38.3 5.3 %shard_map.70 = f32[21,1024]{1,0:T(8,128)} custom-call(bf16[262,1024]{1,0:T(8,128)(2,1)} %pad_maximum_fusion.sig_ref, bf16[3,256,1024]{2,1,0:T(8,128)(2,1)} %get-tuple-element.13.grads_ref), custom_call_target="tpu_custom_call" | custom-call | tf_op jit(solution)/shard_map/pallas_call | solution.py:96
  43.6 0.0 copy-start.5
  43.6 1.1 %reshape.21 = f32[21,64,16]{2,1,0:T(8,128)S(1)} reshape(f32[21,1024]{1,0:T(8,128)} %shard_map.70) | data formatting | bytes 172032 | tf_op jit(solution)/shard_map/reshape | solution.py:251
  44.7 0.3 reduce_sum.18
  45.0 0.1 copy.7
  45.1 0.0 copy-done.5
  45.1 0.1 pad_maximum_fusion.1
  45.2 0.7 reshape.22
  45.8 20.0 %all-to-all-start = ((f32[32,149,2]{1,2,0:T(2,128)}), f32[32,149,2]{1,2,0:T(2,128)S(1)}, u32[]{:S(2)}, u32[]{:S(2)}) async-start(f32[32,149,2]{1,2,0:T(2,128)} %bitcast.8), calls=%async_computation | async-start | bytes 131072 | tf_op jit(solution)/shard_map/all_to_all | solution.py:23
  65.8 0.8 slice.25
  66.6 1.3 %collective-permute-start.3 = (bf16[3,6,1024]{2,1,0:T(8,128)(2,1)S(1)}, bf16[3,6,1024]{2,1,0:T(8,128)(2,1)S(1)}, u32[]{:S(2)}, u32[]{:S(2)}) collective-permute-start(bf16[3,6,1024]{2,1,0:T(8,128)(2,1)S(1)} %slice.25), channel_id=1, source_target_pairs={{4,0},{8,4},{12,8},{16,12},{20,16},{24,20},{28,24},{32,28},{36,32}... | collective-permute-start | bytes 110600 | tf_op jit(solution)/shard_map/ppermute | solution.py:15
  67.9 3.9 %collective-permute-done.3.rim_ref = bf16[3,6,1024]{2,1,0:T(8,128)(2,1)S(1)} collective-permute-done((bf16[3,6,1024]{2,1,0:T(8,128)(2,1)S(1)}, bf16[3,6,1024]{2,1,0:T(8,128)(2,1)S(1)}, u32[]{:S(2)}, u32[]{:S(2)}) %collective-permute-start.3) | collective-permute-done | bytes 36896 | tf_op jit(solution)/shard_map/ppermute | solution.py:15
  71.9 0.0 copy-start.4
  71.9 0.6 copy-done.4
  72.5 5.7 %shard_map.69 = bf16[256,1024]{1,0:T(8,128)(2,1)} custom-call(f32[21,1024]{1,0:T(8,128)} %reshape_reshape.3.taps_ref, bf16[3,256,1024]{2,1,0:T(8,128)(2,1)} %get-tuple-element.13.grads_ref, bf16[3,6,1024]{2,1,0:T(8,128)(2,1)} %copy-done.4), custom_call_target="tpu_custom_call" | custom-call | tf_op jit(solution)/shard_map/pallas_call | solution.py:112
  78.2 5.2 %collective-permute-start.4 = (bf16[1,256,1024]{2,1,0:T(8,128)(2,1)}, bf16[1,256,1024]{2,1,0:T(8,128)(2,1)S(1)}, u32[]{:S(2)}, u32[]{:S(2)}) collective-permute-start(bf16[1,256,1024]{2,1,0:T(8,128)(2,1)} %bitcast.22), channel_id=1, source_target_pairs={{128,0},{256,128},{384,256},{129,1},{257,129},{385,257},{130,2},{2... | collective-permute-start | bytes 1572872 | tf_op jit(solution)/shard_map/ppermute | solution.py:15
  83.4 0.0 all-to-all-done
  83.4 0.6 slice_bitcast_fusion.1
  84.1 0.6 slice_bitcast_fusion.2
  84.6 8.1 %collective-permute-done.4 = bf16[1,256,1024]{2,1,0:T(8,128)(2,1)S(1)} collective-permute-done((bf16[1,256,1024]{2,1,0:T(8,128)(2,1)}, bf16[1,256,1024]{2,1,0:T(8,128)(2,1)S(1)}, u32[]{:S(2)}, u32[]{:S(2)}) %collective-permute-start.4) | collective-permute-done | bytes 524320 | tf_op jit(solution)/shard_map/ppermute | solution.py:15
  92.8 0.8 copy.9
  (1 shorter events, 0.0 us)
Async XLA Ops:
  0.6 7.1 %copy-start = (bf16[1,256,1024]{2,1,0:T(8,128)(2,1)S(1)}, bf16[1,256,1024]{2,1,0:T(8,128)(2,1)}, u32[]{:S(2)}) copy-start(bf16[1,256,1024]{2,1,0:T(8,128)(2,1)} %param.4) | copy-start | bytes 1572868
  1.4 6.3 %collective-permute-start = (bf16[6,1024]{1,0:T(8,128)(2,1)S(1)}, bf16[6,1024]{1,0:T(8,128)(2,1)S(1)}, u32[]{:S(2)}, u32[]{:S(2)}) collective-permute-start(bf16[6,1024]{1,0:T(8,128)(2,1)S(1)} %slice_bitcast_fusion), channel_id=1, source_target_pairs={{0,4},{4,8},{8,12},{12,16},{16,20},{20,24},{24,28},{28,32},{32,36}... | collective-permute-start | bytes 36872 | tf_op jit(solution)/shard_map/ppermute | solution.py:15
  8.7 13.7 %copy-start.3 = (bf16[1,128,64]{1,2,0:T(8,128)(2,1)S(1)}, bf16[1,128,64]{1,2,0:T(8,128)(2,1)}, u32[]{:S(2)}) copy-start(bf16[1,128,64]{1,2,0:T(8,128)(2,1)} %param.7) | copy-start | bytes 49156
  16.9 7.3 %collective-permute-start.2 = (bf16[127,1024]{1,0:T(8,128)(2,1)S(1)}, bf16[127,1024]{1,0:T(8,128)(2,1)S(1)}, u32[]{:S(2)}, u32[]{:S(2)}) collective-permute-start(bf16[127,1024]{1,0:T(8,128)(2,1)S(1)} %slice.24), channel_id=1, source_target_pairs={{4,0},{8,4},{12,8},{16,12},{20,16},{24,20},{28,24},{32,28},{36,32}... | collective-permute-start | bytes 780296 | tf_op jit(solution)/shard_map/ppermute | solution.py:15
  18.2 7.5 %collective-permute-start.1 = (bf16[127,1024]{1,0:T(8,128)(2,1)S(1)}, bf16[127,1024]{1,0:T(8,128)(2,1)S(1)}, u32[]{:S(2)}, u32[]{:S(2)}) collective-permute-start(bf16[127,1024]{1,0:T(8,128)(2,1)S(1)} %slice.23), channel_id=1, source_target_pairs={{0,4},{4,8},{8,12},{12,16},{16,20},{20,24},{24,28},{28,32},{32,36}... | collective-permute-start | bytes 780296 | tf_op jit(solution)/shard_map/ppermute | solution.py:15
  24.2 1.5 %copy-start.1 = (bf16[127,1024]{1,0:T(8,128)(2,1)}, bf16[127,1024]{1,0:T(8,128)(2,1)S(1)}, u32[]{:S(2)}) copy-start(bf16[127,1024]{1,0:T(8,128)(2,1)S(1)} %collective-permute-done.2.gate_rim_ref) | copy-start | bytes 780292
  25.7 0.7 copy-start.2
  43.6 1.5 %copy-start.5 = (f32[64,128]{1,0:T(8,128)S(1)}, f32[64,128]{1,0:T(8,128)}, u32[]{:S(2)}) copy-start(f32[64,128]{1,0:T(8,128)} %get-tuple-element.14) | copy-start | bytes 98308
  45.8 37.5 %all-to-all-start = ((f32[32,149,2]{1,2,0:T(2,128)}), f32[32,149,2]{1,2,0:T(2,128)S(1)}, u32[]{:S(2)}, u32[]{:S(2)}) async-start(f32[32,149,2]{1,2,0:T(2,128)} %bitcast.8), calls=%async_computation | async-start | bytes 131072 | tf_op jit(solution)/shard_map/all_to_all | solution.py:23
  66.6 5.2 %collective-permute-start.3 = (bf16[3,6,1024]{2,1,0:T(8,128)(2,1)S(1)}, bf16[3,6,1024]{2,1,0:T(8,128)(2,1)S(1)}, u32[]{:S(2)}, u32[]{:S(2)}) collective-permute-start(bf16[3,6,1024]{2,1,0:T(8,128)(2,1)S(1)} %slice.25), channel_id=1, source_target_pairs={{4,0},{8,4},{12,8},{16,12},{20,16},{24,20},{28,24},{32,28},{36,32}... | collective-permute-start | bytes 110600 | tf_op jit(solution)/shard_map/ppermute | solution.py:15
  71.9 0.6 copy-start.4
  78.2 14.6 %collective-permute-start.4 = (bf16[1,256,1024]{2,1,0:T(8,128)(2,1)}, bf16[1,256,1024]{2,1,0:T(8,128)(2,1)S(1)}, u32[]{:S(2)}, u32[]{:S(2)}) collective-permute-start(bf16[1,256,1024]{2,1,0:T(8,128)(2,1)} %bitcast.22), channel_id=1, source_target_pairs={{128,0},{256,128},{384,256},{129,1},{257,129},{385,257},{130,2},{2... | collective-permute-start | bytes 1572872 | tf_op jit(solution)/shard_map/ppermute | solution.py:15

commit v11 on v10

--- a/solution.py
+++ b/solution.py
@@ -28,11 +28,13 @@
     rim = sig_ref.shape[0] - rows
     lags = rim + 1
     xs_ref[pl.ds(0, rows + rim), :] = sig_ref[...].astype(jnp.float32)
-    for branch, out_ref in enumerate((q_ref, k_ref, v_ref)):
-        acc = None
-        for offset in range(lags):
-            term = taps_ref[pl.ds(branch * lags + offset, 1), :] * xs_ref[pl.ds(rim - offset, rows), :]
-            acc = term if acc is None else acc + term
+    accs = [None, None, None]
+    for offset in range(lags):
+        window = xs_ref[pl.ds(rim - offset, rows), :]
+        for branch in range(3):
+            term = taps_ref[pl.ds(branch * lags + offset, 1), :] * window
+            accs[branch] = term if accs[branch] is None else accs[branch] + term
+    for acc, out_ref in zip(accs, (q_ref, k_ref, v_ref)):
         out_ref[...] = acc.astype(jnp.bfloat16)
     kv_ref[...] = (k_ref[...].astype(jnp.float32) * v_ref[...].astype(jnp.float32)).astype(
         jnp.bfloat16

time: 94.3 us -> 94.2 us (level)
  no operation moved by 1% of the time
where the time goes in v11:
time: 94.2 us; the launch traced here: 93.5 us
  starting transfers between devices  36.3 us (39%)
  Pallas kernels  29.1 us (31%)
  waiting for transfers between devices  14.6 us (15%)
  local copies, waits for them, and re-layouts  10.8 us (11%)
  other arithmetic  1.98 us (2%)
    all_to_all x1, starting transfers between devices, owned_sum(): return jnp.sum(lax.all_to_all(chunks, axis, 0, 0, tiled=False), axis=0)  20 us
    ppermute x5, starting transfers between devices, passed_along(): return lax.ppermute(block, axis, route)  16.3 us
    ppermute x5, waiting for transfers between devices, passed_along(): return lax.ppermute(block, axis, route)  14.6 us
    pallas_call x1, Pallas kernels, medium_terms(): pl.pallas_call(medium_kernel, grid=(chan_count // LANE_BLOCK,), in_specs=...  11.9 us
    pallas_call x1, Pallas kernels, short_front(): pl.pallas_call(front_kernel, grid=(chan_count // SHORT_BLOCK,), in_specs=...  6.16 us
    pallas_call x1, Pallas kernels, input_grads(): pl.pallas_call(input_grad_kernel, grid=(chan_count // SHORT_BLOCK,), in_s...  5.73 us
    pallas_call x1, Pallas kernels, short_partials(): pl.pallas_call(short_partial_kernel, grid=(chan_count // SHORT_BLOCK,), i...  5.3 us
    unnamed x13, local copies, waits for them, and re-layouts  2.12 us
  transfers between devices with their start and end apart: 6, of which 4 were waited for; matrix products, arithmetic and copies ran while one was open for 5% of the time, Pallas kernels for 6%

profile of v11, /device:TPU:1, one launch (start us, length us, event | category | flops | bytes accessed | tf_op | source)
XLA Modules:
  0.0 93.5 jit_solution(9794036133581115006)
XLA Ops:
  0.6 0.0 copy-start
  0.6 0.8 slice_bitcast_fusion
  1.4 4.4 %collective-permute-start = (bf16[6,1024]{1,0:T(8,128)(2,1)S(1)}, bf16[6,1024]{1,0:T(8,128)(2,1)S(1)}, u32[]{:S(2)}, u32[]{:S(2)}) collective-permute-start(bf16[6,1024]{1,0:T(8,128)(2,1)S(1)} %slice_bitcast_fusion), channel_id=1, source_target_pairs={{0,4},{4,8},{8,12},{12,16},{16,20},{20,24},{24,28},{28,32},{32,36}... | collective-permute-start | bytes 36872 | tf_op jit(solution)/shard_map/ppermute | solution.py:15
  5.8 0.7 reshape.23
  6.5 0.2 broadcast_in_dim.15
  6.7 1.0 %reshape_reshape.3.taps_ref = f32[21,1024]{1,0:T(8,128)} reshape(f32[3,7,64,16]{3,2,1,0:T(8,128)S(1)} %broadcast_in_dim.15) | data formatting | bytes 172032 | tf_op jit(solution)/shard_map/reshape;reshape | solution.py:240
  7.8 0.0 collective-permute-done
  7.8 0.0 copy-done
  7.8 0.9 pad_maximum_fusion.sig_ref
  8.7 0.0 copy-start.3
  8.7 6.2 %shard_map.67 = (bf16[256,1024]{1,0:T(8,128)(2,1)}, bf16[256,1024]{1,0:T(8,128)(2,1)}, bf16[256,1024]{1,0:T(8,128)(2,1)}, bf16[256,1024]{1,0:T(8,128)(2,1)}, bf16[256,1024]{1,0:T(8,128)(2,1)}) custom-call(f32[21,1024]{1,0:T(8,128)} %reshape_reshape.3.taps_ref, bf16[262,1024]{1,0:T(8,128)(2,1)} %pad_maximum_fusion.sig_ref, bf16[256,1024]{1,0:T(8,128)(2,1)} %bitcast.19), custom_call_target="tpu_custom_call" | custom-call | tf_op jit(solution)/shard_map/pallas_call | solution.py:53
  14.9 1.0 %slice.23 = bf16[127,1024]{1,0:T(8,128)(2,1)S(1)} slice(bf16[256,1024]{1,0:T(8,128)(2,1)} %get-tuple-element.9.prod_ref), slice={[129:256], [0:1024]} | slice | bytes 520192 | tf_op jit(solution)/shard_map/slice | solution.py:244
  15.9 1.0 %slice.24 = bf16[127,1024]{1,0:T(8,128)(2,1)S(1)} slice(bf16[256,1024]{1,0:T(8,128)(2,1)} %get-tuple-element.10.gate_ref), slice={[0:127], [0:1024]} | slice | bytes 520192 | tf_op jit(solution)/shard_map/slice | solution.py:245
  16.8 1.3 %collective-permute-start.2 = (bf16[127,1024]{1,0:T(8,128)(2,1)S(1)}, bf16[127,1024]{1,0:T(8,128)(2,1)S(1)}, u32[]{:S(2)}, u32[]{:S(2)}) collective-permute-start(bf16[127,1024]{1,0:T(8,128)(2,1)S(1)} %slice.24), channel_id=1, source_target_pairs={{4,0},{8,4},{12,8},{16,12},{20,16},{24,20},{28,24},{32,28},{36,32}... | collective-permute-start | bytes 780296 | tf_op jit(solution)/shard_map/ppermute | solution.py:15
  18.1 4.2 %collective-permute-start.1 = (bf16[127,1024]{1,0:T(8,128)(2,1)S(1)}, bf16[127,1024]{1,0:T(8,128)(2,1)S(1)}, u32[]{:S(2)}, u32[]{:S(2)}) collective-permute-start(bf16[127,1024]{1,0:T(8,128)(2,1)S(1)} %slice.23), channel_id=1, source_target_pairs={{0,4},{4,8},{8,12},{12,16},{16,20},{20,24},{24,28},{28,32},{32,36}... | collective-permute-start | bytes 780296 | tf_op jit(solution)/shard_map/ppermute | solution.py:15
  22.3 0.0 copy-done.3
  22.4 0.1 rev.4
  22.4 0.7 pad_convert_fusion
  23.1 1.0 %collective-permute-done.2.gate_rim_ref = bf16[127,1024]{1,0:T(8,128)(2,1)S(1)} collective-permute-done((bf16[127,1024]{1,0:T(8,128)(2,1)S(1)}, bf16[127,1024]{1,0:T(8,128)(2,1)S(1)}, u32[]{:S(2)}, u32[]{:S(2)}) %collective-permute-start.2) | collective-permute-done | bytes 260128 | tf_op jit(solution)/shard_map/ppermute | solution.py:15
  24.2 0.0 copy-start.1
  24.2 1.5 %collective-permute-done.1.kv_rim_ref = bf16[127,1024]{1,0:T(8,128)(2,1)S(1)} collective-permute-done((bf16[127,1024]{1,0:T(8,128)(2,1)S(1)}, bf16[127,1024]{1,0:T(8,128)(2,1)S(1)}, u32[]{:S(2)}, u32[]{:S(2)}) %collective-permute-start.1) | collective-permute-done | bytes 260128 | tf_op jit(solution)/shard_map/ppermute | solution.py:15
  25.6 0.0 copy-start.2
  25.6 0.0 copy-done.1
  25.6 0.7 copy-done.2
  26.3 11.9 %shard_map.68 = (bf16[3,256,1024]{2,1,0:T(8,128)(2,1)}, f32[64,128]{1,0:T(8,128)}) custom-call(f32[64,256]{1,0:T(8,128)} %get-tuple-element.16.fwd_ref, f32[64,256]{1,0:T(8,128)} %get-tuple-element.15.bwd_ref, bf16[127,1024]{1,0:T(8,128)(2,1)} %copy-done.2, bf16[256,1024]{1,0:T(8,128)(2,1)} %get-tuple-element.9.prod_ref, ...), custom_call_target="tpu_custom_call" | custom-call | tf_op jit(solution)/shard_map/pallas_call | solution.py:203
  38.2 5.3 %shard_map.70 = f32[21,1024]{1,0:T(8,128)} custom-call(bf16[262,1024]{1,0:T(8,128)(2,1)} %pad_maximum_fusion.sig_ref, bf16[3,256,1024]{2,1,0:T(8,128)(2,1)} %get-tuple-element.13.grads_ref), custom_call_target="tpu_custom_call" | custom-call | tf_op jit(solution)/shard_map/pallas_call | solution.py:98
  43.5 0.0 copy-start.5
  43.6 1.1 %reshape.21 = f32[21,64,16]{2,1,0:T(8,128)S(1)} reshape(f32[21,1024]{1,0:T(8,128)} %shard_map.70) | data formatting | bytes 172032 | tf_op jit(solution)/shard_map/reshape | solution.py:253
  44.7 0.3 reduce_sum.18
  45.0 0.1 copy.7
  45.0 0.0 copy-done.5
  45.1 0.1 pad_maximum_fusion.1
  45.1 0.7 reshape.22
  45.8 20.0 %all-to-all-start = ((f32[32,149,2]{1,2,0:T(2,128)}), f32[32,149,2]{1,2,0:T(2,128)S(1)}, u32[]{:S(2)}, u32[]{:S(2)}) async-start(f32[32,149,2]{1,2,0:T(2,128)} %bitcast.8), calls=%async_computation | async-start | bytes 131072 | tf_op jit(solution)/shard_map/all_to_all | solution.py:23
  65.8 0.8 slice.25
  66.6 1.3 %collective-permute-start.3 = (bf16[3,6,1024]{2,1,0:T(8,128)(2,1)S(1)}, bf16[3,6,1024]{2,1,0:T(8,128)(2,1)S(1)}, u32[]{:S(2)}, u32[]{:S(2)}) collective-permute-start(bf16[3,6,1024]{2,1,0:T(8,128)(2,1)S(1)} %slice.25), channel_id=1, source_target_pairs={{4,0},{8,4},{12,8},{16,12},{20,16},{24,20},{28,24},{32,28},{36,32}... | collective-permute-start | bytes 110600 | tf_op jit(solution)/shard_map/ppermute | solution.py:15
  67.9 3.9 %collective-permute-done.3.rim_ref = bf16[3,6,1024]{2,1,0:T(8,128)(2,1)S(1)} collective-permute-done((bf16[3,6,1024]{2,1,0:T(8,128)(2,1)S(1)}, bf16[3,6,1024]{2,1,0:T(8,128)(2,1)S(1)}, u32[]{:S(2)}, u32[]{:S(2)}) %collective-permute-start.3) | collective-permute-done | bytes 36896 | tf_op jit(solution)/shard_map/ppermute | solution.py:15
  71.8 0.0 copy-start.4
  71.8 0.6 copy-done.4
  72.4 5.7 %shard_map.69 = bf16[256,1024]{1,0:T(8,128)(2,1)} custom-call(f32[21,1024]{1,0:T(8,128)} %reshape_reshape.3.taps_ref, bf16[3,256,1024]{2,1,0:T(8,128)(2,1)} %get-tuple-element.13.grads_ref, bf16[3,6,1024]{2,1,0:T(8,128)(2,1)} %copy-done.4), custom_call_target="tpu_custom_call" | custom-call | tf_op jit(solution)/shard_map/pallas_call | solution.py:114
  78.2 5.2 %collective-permute-start.4 = (bf16[1,256,1024]{2,1,0:T(8,128)(2,1)}, bf16[1,256,1024]{2,1,0:T(8,128)(2,1)S(1)}, u32[]{:S(2)}, u32[]{:S(2)}) collective-permute-start(bf16[1,256,1024]{2,1,0:T(8,128)(2,1)} %bitcast.22), channel_id=1, source_target_pairs={{128,0},{256,128},{384,256},{129,1},{257,129},{385,257},{130,2},{2... | collective-permute-start | bytes 1572872 | tf_op jit(solution)/shard_map/ppermute | solution.py:15
  83.3 0.0 all-to-all-done
  83.4 0.6 slice_bitcast_fusion.1
  84.0 0.6 slice_bitcast_fusion.2
  84.6 8.1 %collective-permute-done.4 = bf16[1,256,1024]{2,1,0:T(8,128)(2,1)S(1)} collective-permute-done((bf16[1,256,1024]{2,1,0:T(8,128)(2,1)}, bf16[1,256,1024]{2,1,0:T(8,128)(2,1)S(1)}, u32[]{:S(2)}, u32[]{:S(2)}) %collective-permute-start.4) | collective-permute-done | bytes 524320 | tf_op jit(solution)/shard_map/ppermute | solution.py:15
  92.7 0.8 copy.9
  (1 shorter events, 0.0 us)
Async XLA Ops:
  0.6 7.1 %copy-start = (bf16[1,256,1024]{2,1,0:T(8,128)(2,1)S(1)}, bf16[1,256,1024]{2,1,0:T(8,128)(2,1)}, u32[]{:S(2)}) copy-start(bf16[1,256,1024]{2,1,0:T(8,128)(2,1)} %param.4) | copy-start | bytes 1572868
  1.4 6.3 %collective-permute-start = (bf16[6,1024]{1,0:T(8,128)(2,1)S(1)}, bf16[6,1024]{1,0:T(8,128)(2,1)S(1)}, u32[]{:S(2)}, u32[]{:S(2)}) collective-permute-start(bf16[6,1024]{1,0:T(8,128)(2,1)S(1)} %slice_bitcast_fusion), channel_id=1, source_target_pairs={{0,4},{4,8},{8,12},{12,16},{16,20},{20,24},{24,28},{28,32},{32,36}... | collective-permute-start | bytes 36872 | tf_op jit(solution)/shard_map/ppermute | solution.py:15
  8.7 13.7 %copy-start.3 = (bf16[1,128,64]{1,2,0:T(8,128)(2,1)S(1)}, bf16[1,128,64]{1,2,0:T(8,128)(2,1)}, u32[]{:S(2)}) copy-start(bf16[1,128,64]{1,2,0:T(8,128)(2,1)} %param.7) | copy-start | bytes 49156
  16.8 7.3 %collective-permute-start.2 = (bf16[127,1024]{1,0:T(8,128)(2,1)S(1)}, bf16[127,1024]{1,0:T(8,128)(2,1)S(1)}, u32[]{:S(2)}, u32[]{:S(2)}) collective-permute-start(bf16[127,1024]{1,0:T(8,128)(2,1)S(1)} %slice.24), channel_id=1, source_target_pairs={{4,0},{8,4},{12,8},{16,12},{20,16},{24,20},{28,24},{32,28},{36,32}... | collective-permute-start | bytes 780296 | tf_op jit(solution)/shard_map/ppermute | solution.py:15
  18.1 7.5 %collective-permute-start.1 = (bf16[127,1024]{1,0:T(8,128)(2,1)S(1)}, bf16[127,1024]{1,0:T(8,128)(2,1)S(1)}, u32[]{:S(2)}, u32[]{:S(2)}) collective-permute-start(bf16[127,1024]{1,0:T(8,128)(2,1)S(1)} %slice.23), channel_id=1, source_target_pairs={{0,4},{4,8},{8,12},{12,16},{16,20},{20,24},{24,28},{28,32},{32,36}... | collective-permute-start | bytes 780296 | tf_op jit(solution)/shard_map/ppermute | solution.py:15
  24.2 1.5 %copy-start.1 = (bf16[127,1024]{1,0:T(8,128)(2,1)}, bf16[127,1024]{1,0:T(8,128)(2,1)S(1)}, u32[]{:S(2)}) copy-start(bf16[127,1024]{1,0:T(8,128)(2,1)S(1)} %collective-permute-done.2.gate_rim_ref) | copy-start | bytes 780292
  25.6 0.7 copy-start.2
  43.5 1.5 %copy-start.5 = (f32[64,128]{1,0:T(8,128)S(1)}, f32[64,128]{1,0:T(8,128)}, u32[]{:S(2)}) copy-start(f32[64,128]{1,0:T(8,128)} %get-tuple-element.14) | copy-start | bytes 98308
  45.8 37.5 %all-to-all-start = ((f32[32,149,2]{1,2,0:T(2,128)}), f32[32,149,2]{1,2,0:T(2,128)S(1)}, u32[]{:S(2)}, u32[]{:S(2)}) async-start(f32[32,149,2]{1,2,0:T(2,128)} %bitcast.8), calls=%async_computation | async-start | bytes 131072 | tf_op jit(solution)/shard_map/all_to_all | solution.py:23
  66.6 5.2 %collective-permute-start.3 = (bf16[3,6,1024]{2,1,0:T(8,128)(2,1)S(1)}, bf16[3,6,1024]{2,1,0:T(8,128)(2,1)S(1)}, u32[]{:S(2)}, u32[]{:S(2)}) collective-permute-start(bf16[3,6,1024]{2,1,0:T(8,128)(2,1)S(1)} %slice.25), channel_id=1, source_target_pairs={{4,0},{8,4},{12,8},{16,12},{20,16},{24,20},{28,24},{32,28},{36,32}... | collective-permute-start | bytes 110600 | tf_op jit(solution)/shard_map/ppermute | solution.py:15
  71.8 0.6 copy-start.4
  78.2 14.6 %collective-permute-start.4 = (bf16[1,256,1024]{2,1,0:T(8,128)(2,1)}, bf16[1,256,1024]{2,1,0:T(8,128)(2,1)S(1)}, u32[]{:S(2)}, u32[]{:S(2)}) collective-permute-start(bf16[1,256,1024]{2,1,0:T(8,128)(2,1)} %bitcast.22), channel_id=1, source_target_pairs={{128,0},{256,128},{384,256},{129,1},{257,129},{385,257},{130,2},{2... | collective-permute-start | bytes 1572872 | tf_op jit(solution)/shard_map/ppermute | solution.py:15

commit v12 on v11

--- a/solution.py
+++ b/solution.py
@@ -161,23 +161,25 @@
         bwd = jnp.broadcast_to(bwd_ref[pl.ds(group, 1), :], (rows, span))
         fwd_band = pltpu.roll(fwd, 0, 1, stride=1, stride_axis=0).astype(jnp.bfloat16)
         bwd_band = pltpu.roll(bwd, 0, 1, stride=1, stride_axis=0).astype(jnp.bfloat16)
-        cross = None
-        for blk in range(block_count):
-            start = blk * rows
-            out_rows = pl.ds(start, rows)
-            mixed = jnp.dot(fwd_band, kv_all[start : start + span], preferred_element_type=jnp.float32)
-            mixed_s[out_rows, :] = jnp.where(in_group, mixed, mixed_s[out_rows, :])
-            back = jnp.dot(bwd_band, gate_all[start : start + span], preferred_element_type=jnp.float32)
-            back_s[out_rows, :] = jnp.where(in_group, back, back_s[out_rows, :])
-            gate_rows = jnp.where(in_group, gate_all[start : start + rows], jnp.zeros((), jnp.bfloat16))
-            flip_start = (block_count - 1 - blk) * rows
-            part = lax.dot_general(
-                gate_rows,
-                kv_flipped[flip_start : flip_start + span],
-                (((1,), (1,)), ((), ())),
-                preferred_element_type=jnp.float32,
-            )
-            cross = part if cross is None else cross + part
+        starts = [blk * rows for blk in range(block_count)]
+        kv_windows = jnp.concatenate([kv_all[st : st + span] for st in starts], axis=1)
+        gate_windows = jnp.concatenate([gate_all[st : st + span] for st in starts], axis=1)
+        mixed = jnp.dot(fwd_band, kv_windows, preferred_element_type=jnp.float32)
+        back = jnp.dot(bwd_band, gate_windows, preferred_element_type=jnp.float32)
+        for blk, st in enumerate(starts):
+            out_rows = pl.ds(st, rows)
+            lane_part = slice(blk * lanes, (blk + 1) * lanes)
+            mixed_s[out_rows, :] = jnp.where(in_group, mixed[:, lane_part], mixed_s[out_rows, :])
+            back_s[out_rows, :] = jnp.where(in_group, back[:, lane_part], back_s[out_rows, :])
+        gate_rows = jnp.concatenate(
+            [jnp.where(in_group, gate_all[st : st + rows], jnp.zeros((), jnp.bfloat16)) for st in starts],
+            axis=1,
+        )
+        flips = [(block_count - 1 - blk) * rows for blk in range(block_count)]
+        flipped = jnp.concatenate([kv_flipped[fs : fs + span] for fs in flips], axis=1)
+        cross = lax.dot_general(
+            gate_rows, flipped, (((1,), (1,)), ((), ())), preferred_element_type=jnp.float32
+        )
         rolled = pltpu.roll(cross, 0, 1, stride=1, stride_axis=0)
         taps_ref[pl.ds(group, 1), :] = jnp.sum(rolled[:, span - rows :], axis=0, keepdims=True)
     back_all = back_s[...]

time: 94.2 us -> 92.6 us (0.983)
  Pallas kernels: 29.1 us -> 27 us
    pallas_call x1, Pallas kernels: 11.9 us -> 9.82 us  [medium_terms(): pl.pallas_call(medium_kernel, grid=(chan_count // LANE_BLOCK,), in_specs=...]
where the time goes in v12:
time: 92.6 us; the launch traced here: 91.4 us
  starting transfers between devices  36.3 us (39%)
  Pallas kernels  27 us (29%)
  waiting for transfers between devices  14.6 us (16%)
  local copies, waits for them, and re-layouts  10.8 us (12%)
  other arithmetic  1.98 us (2%)
    all_to_all x1, starting transfers between devices, owned_sum(): return jnp.sum(lax.all_to_all(chunks, axis, 0, 0, tiled=False), axis=0)  20 us
    ppermute x5, starting transfers between devices, passed_along(): return lax.ppermute(block, axis, route)  16.3 us
    ppermute x5, waiting for transfers between devices, passed_along(): return lax.ppermute(block, axis, route)  14.6 us
    pallas_call x1, Pallas kernels, medium_terms(): pl.pallas_call(medium_kernel, grid=(chan_count // LANE_BLOCK,), in_specs=...  9.82 us
    pallas_call x1, Pallas kernels, short_front(): pl.pallas_call(front_kernel, grid=(chan_count // SHORT_BLOCK,), in_specs=...  6.16 us
    pallas_call x1, Pallas kernels, input_grads(): pl.pallas_call(input_grad_kernel, grid=(chan_count // SHORT_BLOCK,), in_s...  5.73 us
    pallas_call x1, Pallas kernels, short_partials(): pl.pallas_call(short_partial_kernel, grid=(chan_count // SHORT_BLOCK,), i...  5.3 us
    unnamed x13, local copies, waits for them, and re-layouts  2.12 us
  transfers between devices with their start and end apart: 6, of which 4 were waited for; matrix products, arithmetic and copies ran while one was open for 5% of the time, Pallas kernels for 6%

profile of v12, /device:TPU:1, one launch (start us, length us, event | category | flops | bytes accessed | tf_op | source)
XLA Modules:
  0.0 91.4 jit_solution(7268039650263702323)
XLA Ops:
  0.6 0.0 copy-start
  0.6 0.8 slice_bitcast_fusion
  1.4 4.4 %collective-permute-start = (bf16[6,1024]{1,0:T(8,128)(2,1)S(1)}, bf16[6,1024]{1,0:T(8,128)(2,1)S(1)}, u32[]{:S(2)}, u32[]{:S(2)}) collective-permute-start(bf16[6,1024]{1,0:T(8,128)(2,1)S(1)} %slice_bitcast_fusion), channel_id=1, source_target_pairs={{0,4},{4,8},{8,12},{12,16},{16,20},{20,24},{24,28},{28,32},{32,36}... | collective-permute-start | bytes 36872 | tf_op jit(solution)/shard_map/ppermute | solution.py:15
  5.8 0.7 reshape.23
  6.5 0.2 broadcast_in_dim.15
  6.7 1.0 %reshape_reshape.3.taps_ref = f32[21,1024]{1,0:T(8,128)} reshape(f32[3,7,64,16]{3,2,1,0:T(8,128)S(1)} %broadcast_in_dim.15) | data formatting | bytes 172032 | tf_op jit(solution)/shard_map/reshape;reshape | solution.py:242
  7.8 0.0 collective-permute-done
  7.8 0.0 copy-done
  7.8 0.9 %pad_maximum_fusion.sig_ref = bf16[262,1024]{1,0:T(8,128)(2,1)} fusion(bf16[256,1024]{1,0:T(8,128)(2,1)S(1)} %bitcast.21, bf16[6,1024]{1,0:T(8,128)(2,1)S(1)} %collective-permute-done), kind=kLoop, calls=%fused_computation | loop fusion | flops 1073152 | bytes 1073152 | tf_op jit(solution)/shard_map/concatenate | solution.py:244
  8.7 0.0 copy-start.3
  8.7 6.2 %shard_map.67 = (bf16[256,1024]{1,0:T(8,128)(2,1)}, bf16[256,1024]{1,0:T(8,128)(2,1)}, bf16[256,1024]{1,0:T(8,128)(2,1)}, bf16[256,1024]{1,0:T(8,128)(2,1)}, bf16[256,1024]{1,0:T(8,128)(2,1)}) custom-call(f32[21,1024]{1,0:T(8,128)} %reshape_reshape.3.taps_ref, bf16[262,1024]{1,0:T(8,128)(2,1)} %pad_maximum_fusion.sig_ref, bf16[256,1024]{1,0:T(8,128)(2,1)} %bitcast.19), custom_call_target="tpu_custom_call" | custom-call | tf_op jit(solution)/shard_map/pallas_call | solution.py:53
  14.9 1.0 %slice.23 = bf16[127,1024]{1,0:T(8,128)(2,1)S(1)} slice(bf16[256,1024]{1,0:T(8,128)(2,1)} %get-tuple-element.9.prod_ref), slice={[129:256], [0:1024]} | slice | bytes 520192 | tf_op jit(solution)/shard_map/slice | solution.py:246
  15.9 1.0 %slice.24 = bf16[127,1024]{1,0:T(8,128)(2,1)S(1)} slice(bf16[256,1024]{1,0:T(8,128)(2,1)} %get-tuple-element.10.gate_ref), slice={[0:127], [0:1024]} | slice | bytes 520192 | tf_op jit(solution)/shard_map/slice | solution.py:247
  16.8 1.3 %collective-permute-start.2 = (bf16[127,1024]{1,0:T(8,128)(2,1)S(1)}, bf16[127,1024]{1,0:T(8,128)(2,1)S(1)}, u32[]{:S(2)}, u32[]{:S(2)}) collective-permute-start(bf16[127,1024]{1,0:T(8,128)(2,1)S(1)} %slice.24), channel_id=1, source_target_pairs={{4,0},{8,4},{12,8},{16,12},{20,16},{24,20},{28,24},{32,28},{36,32}... | collective-permute-start | bytes 780296 | tf_op jit(solution)/shard_map/ppermute | solution.py:15
  18.1 4.2 %collective-permute-start.1 = (bf16[127,1024]{1,0:T(8,128)(2,1)S(1)}, bf16[127,1024]{1,0:T(8,128)(2,1)S(1)}, u32[]{:S(2)}, u32[]{:S(2)}) collective-permute-start(bf16[127,1024]{1,0:T(8,128)(2,1)S(1)} %slice.23), channel_id=1, source_target_pairs={{0,4},{4,8},{8,12},{12,16},{16,20},{20,24},{24,28},{28,32},{32,36}... | collective-permute-start | bytes 780296 | tf_op jit(solution)/shard_map/ppermute | solution.py:15
  22.3 0.0 copy-done.3
  22.4 0.1 rev.4
  22.4 0.7 pad_convert_fusion
  23.1 1.0 %collective-permute-done.2.gate_rim_ref = bf16[127,1024]{1,0:T(8,128)(2,1)S(1)} collective-permute-done((bf16[127,1024]{1,0:T(8,128)(2,1)S(1)}, bf16[127,1024]{1,0:T(8,128)(2,1)S(1)}, u32[]{:S(2)}, u32[]{:S(2)}) %collective-permute-start.2) | collective-permute-done | bytes 260128 | tf_op jit(solution)/shard_map/ppermute | solution.py:15
  24.2 0.0 copy-start.1
  24.2 1.5 %collective-permute-done.1.kv_rim_ref = bf16[127,1024]{1,0:T(8,128)(2,1)S(1)} collective-permute-done((bf16[127,1024]{1,0:T(8,128)(2,1)S(1)}, bf16[127,1024]{1,0:T(8,128)(2,1)S(1)}, u32[]{:S(2)}, u32[]{:S(2)}) %collective-permute-start.1) | collective-permute-done | bytes 260128 | tf_op jit(solution)/shard_map/ppermute | solution.py:15
  25.6 0.0 copy-start.2
  25.6 0.0 copy-done.1
  25.6 0.7 copy-done.2
  26.3 9.8 %shard_map.68 = (bf16[3,256,1024]{2,1,0:T(8,128)(2,1)}, f32[64,128]{1,0:T(8,128)}) custom-call(f32[64,256]{1,0:T(8,128)} %get-tuple-element.16.fwd_ref, f32[64,256]{1,0:T(8,128)} %get-tuple-element.15.bwd_ref, bf16[127,1024]{1,0:T(8,128)(2,1)} %copy-done.2, bf16[256,1024]{1,0:T(8,128)(2,1)} %get-tuple-element.9.prod_ref, ...), custom_call_target="tpu_custom_call" | custom-call | tf_op jit(solution)/shard_map/pallas_call | solution.py:205
  36.2 5.3 %shard_map.70 = f32[21,1024]{1,0:T(8,128)} custom-call(bf16[262,1024]{1,0:T(8,128)(2,1)} %pad_maximum_fusion.sig_ref, bf16[3,256,1024]{2,1,0:T(8,128)(2,1)} %get-tuple-element.13.grads_ref), custom_call_target="tpu_custom_call" | custom-call | tf_op jit(solution)/shard_map/pallas_call | solution.py:98
  41.5 0.0 copy-start.5
  41.5 1.1 %reshape.21 = f32[21,64,16]{2,1,0:T(8,128)S(1)} reshape(f32[21,1024]{1,0:T(8,128)} %shard_map.70) | data formatting | bytes 172032 | tf_op jit(solution)/shard_map/reshape | solution.py:255
  42.6 0.3 reduce_sum.18
  42.9 0.1 copy.7
  43.0 0.0 copy-done.5
  43.0 0.1 pad_maximum_fusion.1
  43.1 0.7 reshape.22
  43.7 20.0 %all-to-all-start = ((f32[32,149,2]{1,2,0:T(2,128)}), f32[32,149,2]{1,2,0:T(2,128)S(1)}, u32[]{:S(2)}, u32[]{:S(2)}) async-start(f32[32,149,2]{1,2,0:T(2,128)} %bitcast.8), calls=%async_computation | async-start | bytes 131072 | tf_op jit(solution)/shard_map/all_to_all | solution.py:23
  63.7 0.8 slice.25
  64.5 1.3 %collective-permute-start.3 = (bf16[3,6,1024]{2,1,0:T(8,128)(2,1)S(1)}, bf16[3,6,1024]{2,1,0:T(8,128)(2,1)S(1)}, u32[]{:S(2)}, u32[]{:S(2)}) collective-permute-start(bf16[3,6,1024]{2,1,0:T(8,128)(2,1)S(1)} %slice.25), channel_id=1, source_target_pairs={{4,0},{8,4},{12,8},{16,12},{20,16},{24,20},{28,24},{32,28},{36,32}... | collective-permute-start | bytes 110600 | tf_op jit(solution)/shard_map/ppermute | solution.py:15
  65.8 3.9 %collective-permute-done.3.rim_ref = bf16[3,6,1024]{2,1,0:T(8,128)(2,1)S(1)} collective-permute-done((bf16[3,6,1024]{2,1,0:T(8,128)(2,1)S(1)}, bf16[3,6,1024]{2,1,0:T(8,128)(2,1)S(1)}, u32[]{:S(2)}, u32[]{:S(2)}) %collective-permute-start.3) | collective-permute-done | bytes 36896 | tf_op jit(solution)/shard_map/ppermute | solution.py:15
  69.7 0.0 copy-start.4
  69.7 0.6 copy-done.4
  70.3 5.7 %shard_map.69 = bf16[256,1024]{1,0:T(8,128)(2,1)} custom-call(f32[21,1024]{1,0:T(8,128)} %reshape_reshape.3.taps_ref, bf16[3,256,1024]{2,1,0:T(8,128)(2,1)} %get-tuple-element.13.grads_ref, bf16[3,6,1024]{2,1,0:T(8,128)(2,1)} %copy-done.4), custom_call_target="tpu_custom_call" | custom-call | tf_op jit(solution)/shard_map/pallas_call | solution.py:114
  76.1 5.2 %collective-permute-start.4 = (bf16[1,256,1024]{2,1,0:T(8,128)(2,1)}, bf16[1,256,1024]{2,1,0:T(8,128)(2,1)S(1)}, u32[]{:S(2)}, u32[]{:S(2)}) collective-permute-start(bf16[1,256,1024]{2,1,0:T(8,128)(2,1)} %bitcast.22), channel_id=1, source_target_pairs={{128,0},{256,128},{384,256},{129,1},{257,129},{385,257},{130,2},{2... | collective-permute-start | bytes 1572872 | tf_op jit(solution)/shard_map/ppermute | solution.py:15
  81.2 0.0 all-to-all-done
  81.3 0.6 slice_bitcast_fusion.1
  81.9 0.6 slice_bitcast_fusion.2
  82.5 8.1 %collective-permute-done.4 = bf16[1,256,1024]{2,1,0:T(8,128)(2,1)S(1)} collective-permute-done((bf16[1,256,1024]{2,1,0:T(8,128)(2,1)}, bf16[1,256,1024]{2,1,0:T(8,128)(2,1)S(1)}, u32[]{:S(2)}, u32[]{:S(2)}) %collective-permute-start.4) | collective-permute-done | bytes 524320 | tf_op jit(solution)/shard_map/ppermute | solution.py:15
  90.6 0.8 copy.9
  (1 shorter events, 0.0 us)
Async XLA Ops:
  0.6 7.1 %copy-start = (bf16[1,256,1024]{2,1,0:T(8,128)(2,1)S(1)}, bf16[1,256,1024]{2,1,0:T(8,128)(2,1)}, u32[]{:S(2)}) copy-start(bf16[1,256,1024]{2,1,0:T(8,128)(2,1)} %param.4) | copy-start | bytes 1572868
  1.4 6.3 %collective-permute-start = (bf16[6,1024]{1,0:T(8,128)(2,1)S(1)}, bf16[6,1024]{1,0:T(8,128)(2,1)S(1)}, u32[]{:S(2)}, u32[]{:S(2)}) collective-permute-start(bf16[6,1024]{1,0:T(8,128)(2,1)S(1)} %slice_bitcast_fusion), channel_id=1, source_target_pairs={{0,4},{4,8},{8,12},{12,16},{16,20},{20,24},{24,28},{28,32},{32,36}... | collective-permute-start | bytes 36872 | tf_op jit(solution)/shard_map/ppermute | solution.py:15
  8.7 13.7 %copy-start.3 = (bf16[1,128,64]{1,2,0:T(8,128)(2,1)S(1)}, bf16[1,128,64]{1,2,0:T(8,128)(2,1)}, u32[]{:S(2)}) copy-start(bf16[1,128,64]{1,2,0:T(8,128)(2,1)} %param.7) | copy-start | bytes 49156
  16.8 7.3 %collective-permute-start.2 = (bf16[127,1024]{1,0:T(8,128)(2,1)S(1)}, bf16[127,1024]{1,0:T(8,128)(2,1)S(1)}, u32[]{:S(2)}, u32[]{:S(2)}) collective-permute-start(bf16[127,1024]{1,0:T(8,128)(2,1)S(1)} %slice.24), channel_id=1, source_target_pairs={{4,0},{8,4},{12,8},{16,12},{20,16},{24,20},{28,24},{32,28},{36,32}... | collective-permute-start | bytes 780296 | tf_op jit(solution)/shard_map/ppermute | solution.py:15
  18.1 7.5 %collective-permute-start.1 = (bf16[127,1024]{1,0:T(8,128)(2,1)S(1)}, bf16[127,1024]{1,0:T(8,128)(2,1)S(1)}, u32[]{:S(2)}, u32[]{:S(2)}) collective-permute-start(bf16[127,1024]{1,0:T(8,128)(2,1)S(1)} %slice.23), channel_id=1, source_target_pairs={{0,4},{4,8},{8,12},{12,16},{16,20},{20,24},{24,28},{28,32},{32,36}... | collective-permute-start | bytes 780296 | tf_op jit(solution)/shard_map/ppermute | solution.py:15
  24.2 1.5 %copy-start.1 = (bf16[127,1024]{1,0:T(8,128)(2,1)}, bf16[127,1024]{1,0:T(8,128)(2,1)S(1)}, u32[]{:S(2)}) copy-start(bf16[127,1024]{1,0:T(8,128)(2,1)S(1)} %collective-permute-done.2.gate_rim_ref) | copy-start | bytes 780292
  25.6 0.7 copy-start.2
  41.5 1.5 %copy-start.5 = (f32[64,128]{1,0:T(8,128)S(1)}, f32[64,128]{1,0:T(8,128)}, u32[]{:S(2)}) copy-start(f32[64,128]{1,0:T(8,128)} %get-tuple-element.14) | copy-start | bytes 98308
  43.7 37.5 %all-to-all-start = ((f32[32,149,2]{1,2,0:T(2,128)}), f32[32,149,2]{1,2,0:T(2,128)S(1)}, u32[]{:S(2)}, u32[]{:S(2)}) async-start(f32[32,149,2]{1,2,0:T(2,128)} %bitcast.8), calls=%async_computation | async-start | bytes 131072 | tf_op jit(solution)/shard_map/all_to_all | solution.py:23
  64.5 5.2 %collective-permute-start.3 = (bf16[3,6,1024]{2,1,0:T(8,128)(2,1)S(1)}, bf16[3,6,1024]{2,1,0:T(8,128)(2,1)S(1)}, u32[]{:S(2)}, u32[]{:S(2)}) collective-permute-start(bf16[3,6,1024]{2,1,0:T(8,128)(2,1)S(1)} %slice.25), channel_id=1, source_target_pairs={{4,0},{8,4},{12,8},{16,12},{20,16},{24,20},{28,24},{32,28},{36,32}... | collective-permute-start | bytes 110600 | tf_op jit(solution)/shard_map/ppermute | solution.py:15
  69.7 0.6 copy-start.4
  76.1 14.6 %collective-permute-start.4 = (bf16[1,256,1024]{2,1,0:T(8,128)(2,1)}, bf16[1,256,1024]{2,1,0:T(8,128)(2,1)S(1)}, u32[]{:S(2)}, u32[]{:S(2)}) collective-permute-start(bf16[1,256,1024]{2,1,0:T(8,128)(2,1)} %bitcast.22), channel_id=1, source_target_pairs={{128,0},{256,128},{384,256},{129,1},{257,129},{385,257},{130,2},{2... | collective-permute-start | bytes 1572872 | tf_op jit(solution)/shard_map/ppermute | solution.py:15

commit v13 on v12

--- a/solution.py
+++ b/solution.py
@@ -6,7 +6,7 @@
 from jax.sharding import PartitionSpec as P
 
 LANE_BLOCK = 128
-SHORT_BLOCK = 256
+SHORT_BLOCK = 512
 
 
 def passed_along(block, axis, distance):

time: 92.6 us -> 93.9 us (1.014)
  Pallas kernels: 27 us -> 28.4 us
  transfers between devices with their start and end apart: 6 -> 6, of which waited for: 4 -> 4; matrix products, arithmetic and copies ran while one was open for 5% -> 5% of each run, Pallas kernels for 6% -> 7%
where the time goes in v13:
time: 93.9 us; the launch traced here: 92.9 us
  starting transfers between devices  36.3 us (39%)
  Pallas kernels  28.4 us (30%)
  waiting for transfers between devices  14.6 us (16%)
  local copies, waits for them, and re-layouts  10.8 us (12%)
  other arithmetic  1.98 us (2%)
    all_to_all x1, starting transfers between devices, owned_sum(): return jnp.sum(lax.all_to_all(chunks, axis, 0, 0, tiled=False), axis=0)  20 us
    ppermute x5, starting transfers between devices, passed_along(): return lax.ppermute(block, axis, route)  16.3 us
    ppermute x5, waiting for transfers between devices, passed_along(): return lax.ppermute(block, axis, route)  14.6 us
    pallas_call x1, Pallas kernels, medium_terms(): pl.pallas_call(medium_kernel, grid=(chan_count // LANE_BLOCK,), in_specs=...  9.82 us
    pallas_call x1, Pallas kernels, short_front(): pl.pallas_call(front_kernel, grid=(chan_count // SHORT_BLOCK,), in_specs=...  6.78 us
    pallas_call x1, Pallas kernels, input_grads(): pl.pallas_call(input_grad_kernel, grid=(chan_count // SHORT_BLOCK,), in_s...  6.48 us
    pallas_call x1, Pallas kernels, short_partials(): pl.pallas_call(short_partial_kernel, grid=(chan_count // SHORT_BLOCK,), i...  5.35 us
    unnamed x13, local copies, waits for them, and re-layouts  2.12 us
  transfers between devices with their start and end apart: 6, of which 4 were waited for; matrix products, arithmetic and copies ran while one was open for 5% of the time, Pallas kernels for 7%

profile of v13, /device:TPU:1, one launch (start us, length us, event | category | flops | bytes accessed | tf_op | source)
XLA Modules:
  0.0 92.9 jit_solution(8832698880243974666)
XLA Ops:
  0.6 0.0 copy-start
  0.6 0.8 slice_bitcast_fusion
  1.4 4.4 %collective-permute-start = (bf16[6,1024]{1,0:T(8,128)(2,1)S(1)}, bf16[6,1024]{1,0:T(8,128)(2,1)S(1)}, u32[]{:S(2)}, u32[]{:S(2)}) collective-permute-start(bf16[6,1024]{1,0:T(8,128)(2,1)S(1)} %slice_bitcast_fusion), channel_id=1, source_target_pairs={{0,4},{4,8},{8,12},{12,16},{16,20},{20,24},{24,28},{28,32},{32,36}... | collective-permute-start | bytes 36872 | tf_op jit(solution)/shard_map/ppermute | solution.py:15
  5.8 0.7 reshape.23
  6.5 0.2 broadcast_in_dim.15
  6.7 1.0 %reshape_reshape.3.taps_ref = f32[21,1024]{1,0:T(8,128)} reshape(f32[3,7,64,16]{3,2,1,0:T(8,128)S(1)} %broadcast_in_dim.15) | data formatting | bytes 172032 | tf_op jit(solution)/shard_map/reshape;reshape | solution.py:242
  7.8 0.0 collective-permute-done
  7.8 0.0 copy-done
  7.8 0.9 %pad_maximum_fusion.sig_ref = bf16[262,1024]{1,0:T(8,128)(2,1)} fusion(bf16[256,1024]{1,0:T(8,128)(2,1)S(1)} %bitcast.21, bf16[6,1024]{1,0:T(8,128)(2,1)S(1)} %collective-permute-done), kind=kLoop, calls=%fused_computation | loop fusion | flops 1073152 | bytes 1073152 | tf_op jit(solution)/shard_map/concatenate | solution.py:244
  8.7 0.0 copy-start.3
  8.7 6.8 %shard_map.67 = (bf16[256,1024]{1,0:T(8,128)(2,1)}, bf16[256,1024]{1,0:T(8,128)(2,1)}, bf16[256,1024]{1,0:T(8,128)(2,1)}, bf16[256,1024]{1,0:T(8,128)(2,1)}, bf16[256,1024]{1,0:T(8,128)(2,1)}) custom-call(f32[21,1024]{1,0:T(8,128)} %reshape_reshape.3.taps_ref, bf16[262,1024]{1,0:T(8,128)(2,1)} %pad_maximum_fusion.sig_ref, bf16[256,1024]{1,0:T(8,128)(2,1)} %bitcast.19), custom_call_target="tpu_custom_call" | custom-call | tf_op jit(solution)/shard_map/pallas_call | solution.py:53
  15.5 1.0 %slice.23 = bf16[127,1024]{1,0:T(8,128)(2,1)S(1)} slice(bf16[256,1024]{1,0:T(8,128)(2,1)} %get-tuple-element.9.prod_ref), slice={[129:256], [0:1024]} | slice | bytes 520192 | tf_op jit(solution)/shard_map/slice | solution.py:246
  16.5 1.0 %slice.24 = bf16[127,1024]{1,0:T(8,128)(2,1)S(1)} slice(bf16[256,1024]{1,0:T(8,128)(2,1)} %get-tuple-element.10.gate_ref), slice={[0:127], [0:1024]} | slice | bytes 520192 | tf_op jit(solution)/shard_map/slice | solution.py:247
  17.5 1.3 %collective-permute-start.2 = (bf16[127,1024]{1,0:T(8,128)(2,1)S(1)}, bf16[127,1024]{1,0:T(8,128)(2,1)S(1)}, u32[]{:S(2)}, u32[]{:S(2)}) collective-permute-start(bf16[127,1024]{1,0:T(8,128)(2,1)S(1)} %slice.24), channel_id=1, source_target_pairs={{4,0},{8,4},{12,8},{16,12},{20,16},{24,20},{28,24},{32,28},{36,32}... | collective-permute-start | bytes 780296 | tf_op jit(solution)/shard_map/ppermute | solution.py:15
  18.8 4.2 %collective-permute-start.1 = (bf16[127,1024]{1,0:T(8,128)(2,1)S(1)}, bf16[127,1024]{1,0:T(8,128)(2,1)S(1)}, u32[]{:S(2)}, u32[]{:S(2)}) collective-permute-start(bf16[127,1024]{1,0:T(8,128)(2,1)S(1)} %slice.23), channel_id=1, source_target_pairs={{0,4},{4,8},{8,12},{12,16},{16,20},{20,24},{24,28},{28,32},{32,36}... | collective-permute-start | bytes 780296 | tf_op jit(solution)/shard_map/ppermute | solution.py:15
  23.0 0.0 copy-done.3
  23.0 0.1 rev.4
  23.1 0.7 pad_convert_fusion
  23.7 1.0 %collective-permute-done.2.gate_rim_ref = bf16[127,1024]{1,0:T(8,128)(2,1)S(1)} collective-permute-done((bf16[127,1024]{1,0:T(8,128)(2,1)S(1)}, bf16[127,1024]{1,0:T(8,128)(2,1)S(1)}, u32[]{:S(2)}, u32[]{:S(2)}) %collective-permute-start.2) | collective-permute-done | bytes 260128 | tf_op jit(solution)/shard_map/ppermute | solution.py:15
  24.8 0.0 copy-start.1
  24.8 1.5 %collective-permute-done.1.kv_rim_ref = bf16[127,1024]{1,0:T(8,128)(2,1)S(1)} collective-permute-done((bf16[127,1024]{1,0:T(8,128)(2,1)S(1)}, bf16[127,1024]{1,0:T(8,128)(2,1)S(1)}, u32[]{:S(2)}, u32[]{:S(2)}) %collective-permute-start.1) | collective-permute-done | bytes 260128 | tf_op jit(solution)/shard_map/ppermute | solution.py:15
  26.2 0.0 copy-start.2
  26.2 0.0 copy-done.1
  26.3 0.7 copy-done.2
  26.9 9.8 %shard_map.68 = (bf16[3,256,1024]{2,1,0:T(8,128)(2,1)}, f32[64,128]{1,0:T(8,128)}) custom-call(f32[64,256]{1,0:T(8,128)} %get-tuple-element.16.fwd_ref, f32[64,256]{1,0:T(8,128)} %get-tuple-element.15.bwd_ref, bf16[127,1024]{1,0:T(8,128)(2,1)} %copy-done.2, bf16[256,1024]{1,0:T(8,128)(2,1)} %get-tuple-element.9.prod_ref, ...), custom_call_target="tpu_custom_call" | custom-call | tf_op jit(solution)/shard_map/pallas_call | solution.py:205
  36.8 5.3 %shard_map.70 = f32[21,1024]{1,0:T(8,128)} custom-call(bf16[262,1024]{1,0:T(8,128)(2,1)} %pad_maximum_fusion.sig_ref, bf16[3,256,1024]{2,1,0:T(8,128)(2,1)} %get-tuple-element.13.grads_ref), custom_call_target="tpu_custom_call" | custom-call | tf_op jit(solution)/shard_map/pallas_call | solution.py:98
  42.1 0.0 copy-start.5
  42.1 1.1 %reshape.21 = f32[21,64,16]{2,1,0:T(8,128)S(1)} reshape(f32[21,1024]{1,0:T(8,128)} %shard_map.70) | data formatting | bytes 172032 | tf_op jit(solution)/shard_map/reshape | solution.py:255
  43.3 0.3 reduce_sum.18
  43.5 0.1 copy.7
  43.6 0.0 copy-done.5
  43.6 0.1 pad_maximum_fusion.1
  43.7 0.7 reshape.22
  44.4 20.0 %all-to-all-start = ((f32[32,149,2]{1,2,0:T(2,128)}), f32[32,149,2]{1,2,0:T(2,128)S(1)}, u32[]{:S(2)}, u32[]{:S(2)}) async-start(f32[32,149,2]{1,2,0:T(2,128)} %bitcast.8), calls=%async_computation | async-start | bytes 131072 | tf_op jit(solution)/shard_map/all_to_all | solution.py:23
  64.4 0.8 slice.25
  65.2 1.3 %collective-permute-start.3 = (bf16[3,6,1024]{2,1,0:T(8,128)(2,1)S(1)}, bf16[3,6,1024]{2,1,0:T(8,128)(2,1)S(1)}, u32[]{:S(2)}, u32[]{:S(2)}) collective-permute-start(bf16[3,6,1024]{2,1,0:T(8,128)(2,1)S(1)} %slice.25), channel_id=1, source_target_pairs={{4,0},{8,4},{12,8},{16,12},{20,16},{24,20},{28,24},{32,28},{36,32}... | collective-permute-start | bytes 110600 | tf_op jit(solution)/shard_map/ppermute | solution.py:15
  66.5 3.9 %collective-permute-done.3.rim_ref = bf16[3,6,1024]{2,1,0:T(8,128)(2,1)S(1)} collective-permute-done((bf16[3,6,1024]{2,1,0:T(8,128)(2,1)S(1)}, bf16[3,6,1024]{2,1,0:T(8,128)(2,1)S(1)}, u32[]{:S(2)}, u32[]{:S(2)}) %collective-permute-start.3) | collective-permute-done | bytes 36896 | tf_op jit(solution)/shard_map/ppermute | solution.py:15
  70.4 0.0 copy-start.4
  70.4 0.6 copy-done.4
  71.0 6.5 %shard_map.69 = bf16[256,1024]{1,0:T(8,128)(2,1)} custom-call(f32[21,1024]{1,0:T(8,128)} %reshape_reshape.3.taps_ref, bf16[3,256,1024]{2,1,0:T(8,128)(2,1)} %get-tuple-element.13.grads_ref, bf16[3,6,1024]{2,1,0:T(8,128)(2,1)} %copy-done.4), custom_call_target="tpu_custom_call" | custom-call | tf_op jit(solution)/shard_map/pallas_call | solution.py:114
  77.5 5.2 %collective-permute-start.4 = (bf16[1,256,1024]{2,1,0:T(8,128)(2,1)}, bf16[1,256,1024]{2,1,0:T(8,128)(2,1)S(1)}, u32[]{:S(2)}, u32[]{:S(2)}) collective-permute-start(bf16[1,256,1024]{2,1,0:T(8,128)(2,1)} %bitcast.22), channel_id=1, source_target_pairs={{128,0},{256,128},{384,256},{129,1},{257,129},{385,257},{130,2},{2... | collective-permute-start | bytes 1572872 | tf_op jit(solution)/shard_map/ppermute | solution.py:15
  82.7 0.0 all-to-all-done
  82.7 0.6 slice_bitcast_fusion.1
  83.4 0.6 slice_bitcast_fusion.2
  83.9 8.1 %collective-permute-done.4 = bf16[1,256,1024]{2,1,0:T(8,128)(2,1)S(1)} collective-permute-done((bf16[1,256,1024]{2,1,0:T(8,128)(2,1)}, bf16[1,256,1024]{2,1,0:T(8,128)(2,1)S(1)}, u32[]{:S(2)}, u32[]{:S(2)}) %collective-permute-start.4) | collective-permute-done | bytes 524320 | tf_op jit(solution)/shard_map/ppermute | solution.py:15
  92.1 0.8 copy.9
  (1 shorter events, 0.0 us)
Async XLA Ops:
  0.6 7.1 %copy-start = (bf16[1,256,1024]{2,1,0:T(8,128)(2,1)S(1)}, bf16[1,256,1024]{2,1,0:T(8,128)(2,1)}, u32[]{:S(2)}) copy-start(bf16[1,256,1024]{2,1,0:T(8,128)(2,1)} %param.4) | copy-start | bytes 1572868
  1.4 6.3 %collective-permute-start = (bf16[6,1024]{1,0:T(8,128)(2,1)S(1)}, bf16[6,1024]{1,0:T(8,128)(2,1)S(1)}, u32[]{:S(2)}, u32[]{:S(2)}) collective-permute-start(bf16[6,1024]{1,0:T(8,128)(2,1)S(1)} %slice_bitcast_fusion), channel_id=1, source_target_pairs={{0,4},{4,8},{8,12},{12,16},{16,20},{20,24},{24,28},{28,32},{32,36}... | collective-permute-start | bytes 36872 | tf_op jit(solution)/shard_map/ppermute | solution.py:15
  8.7 14.3 %copy-start.3 = (bf16[1,128,64]{1,2,0:T(8,128)(2,1)S(1)}, bf16[1,128,64]{1,2,0:T(8,128)(2,1)}, u32[]{:S(2)}) copy-start(bf16[1,128,64]{1,2,0:T(8,128)(2,1)} %param.7) | copy-start | bytes 49156
  17.5 7.3 %collective-permute-start.2 = (bf16[127,1024]{1,0:T(8,128)(2,1)S(1)}, bf16[127,1024]{1,0:T(8,128)(2,1)S(1)}, u32[]{:S(2)}, u32[]{:S(2)}) collective-permute-start(bf16[127,1024]{1,0:T(8,128)(2,1)S(1)} %slice.24), channel_id=1, source_target_pairs={{4,0},{8,4},{12,8},{16,12},{20,16},{24,20},{28,24},{32,28},{36,32}... | collective-permute-start | bytes 780296 | tf_op jit(solution)/shard_map/ppermute | solution.py:15
  18.8 7.5 %collective-permute-start.1 = (bf16[127,1024]{1,0:T(8,128)(2,1)S(1)}, bf16[127,1024]{1,0:T(8,128)(2,1)S(1)}, u32[]{:S(2)}, u32[]{:S(2)}) collective-permute-start(bf16[127,1024]{1,0:T(8,128)(2,1)S(1)} %slice.23), channel_id=1, source_target_pairs={{0,4},{4,8},{8,12},{12,16},{16,20},{20,24},{24,28},{28,32},{32,36}... | collective-permute-start | bytes 780296 | tf_op jit(solution)/shard_map/ppermute | solution.py:15
  24.8 1.5 %copy-start.1 = (bf16[127,1024]{1,0:T(8,128)(2,1)}, bf16[127,1024]{1,0:T(8,128)(2,1)S(1)}, u32[]{:S(2)}) copy-start(bf16[127,1024]{1,0:T(8,128)(2,1)S(1)} %collective-permute-done.2.gate_rim_ref) | copy-start | bytes 780292
  26.2 0.7 copy-start.2
  42.1 1.5 %copy-start.5 = (f32[64,128]{1,0:T(8,128)S(1)}, f32[64,128]{1,0:T(8,128)}, u32[]{:S(2)}) copy-start(f32[64,128]{1,0:T(8,128)} %get-tuple-element.14) | copy-start | bytes 98308
  44.4 38.3 %all-to-all-start = ((f32[32,149,2]{1,2,0:T(2,128)}), f32[32,149,2]{1,2,0:T(2,128)S(1)}, u32[]{:S(2)}, u32[]{:S(2)}) async-start(f32[32,149,2]{1,2,0:T(2,128)} %bitcast.8), calls=%async_computation | async-start | bytes 131072 | tf_op jit(solution)/shard_map/all_to_all | solution.py:23
  65.2 5.2 %collective-permute-start.3 = (bf16[3,6,1024]{2,1,0:T(8,128)(2,1)S(1)}, bf16[3,6,1024]{2,1,0:T(8,128)(2,1)S(1)}, u32[]{:S(2)}, u32[]{:S(2)}) collective-permute-start(bf16[3,6,1024]{2,1,0:T(8,128)(2,1)S(1)} %slice.25), channel_id=1, source_target_pairs={{4,0},{8,4},{12,8},{16,12},{20,16},{24,20},{28,24},{32,28},{36,32}... | collective-permute-start | bytes 110600 | tf_op jit(solution)/shard_map/ppermute | solution.py:15
  70.4 0.6 copy-start.4
  77.5 14.6 %collective-permute-start.4 = (bf16[1,256,1024]{2,1,0:T(8,128)(2,1)}, bf16[1,256,1024]{2,1,0:T(8,128)(2,1)S(1)}, u32[]{:S(2)}, u32[]{:S(2)}) collective-permute-start(bf16[1,256,1024]{2,1,0:T(8,128)(2,1)} %bitcast.22), channel_id=1, source_target_pairs={{128,0},{256,128},{384,256},{129,1},{257,129},{385,257},{130,2},{2... | collective-permute-start | bytes 1572872 | tf_op jit(solution)/shard_map/ppermute | solution.py:15
